TPU v7x, 256 devices: a whole 4x4x8 slice. The times are simulated.
256 devices in a mesh: seq: 64 (over y, z, core), head: 4 (over x).
Axes of the slice: x: 4, y: 4, z: 8, core: 2. Of those that a mesh axis runs over, the one named last changes fastest.
Arguments:
- queries: bfloat16 [8192, 1024], P('seq', 'head'), may hold values from -6 to 6
- raw_keys: bfloat16 [8192, 1024], P('seq', 'head'), may hold values from -6 to 6
- values: bfloat16 [8192, 1024], P('seq', 'head'), may hold values from -6 to 6
- write_rate: float32 [8192, 8], P('seq', 'head'), may hold values from 0.0005 to 1
- out_weight: bfloat16 [1024, 1024], P('head'), may hold values from -0.1875 to 0.1875
- out_grad: bfloat16 [8192, 1024], P('seq', 'head'), may hold values from -6 to 6
Outputs:
- layer_out: bfloat16 [8192, 1024], P('seq', 'head')
- query_grad: bfloat16 [8192, 1024], P('seq', 'head')
- key_grad: bfloat16 [8192, 1024], P('seq', 'head')
- value_grad: bfloat16 [8192, 1024], P('seq', 'head')
- rate_grad: float32 [8192, 8], P('seq', 'head')
All inputs are finite; a program needn't handle non-finite values.
Results may differ from a plain program's by a relative error of at most 0.0049.
Values may be sent and summed in bfloat16 or wider, within the bound.
No kernel may reach another device: no remote copies, remote signals or barrier semaphores. Data moves between devices by JAX's collectives and lax.ppermute only.
A program may use at most 128 MiB of HBM per device.

v0:
```python
import jax
import jax.numpy as jnp
from jax import lax
from jax.sharding import PartitionSpec as P

BLOCK = 64


epsilon = 1e-06
highest = lax.Precision.HIGHEST


def prefix(part, axis, combine, identity, reverse):
    count = lax.axis_size(axis)
    place = lax.axis_index(axis)
    ahead = count - 1 - place if reverse else place
    gathered = jax.tree.map(lambda a: lax.all_gather(a, axis), part)
    state = jax.tree.map(lambda a, e: jnp.zeros_like(a) + jnp.asarray(e, a.dtype), part, identity)

    def one(turn, state):
        source = count - 1 - turn if reverse else turn
        return combine(
            state, jax.tree.map(lambda a: lax.dynamic_index_in_dim(a, source, 0, False), gathered)
        )

    return lax.fori_loop(0, ahead, one, state)


def unit_rows(array):
    return array * lax.rsqrt(jnp.sum(array * array, -1, keepdims=True) + epsilon)


def to_blocks(array, head_count):
    rows = array.shape[0]
    head_width = array.shape[1] // head_count
    return array.reshape(rows // BLOCK, BLOCK, head_count, head_width).transpose(2, 0, 1, 3)


def rate_blocks(decay_rate):
    rows = decay_rate.shape[0]
    head_count = decay_rate.shape[1]
    return decay_rate.reshape(rows // BLOCK, BLOCK, head_count).transpose(2, 0, 1)


def from_blocks(block_outputs):
    block_count, head_count, size, head_width = block_outputs.shape
    return block_outputs.transpose(0, 2, 1, 3).reshape(block_count * size, head_count * head_width)


def block_factors(query_blocks, key_blocks, value_blocks, rate_parts):
    unit_query = unit_rows(query_blocks)
    unit_key = unit_rows(key_blocks)
    size = unit_key.shape[-2]
    identity_block = jnp.eye(size, dtype=jnp.float32)
    key_gram = jnp.einsum(
        "hncd,hnsd->hncs", unit_key * rate_parts[..., None], unit_key, precision=highest
    )
    strict_lower = jnp.tril(key_gram, -1)
    result = identity_block - strict_lower
    power_term = strict_lower
    span_done = 2
    while span_done < size:
        power_term = jnp.einsum("hnij,hnjk->hnik", power_term, power_term, precision=highest)
        result = result + jnp.einsum("hnij,hnjk->hnik", result, power_term, precision=highest)
        span_done = span_done * 2
    scaled = result * rate_parts[..., None, :]
    key_mix = jnp.einsum("hncs,hnsd->hncd", scaled, unit_key, precision=highest)
    value_mix = jnp.einsum("hncs,hnsd->hncd", scaled, value_blocks, precision=highest)
    causal_scores = jnp.tril(jnp.einsum("hncd,hnsd->hncs", unit_query, unit_key, precision=highest))
    return (unit_query, unit_key, key_mix, value_mix, causal_scores)


def run_blocks(factors, start_state):
    moved = tuple((jnp.moveaxis(member, 1, 0) for member in factors))

    def advance_block(state, pieces):
        unit_query, unit_key, key_mix, value_mix, causal_scores = pieces
        innovation = value_mix - jnp.einsum("hcd,hde->hce", key_mix, state, precision=highest)
        block_out = jnp.einsum("hcd,hde->hce", unit_query, state, precision=highest)
        block_out = block_out + jnp.einsum(
            "hcs,hse->hce", causal_scores, innovation, precision=highest
        )
        state = state + jnp.einsum("hcd,hce->hde", unit_key, innovation, precision=highest)
        return (state, block_out)

    return lax.scan(advance_block, start_state, moved)


def compose(earlier, later):
    early_map, early_shift = earlier
    late_map, late_shift = later
    joined_map = jnp.einsum("hij,hjk->hik", late_map, early_map, precision=highest)
    joined_shift = jnp.einsum("hij,hjk->hik", late_map, early_shift, precision=highest) + late_shift
    return (joined_map, joined_shift)


def body(queries, raw_keys, values, write_rate, out_weight, out_grad):
    head_count = write_rate.shape[1]
    head_width = queries.shape[1] // head_count
    token_count = queries.shape[0]

    def factor_inputs(float_query, float_key, float_value, rates):
        return block_factors(
            to_blocks(float_query, head_count),
            to_blocks(float_key, head_count),
            to_blocks(float_value, head_count),
            rate_blocks(rates),
        )

    factors, pull_factors = jax.vjp(
        factor_inputs,
        queries.astype(jnp.float32),
        raw_keys.astype(jnp.float32),
        values.astype(jnp.float32),
        write_rate,
    )
    unit_query, unit_key, key_mix, value_mix, causal_scores = factors
    identity_heads = jnp.broadcast_to(
        jnp.eye(head_width, dtype=jnp.float32), (head_count, head_width, head_width)
    )
    zero_heads = jnp.zeros((head_count, head_width, head_width), jnp.float32)
    widened = (
        unit_query,
        unit_key,
        key_mix,
        jnp.concatenate([jnp.zeros_like(value_mix), value_mix], -1),
        causal_scores,
    )
    joined_state, joined_outputs = run_blocks(
        widened, jnp.concatenate([identity_heads, zero_heads], -1)
    )
    transition = joined_state[..., :head_width]
    offset = joined_state[..., head_width:]
    query_effect = joined_outputs[..., :head_width]
    attended_grad = lax.dot_general(
        lax.all_gather(out_grad, "head", axis=1, tiled=True),
        out_weight,
        (((1,), (1,)), ((), ())),
        preferred_element_type=jnp.float32,
    )
    grad_blocks = attended_grad.reshape(
        token_count // BLOCK, BLOCK, head_count, head_width
    ).transpose(0, 2, 1, 3)
    local_adjoint = jnp.einsum("nhcd,nhce->hde", query_effect, grad_blocks, precision=highest)
    unused_map, entry_state = prefix(
        (transition, offset), "seq", compose, (identity_heads, zero_heads), False
    )
    unused_adjoint_map, exit_adjoint = prefix(
        (jnp.swapaxes(transition, 1, 2), local_adjoint),
        "seq",
        compose,
        (identity_heads, zero_heads),
        True,
    )

    def run_from_entry(factor_tuple):
        return run_blocks(factor_tuple, entry_state)

    (final_state, block_outputs), pull_run = jax.vjp(run_from_entry, factors)
    factor_grads = pull_run((exit_adjoint, grad_blocks))
    query_part, key_part, value_part, rate_grad = pull_factors(factor_grads[0])
    attended_bf = from_blocks(block_outputs).astype(jnp.bfloat16)
    partial_out = jnp.dot(attended_bf, out_weight, preferred_element_type=jnp.float32)
    layer_out = lax.psum_scatter(partial_out, "head", scatter_dimension=1, tiled=True).astype(
        jnp.bfloat16
    )
    return (
        layer_out,
        query_part.astype(jnp.bfloat16),
        key_part.astype(jnp.bfloat16),
        value_part.astype(jnp.bfloat16),
        rate_grad,
    )


def solution(mesh):
    placed = (
        P("seq", "head"),
        P("seq", "head"),
        P("seq", "head"),
        P("seq", "head"),
        P("head", None),
        P("seq", "head"),
    )
    return jax.shard_map(
        body,
        mesh=mesh,
        in_specs=placed,
        out_specs=(
            P("seq", "head"),
            P("seq", "head"),
            P("seq", "head"),
            P("seq", "head"),
            P("seq", "head"),
        ),
        check_vma=False,
    )
```

profile of v0, /device:TPU:8, one launch (start us, length us, event | category | flops | bytes accessed | tf_op | source)
XLA Modules:
  0.0 506.4 jit_solution(13383869806528043871)
XLA Ops:
  16.5 4.0 while.78
  20.5 12.6 %all_gather.33 = bf16[128,1024]{1,0:T(8,128)(2,1)S(1)} all-gather(bf16[128,256]{1,0:T(8,128)(2,1)S(1)} %copy-done.15), channel_id=1, replica_groups=mesh['seq'=64,'head'=4] {'head'}, dimensions={1}, use_global_device_ids=true | all-gather | bytes 327680 | tf_op jit(solution)/shard_map/all_gather | solution.py:136
  33.5 1.9 convolution_bitcast_fusion.4
  39.1 80.6 %all-gather.15.cloned.1.call-done = f32[128,128,128]{2,1,0:T(8,128)} async-done(((f32[2,128,128]{2,1,0:T(8,128)}), f32[128,128,128]{2,1,0:T(8,128)}) %all-gather.15.cloned.1.call-update) | async-done | bytes 8388624 | tf_op jit(solution)/shard_map/all_gather | solution.py:17
  119.6 82.6 %all-gather.13.cloned.1.call-done = f32[128,128,128]{2,1,0:T(8,128)} async-done(((f32[2,128,128]{2,1,0:T(8,128)}), f32[128,128,128]{2,1,0:T(8,128)}) %all-gather.13.cloned.1.call-update) | async-done | bytes 8388624 | tf_op jit(solution)/shard_map/all_gather | solution.py:17
  202.2 60.8 %while.81 = (s32[]{:T(128)}, f32[2,128,128]{2,1,0:T(8,128)S(1)}, s32[]{:T(128)}, f32[64,2,128,128]{3,2,1,0:T(8,128)}, f32[64,2,128,128]{3,2,1,0:T(8,128)}, /*index=5*/s32[]{:T(128)}, s32[]{:T(128)}, s32[]{:T(128)}, s32[]{:T(128)}) while((s32[]{:T(128)}, f32[2,128,128]{2,1,0:T(8,128)S(1)}, s32[]{:T(128)}, f32[64,2,128,128]{3,2,1,0:T(8,128)}, ...), condition=%wide.region_10.11_spmd, body=%wide.region_9.10_spmd.sunk | while | flops 50364420 | bytes 787595 | solution.py:26
  213.9 1.2 convolution_add_fusion.38
  215.2 1.3 convolution_add_fusion.38
  219.1 1.2 convolution_add_fusion.38
  221.7 1.2 convolution_add_fusion.38
  225.6 1.2 convolution_add_fusion.38
  228.1 1.2 convolution_add_fusion.38
  229.4 1.2 convolution_add_fusion.38
  241.1 1.2 convolution_add_fusion.38
  252.7 1.2 convolution_add_fusion.38
  257.9 1.3 convolution_add_fusion.38
  259.2 1.3 convolution_add_fusion.38
  263.1 21.8 %all-gather.9.cloned.1.call-done = f32[128,128,128]{2,1,0:T(8,128)} async-done(((f32[2,128,128]{2,1,0:T(8,128)}), f32[128,128,128]{2,1,0:T(8,128)}) %all-gather.9.cloned.1.call-update) | async-done | bytes 8388624 | tf_op jit(solution)/shard_map/all_gather | solution.py:17
  284.9 82.4 %all-gather.11.cloned.1.call-done = f32[128,128,128]{2,1,0:T(8,128)} async-done(((f32[2,128,128]{2,1,0:T(8,128)}), f32[128,128,128]{2,1,0:T(8,128)}) %all-gather.11.cloned.1.call-update) | async-done | bytes 8388624 | tf_op jit(solution)/shard_map/all_gather | solution.py:17
  367.3 20.8 %while.79 = (s32[]{:T(128)}, f32[2,128,128]{2,1,0:T(8,128)S(1)}, s32[]{:T(128)}, f32[64,2,128,128]{3,2,1,0:T(8,128)}, f32[64,2,128,128]{3,2,1,0:T(8,128)}, /*index=5*/s32[]{:T(128)}, s32[]{:T(128)}, s32[]{:T(128)}) while((s32[]{:T(128)}, f32[2,128,128]{2,1,0:T(8,128)S(1)}, s32[]{:T(128)}, f32[64,2,128,128]{3,2,1,0:T(8,128)}, ...), condition=%wide.region_5.6_spmd, body=%wide.region_4.5_spmd.sunk | while | flops 50364420 | bytes 787575 | solution.py:26
  388.2 3.5 while.80
  394.3 10.4 %while.82 = (s32[]{:T(128)}, f32[2,128,128]{2,1,0:T(8,128)S(1)}, f32[2,2,64,128]{3,2,0,1:T(8,128)}, f32[2,2,64,128]{3,2,0,1:T(8,128)}, f32[2,2,64,128]{3,2,1,0:T...) while((s32[]{:T(128)}, f32[2,128,128]{2,1,0:T(8,128)S(1)}, ...), condition=%wide.region_12.13_spmd, body=%wide.region_11.12_spmd.sunk | while | flops 176275456 | bytes 2367137 | solution.py:86
  420.9 77.4 %reduce-scatter.2.cloned.1.call-done = f32[128,256]{1,0:T(8,128)} async-done(((f32[128,1024]{1,0:T(8,128)}), f32[128,256]{1,0:T(8,128)}) %reduce-scatter.2.cloned.1.call-update) | async-done | bytes 131088 | tf_op jit(solution)/shard_map/reduce_scatter | solution.py:164
  498.3 1.5 convert_element_type.51
  (298 shorter events, 114.2 us)
Async XLA Ops:
  7.2 25.9 %copy-start = (bf16[256,1024]{1,0:T(8,128)(2,1)S(1)}, bf16[256,1024]{1,0:T(8,128)(2,1)}, u32[]{:S(2)}) copy-start(bf16[256,1024]{1,0:T(8,128)(2,1)} %param.20) | copy-start | bytes 1572868
  7.2 112.4 %all-gather.15.cloned.1.call-start = ((), (), s32[]{:S(2)}) async-start(), calls=%async_computation.5 | async-start | bytes 8519680 | tf_op jit(solution)/shard_map/all_gather | solution.py:17
  7.2 4.0 copy-start.10
  8.4 3.7 copy-start.20
  9.4 2.7 copy-start.18
  10.3 4.7 copy-start.16
  12.4 8.1 %copy-start.15 = (bf16[128,256]{1,0:T(8,128)(2,1)S(1)}, bf16[128,256]{1,0:T(8,128)(2,1)}, u32[]{:S(2)}) copy-start(bf16[128,256]{1,0:T(8,128)(2,1)} %param.21) | copy-start | bytes 196612
  12.7 3.8 copy-start.1
  35.4 166.8 %all-gather.13.cloned.1.call-start = ((), (), s32[]{:S(2)}) async-start(), calls=%async_computation.4 | async-start | bytes 8519680 | tf_op jit(solution)/shard_map/all_gather | solution.py:17
  37.0 247.8 %all-gather.9.cloned.1.call-start = ((), (), s32[]{:S(2)}) async-start(), calls=%async_computation.2 | async-start | bytes 8519680 | tf_op jit(solution)/shard_map/all_gather | solution.py:17
  37.8 329.5 %all-gather.11.cloned.1.call-start = ((), (), s32[]{:S(2)}) async-start(), calls=%async_computation.3 | async-start | bytes 8519680 | tf_op jit(solution)/shard_map/all_gather | solution.py:17
  38.3 460.0 %reduce-scatter.2.cloned.1.call-start = ((), (), s32[]{:S(2)}) async-start(), calls=%async_computation.1 | async-start | bytes 655360 | tf_op jit(solution)/shard_map/reduce_scatter | solution.py:164
  392.4 17.0 %copy-start.2 = (f32[2,2,64,64]{3,2,1,0:T(8,128)S(1)}, f32[2,2,64,64]{3,2,1,0:T(8,128)}, u32[]{:S(2)}) copy-start(f32[2,2,64,64]{3,2,1,0:T(8,128)} %copy-done.1) | copy-start | bytes 196612
  394.3 17.3 %copy-start.4 = (f32[2,2,64,64]{3,2,1,0:T(8,128)S(1)}, f32[2,2,64,64]{3,2,1,0:T(8,128)}, u32[]{:S(2)}) copy-start(f32[2,2,64,64]{3,2,1,0:T(8,128)} %copy-done.3) | copy-start | bytes 196612
  404.7 8.1 %copy-start.11 = (f32[64,64]{1,0:T(8,128)S(1)}, f32[64,64]{1,0:T(8,128)}, u32[]{:S(2)}) copy-start(f32[64,64]{1,0:T(8,128)} %copy-done.10) | copy-start | bytes 49156
  404.7 9.2 %copy-start.14 = (pred[64,64]{1,0:T(8,128)(4,1)S(1)}, pred[64,64]{1,0:T(8,128)(4,1)}, u32[]{:S(2)}) copy-start(pred[64,64]{1,0:T(8,128)(4,1)} %copy-done.13) | copy-start | bytes 12292
  404.7 10.0 %copy-start.7 = (f32[2,2,64,64]{3,2,1,0:T(8,128)S(1)}, f32[2,2,64,64]{3,2,1,0:T(8,128)}, u32[]{:S(2)}) copy-start(f32[2,2,64,64]{3,2,1,0:T(8,128)} %get-tuple-element.516) | copy-start | bytes 196612
  404.7 10.0 %copy-start.17 = (f32[2,2,64]{2,1,0:T(2,128)S(1)}, f32[2,2,64]{2,1,0:T(2,128)}, u32[]{:S(2)}) copy-start(f32[2,2,64]{2,1,0:T(2,128)} %copy-done.16) | copy-start | bytes 3076
  404.7 10.5 %copy-start.6 = (f32[2,2,64,128]{3,2,0,1:T(8,128)S(1)}, f32[2,2,64,128]{3,2,0,1:T(8,128)}, u32[]{:S(2)}) copy-start(f32[2,2,64,128]{3,2,0,1:T(8,128)} %get-tuple-element.517) | copy-start | bytes 393220
  404.8 11.0 %copy-start.21 = (f32[2,2,64]{2,1,0:T(2,128)S(1)}, f32[2,2,64]{2,1,0:T(2,128)}, u32[]{:S(2)}) copy-start(f32[2,2,64]{2,1,0:T(2,128)} %copy-done.20) | copy-start | bytes 3076
  404.8 11.0 %copy-start.12 = (bf16[2,2,64,128]{3,2,1,0:T(8,128)(2,1)S(1)}, bf16[2,2,64,128]{3,2,1,0:T(8,128)(2,1)}, u32[]{:S(2)}) copy-start(bf16[2,2,64,128]{3,2,1,0:T(8,128)(2,1)} %get-tuple-element.510) | copy-start | bytes 196612
  404.8 13.7 %copy-start.8 = (f32[2,2,64,128]{3,2,1,0:T(8,128)S(1)}, f32[2,2,64,128]{3,2,1,0:T(8,128)}, u32[]{:S(2)}) copy-start(f32[2,2,64,128]{3,2,1,0:T(8,128)} %get-tuple-element.519) | copy-start | bytes 393220
  404.8 14.8 %copy-start.5 = (f32[2,2,64,128]{3,2,0,1:T(8,128)S(1)}, f32[2,2,64,128]{3,2,0,1:T(8,128)}, u32[]{:S(2)}) copy-start(f32[2,2,64,128]{3,2,0,1:T(8,128)} %get-tuple-element.515) | copy-start | bytes 393220
  404.8 15.3 %copy-start.19 = (f32[2,2,64]{2,1,0:T(2,128)S(1)}, f32[2,2,64]{2,1,0:T(2,128)}, u32[]{:S(2)}) copy-start(f32[2,2,64]{2,1,0:T(2,128)} %copy-done.18) | copy-start | bytes 3076
  (3 other events, 2.8 us)
Sparse Core Ops, SparseCore 0:
  35.6 84.0 all-gather.14
  122.4 79.7 all-gather.12
  205.0 79.8 all-gather.8
  287.5 79.7 all-gather.10
  417.1 81.1 reduce-scatter.1
where the time goes:
time: 508 us; the launch traced here: 506 us
  waiting for transfers between devices  346 us (68%)
  matrix products  115 us (23%)
  between operations  14.6 us (3%)
  blocking collectives  12.6 us (2%)
  local copies, waits for them, and re-layouts  12 us (2%)
    all_gather x4, waiting for transfers between devices, prefix(): gathered = jax.tree.map(lambda a: lax.all_gather(a, axis), part)  267 us
    dot_general x63, matrix products, compose(): jnp.einsum('hij,hjk->hik', late_map, early_shift, precision=highest)  78.3 us
    reduce_scatter x1, waiting for transfers between devices, body(): lax.psum_scatter(partial_out, 'head', scatter_dimension=1, tiled=True)  77.4 us
    all_gather x1, blocking collectives, body(): lax.all_gather(out_grad, 'head', axis=1, tiled=True)  12.6 us
  transfers between devices with their start and end apart: 5, of which 5 were waited for; matrix products, arithmetic and copies ran while one was open for 13% of the time, Pallas kernels for 0%

commit v1 on v0

v1 whole, which is shorter than its diff:
```python
import jax
import jax.numpy as jnp
from jax import lax
from jax.sharding import PartitionSpec as P

BLOCK = 64


epsilon = 1e-06
highest = lax.Precision.HIGHEST


def unit_rows(array):
    return array * lax.rsqrt(jnp.sum(array * array, -1, keepdims=True) + epsilon)


def to_blocks(array, head_count):
    rows = array.shape[0]
    head_width = array.shape[1] // head_count
    return array.reshape(rows // BLOCK, BLOCK, head_count, head_width).transpose(2, 0, 1, 3)


def rate_blocks(decay_rate):
    rows = decay_rate.shape[0]
    head_count = decay_rate.shape[1]
    return decay_rate.reshape(rows // BLOCK, BLOCK, head_count).transpose(2, 0, 1)


def from_blocks(block_outputs):
    block_count, head_count, size, head_width = block_outputs.shape
    return block_outputs.transpose(0, 2, 1, 3).reshape(block_count * size, head_count * head_width)


def block_factors(query_blocks, key_blocks, value_blocks, rate_parts):
    unit_query = unit_rows(query_blocks)
    unit_key = unit_rows(key_blocks)
    size = unit_key.shape[-2]
    identity_block = jnp.eye(size, dtype=jnp.float32)
    key_gram = jnp.einsum(
        "hncd,hnsd->hncs", unit_key * rate_parts[..., None], unit_key, precision=highest
    )
    strict_lower = jnp.tril(key_gram, -1)
    result = identity_block - strict_lower
    power_term = strict_lower
    span_done = 2
    while span_done < size:
        power_term = jnp.einsum("hnij,hnjk->hnik", power_term, power_term, precision=highest)
        result = result + jnp.einsum("hnij,hnjk->hnik", result, power_term, precision=highest)
        span_done = span_done * 2
    scaled = result * rate_parts[..., None, :]
    key_mix = jnp.einsum("hncs,hnsd->hncd", scaled, unit_key, precision=highest)
    value_mix = jnp.einsum("hncs,hnsd->hncd", scaled, value_blocks, precision=highest)
    causal_scores = jnp.tril(jnp.einsum("hncd,hnsd->hncs", unit_query, unit_key, precision=highest))
    return (unit_query, unit_key, key_mix, value_mix, causal_scores)


def run_blocks(factors, start_state):
    moved = tuple((jnp.moveaxis(member, 1, 0) for member in factors))

    def advance_block(state, pieces):
        unit_query, unit_key, key_mix, value_mix, causal_scores = pieces
        innovation = value_mix - jnp.einsum("hcd,hde->hce", key_mix, state, precision=highest)
        block_out = jnp.einsum("hcd,hde->hce", unit_query, state, precision=highest)
        block_out = block_out + jnp.einsum(
            "hcs,hse->hce", causal_scores, innovation, precision=highest
        )
        state = state + jnp.einsum("hcd,hce->hde", unit_key, innovation, precision=highest)
        return (state, block_out)

    return lax.scan(advance_block, start_state, moved)


def mm(left, right):
    return jnp.einsum("hij,hjk->hik", left, right, precision=highest)


def scan_both(transition, offset, local_adjoint, count, axis):
    place = lax.axis_index(axis)
    fwd_map, fwd_shift = transition, offset
    bwd_map, bwd_shift = jnp.swapaxes(transition, 1, 2), local_adjoint
    step = 1
    while step < count:
        last = 2 * step >= count
        ahead = [(i, i + step) for i in range(count - step)]
        behind = [(i, i - step) for i in range(step, count)]
        if last:
            got_shift = lax.ppermute(fwd_shift, axis, ahead)
            back_shift = lax.ppermute(bwd_shift, axis, behind)
        else:
            got_map, got_shift = lax.ppermute((fwd_map, fwd_shift), axis, ahead)
            back_map, back_shift = lax.ppermute((bwd_map, bwd_shift), axis, behind)
        fwd_shift = fwd_shift + mm(fwd_map, got_shift)
        bwd_shift = bwd_shift + mm(bwd_map, back_shift)
        if not last:
            fwd_map = jnp.where(place >= step, mm(fwd_map, got_map), fwd_map)
            bwd_map = jnp.where(place + step < count, mm(bwd_map, back_map), bwd_map)
        step *= 2
    entry_state = lax.ppermute(fwd_shift, axis, [(i, i + 1) for i in range(count - 1)])
    exit_adjoint = lax.ppermute(bwd_shift, axis, [(i, i - 1) for i in range(1, count)])
    return entry_state, exit_adjoint


def head_ring(part, count, axis):
    return [part] + [
        lax.ppermute(part, axis, [(i, (i + k) % count) for i in range(count)])
        for k in range(1, count)
    ]


def make_body(seq_count, head_devices):
    def body(queries, raw_keys, values, write_rate, out_weight, out_grad):
        head_count = write_rate.shape[1]
        head_width = queries.shape[1] // head_count
        token_count = queries.shape[0]
        width = queries.shape[1]
        here = lax.axis_index("head")

        weight_cols = [lax.dynamic_slice_in_dim(out_weight, here * width, width, 1)]
        for k in range(1, head_devices):
            block = lax.dynamic_slice_in_dim(
                out_weight, ((here + k) % head_devices) * width, width, 1
            )
            weight_cols.append(
                lax.ppermute(
                    block, "head", [(i, (i + k) % head_devices) for i in range(head_devices)]
                )
            )
        weight_mine = jnp.concatenate(weight_cols, 0)

        grad_parts = head_ring(out_grad, head_devices, "head")
        weight_rows = jnp.concatenate(
            [
                lax.dynamic_slice_in_dim(
                    out_weight, ((here - k) % head_devices) * width, width, 1
                )
                for k in range(head_devices)
            ],
            1,
        )

        def factor_inputs(float_query, float_key, float_value, rates):
            return block_factors(
                to_blocks(float_query, head_count),
                to_blocks(float_key, head_count),
                to_blocks(float_value, head_count),
                rate_blocks(rates),
            )

        factors, pull_factors = jax.vjp(
            factor_inputs,
            queries.astype(jnp.float32),
            raw_keys.astype(jnp.float32),
            values.astype(jnp.float32),
            write_rate,
        )
        unit_query, unit_key, key_mix, value_mix, causal_scores = factors
        identity_heads = jnp.broadcast_to(
            jnp.eye(head_width, dtype=jnp.float32), (head_count, head_width, head_width)
        )
        zero_heads = jnp.zeros((head_count, head_width, head_width), jnp.float32)
        widened = (
            unit_query,
            unit_key,
            key_mix,
            jnp.concatenate([jnp.zeros_like(value_mix), value_mix], -1),
            causal_scores,
        )
        joined_state, joined_outputs = run_blocks(
            widened, jnp.concatenate([identity_heads, zero_heads], -1)
        )
        transition = joined_state[..., :head_width]
        offset = joined_state[..., head_width:]
        query_effect = joined_outputs[..., :head_width]
        attended_grad = lax.dot_general(
            jnp.concatenate(grad_parts, 1),
            weight_rows,
            (((1,), (1,)), ((), ())),
            preferred_element_type=jnp.float32,
        )
        grad_blocks = attended_grad.reshape(
            token_count // BLOCK, BLOCK, head_count, head_width
        ).transpose(0, 2, 1, 3)
        local_adjoint = jnp.einsum("nhcd,nhce->hde", query_effect, grad_blocks, precision=highest)
        entry_state, exit_adjoint = scan_both(transition, offset, local_adjoint, seq_count, "seq")

        def run_from_entry(factor_tuple):
            return run_blocks(factor_tuple, entry_state)

        (final_state, block_outputs), pull_run = jax.vjp(run_from_entry, factors)
        attended_bf = from_blocks(block_outputs).astype(jnp.bfloat16)
        attended_parts = head_ring(attended_bf, head_devices, "head")
        layer_out = jnp.dot(
            jnp.concatenate(attended_parts, 1), weight_mine, preferred_element_type=jnp.float32
        ).astype(jnp.bfloat16)
        factor_grads = pull_run((exit_adjoint, grad_blocks))
        query_part, key_part, value_part, rate_grad = pull_factors(factor_grads[0])
        return (
            layer_out,
            query_part.astype(jnp.bfloat16),
            key_part.astype(jnp.bfloat16),
            value_part.astype(jnp.bfloat16),
            rate_grad,
        )

    return body


def solution(mesh):
    placed = (
        P("seq", "head"),
        P("seq", "head"),
        P("seq", "head"),
        P("seq", "head"),
        P("head", None),
        P("seq", "head"),
    )
    return jax.shard_map(
        make_body(mesh.shape["seq"], mesh.shape["head"]),
        mesh=mesh,
        in_specs=placed,
        out_specs=(
            P("seq", "head"),
            P("seq", "head"),
            P("seq", "head"),
            P("seq", "head"),
            P("seq", "head"),
        ),
        check_vma=False,
    )
```

time: 508 us -> 196 us (0.39)
  waiting for transfers between devices: 346 us -> 43.2 us
  starting transfers between devices: 0.2 us -> 94.2 us
  matrix products: 115 us -> 38.7 us
  blocking collectives: 12.6 us -> 0 us
  between operations: 14.6 us -> 2.08 us
    all_gather x4 -> x0, waiting for transfers between devices: 267 us -> none  [prefix(): gathered = jax.tree.map(lambda a: lax.all_gather(a, axis), part)]
    ppermute x0 -> x33, starting transfers between devices: none -> 94.2 us  [the longest x10 38.3 us: scan_both(): back_map, back_shift = lax.ppermute((bwd_map, bwd_shift), axis, behind)]
    reduce_scatter x1 -> x0, waiting for transfers between devices: 77.4 us -> none  [body(): lax.psum_scatter(partial_out, 'head', scatter_dimension=1, tiled=True)]
    dot_general x65 -> x24, matrix products: 79.6 us -> 11.5 us  [the longest x22 8.44 us: mm(): return jnp.einsum('hij,hjk->hik', left, right, precision=highest)]
    ppermute x0 -> x33, waiting for transfers between devices: none -> 43.2 us  [the longest x10 29.7 us: scan_both(): got_map, got_shift = lax.ppermute((fwd_map, fwd_shift), axis, ahead)]
    all_gather x1 -> x0, blocking collectives: 12.6 us -> none  [body(): lax.all_gather(out_grad, 'head', axis=1, tiled=True)]
    unnamed x47 -> x52, local copies, waits for them, and re-layouts: 2.4 us -> 9.07 us
  transfers between devices with their start and end apart: 5 -> 33, of which waited for: 5 -> 13; matrix products, arithmetic and copies ran while one was open for 13% -> 23% of each run, Pallas kernels for 0% -> 0%
where the time goes in v1:
time: 196 us; the launch traced here: 193 us
  starting transfers between devices  94.2 us (48%)
  waiting for transfers between devices  43.2 us (22%)
  matrix products  38.7 us (20%)
  local copies, waits for them, and re-layouts  12.4 us (6%)
  between operations  2.08 us (1%)
    ppermute x10, starting transfers between devices, scan_both(): back_map, back_shift = lax.ppermute((bwd_map, bwd_shift), axis, behind)  38.3 us
    ppermute x10, starting transfers between devices, scan_both(): got_map, got_shift = lax.ppermute((fwd_map, fwd_shift), axis, ahead)  34.3 us
    ppermute x10, waiting for transfers between devices, scan_both(): got_map, got_shift = lax.ppermute((fwd_map, fwd_shift), axis, ahead)  29.7 us
    ppermute x6, starting transfers between devices, head_ring(): lax.ppermute(part, axis, [(i, (i + k) % count) for i in range(count)])  11.4 us
    unnamed x52, local copies, waits for them, and re-layouts  9.07 us
    ppermute x10, waiting for transfers between devices, scan_both(): back_map, back_shift = lax.ppermute((bwd_map, bwd_shift), axis, behind)  8.6 us
    dot_general x22, matrix products, mm(): return jnp.einsum('hij,hjk->hik', left, right, precision=highest)  8.44 us
    dot_general x15, matrix products, block_factors(): jnp.einsum('hnij,hnjk->hnik', power_term, power_term, precision=highest)  4.96 us
  transfers between devices with their start and end apart: 33, of which 13 were waited for; matrix products, arithmetic and copies ran while one was open for 23% of the time, Pallas kernels for 0%

profile of v1, /device:TPU:8, one launch (start us, length us, event | category | flops | bytes accessed | tf_op | source)
XLA Modules:
  0.0 192.7 jit_solution(1385322692409679026)
XLA Ops:
  2.2 2.7 %collective-permute-start.19 = (bf16[128,256]{1,0:T(8,128)(2,1)}, bf16[128,256]{1,0:T(8,128)(2,1)}, u32[]{:S(2)}, u32[]{:S(2)}) collective-permute-start(bf16[128,256]{1,0:T(8,128)(2,1)} %param.17), channel_id=1, source_target_pairs={{0,2},{1,3},{2,0},{3,1},{4,6},{5,7},{6,4},{7,5},{8,10},{9,11},{10,... | collective-permute-start | bytes 196616 | tf_op jit(solution)/shard_map/ppermute | solution.py:105
  15.7 4.0 %while.52 = (s32[]{:T(128)}, f32[2,128,256]{2,1,0:T(8,128)S(1)}, f32[2,2,64,256]{3,2,0,1:T(8,128)}, f32[2,2,64,128]{3,2,1,0:T(8,128)S(1)}, f32[2,2,64,256]{3,2,0...) while((s32[]{:T(128)}, f32[2,128,256]{2,1,0:T(8,128)S(1)}, ...), condition=%wide.region_3.4_spmd, body=%wide.region_2.3_spmd.sunk | while | flops 176291840 | bytes 2230373 | solution.py:70
  20.5 6.2 %collective-permute-start.22 = (f32[2,128,128]{1,2,0:T(8,128)}, f32[2,128,128]{1,2,0:T(8,128)}, u32[]{:S(2)}, u32[]{:S(2)}) collective-permute-start(f32[2,128,128]{1,2,0:T(8,128)} %get-tuple-element.532), channel_id=1, source_target_pairs={{4,0},{8,4},{12,8},{16,12},{20,16},{24,20},{28,24},{32,28},{36,32}... | collective-permute-start | bytes 393224 | tf_op jit(solution)/shard_map/ppermute | solution.py:91
  39.6 4.4 %collective-permute-start.21 = (f32[2,128,128]{2,1,0:T(8,128)S(1)}, f32[2,128,128]{2,1,0:T(8,128)S(1)}, u32[]{:S(2)}, u32[]{:S(2)}) collective-permute-start(f32[2,128,128]{2,1,0:T(8,128)S(1)} %convolution_bitcast_fusion.4), channel_id=1, source_target_pairs={{4,0},{8,4},{12,8},{16,12},{20,16},{24,20},{28,24},{32,28},{36,32}... | collective-permute-start | bytes 393224 | tf_op jit(solution)/shard_map/ppermute | solution.py:91
  45.1 2.9 %collective-permute-start.24 = (f32[2,128,128]{1,2,0:T(8,128)S(1)}, f32[2,128,128]{1,2,0:T(8,128)S(1)}, u32[]{:S(2)}, u32[]{:S(2)}) collective-permute-start(f32[2,128,128]{1,2,0:T(8,128)S(1)} %convolution_select_fusion.9), channel_id=1, source_target_pairs={{8,0},{12,4},{16,8},{20,12},{24,16},{28,20},{32,24},{36,28},{40,32... | collective-permute-start | bytes 393224 | tf_op jit(solution)/shard_map/ppermute | solution.py:91
  49.2 3.0 %collective-permute-start.2 = (f32[2,128,128]{2,1,0:T(8,128)S(1)}, f32[2,128,128]{2,1,0:T(8,128)S(1)}, u32[]{:S(2)}, u32[]{:S(2)}) collective-permute-start(f32[2,128,128]{2,1,0:T(8,128)S(1)} %convolution_add_fusion.38), channel_id=1, source_target_pairs={{0,8},{4,12},{8,16},{12,20},{16,24},{20,28},{24,32},{28,36},{32,40... | collective-permute-start | bytes 393224 | tf_op jit(solution)/shard_map/ppermute | solution.py:90
  52.6 6.2 %collective-permute-done.2 = f32[2,128,128]{2,1,0:T(8,128)S(1)} collective-permute-done((f32[2,128,128]{2,1,0:T(8,128)S(1)}, f32[2,128,128]{2,1,0:T(8,128)S(1)}, u32[]{:S(2)}, u32[]{:S(2)}) %collective-permute-start.2) | collective-permute-done | bytes 131104 | tf_op jit(solution)/shard_map/ppermute | solution.py:90
  61.0 6.0 %collective-permute-start.23 = (f32[2,128,128]{2,1,0:T(8,128)S(1)}, f32[2,128,128]{2,1,0:T(8,128)S(1)}, u32[]{:S(2)}, u32[]{:S(2)}) collective-permute-start(f32[2,128,128]{2,1,0:T(8,128)S(1)} %convolution_add_fusion.32), channel_id=1, source_target_pairs={{8,0},{12,4},{16,8},{20,12},{24,16},{28,20},{32,24},{36,28},{40,32... | collective-permute-start | bytes 393224 | tf_op jit(solution)/shard_map/ppermute | solution.py:91
  70.2 2.9 %collective-permute-done.23 = f32[2,128,128]{2,1,0:T(8,128)S(1)} collective-permute-done((f32[2,128,128]{2,1,0:T(8,128)S(1)}, f32[2,128,128]{2,1,0:T(8,128)S(1)}, u32[]{:S(2)}, u32[]{:S(2)}) %collective-permute-start.23) | collective-permute-done | bytes 131104 | tf_op jit(solution)/shard_map/ppermute | solution.py:91
  75.4 7.6 %collective-permute-done.4 = f32[2,128,128]{2,1,0:T(8,128)S(1)} collective-permute-done((f32[2,128,128]{2,1,0:T(8,128)S(1)}, f32[2,128,128]{2,1,0:T(8,128)S(1)}, u32[]{:S(2)}, u32[]{:S(2)}) %collective-permute-start.4) | collective-permute-done | bytes 131104 | tf_op jit(solution)/shard_map/ppermute | solution.py:90
  85.2 6.9 %collective-permute-start.25 = (f32[2,128,128]{2,1,0:T(8,128)S(1)}, f32[2,128,128]{2,1,0:T(8,128)S(1)}, u32[]{:S(2)}, u32[]{:S(2)}) collective-permute-start(f32[2,128,128]{2,1,0:T(8,128)S(1)} %convolution_add_fusion.31), channel_id=1, source_target_pairs={{16,0},{20,4},{24,8},{28,12},{32,16},{36,20},{40,24},{44,28},{48,3... | collective-permute-start | bytes 393224 | tf_op jit(solution)/shard_map/ppermute | solution.py:91
  92.4 4.3 %collective-permute-done.5 = f32[2,128,128]{2,1,0:T(8,128)S(1)} collective-permute-done((f32[2,128,128]{2,1,0:T(8,128)S(1)}, f32[2,128,128]{2,1,0:T(8,128)S(1)}, u32[]{:S(2)}, u32[]{:S(2)}) %collective-permute-start.5) | collective-permute-done | bytes 131104 | tf_op jit(solution)/shard_map/ppermute | solution.py:90
  98.9 7.8 %collective-permute-start.6 = (f32[2,128,128]{2,1,0:T(8,128)S(1)}, f32[2,128,128]{2,1,0:T(8,128)S(1)}, u32[]{:S(2)}, u32[]{:S(2)}) collective-permute-start(f32[2,128,128]{2,1,0:T(8,128)S(1)} %convolution_add_fusion.36), channel_id=1, source_target_pairs={{0,32},{4,36},{8,40},{12,44},{16,48},{20,52},{24,56},{28,60},{32,6... | collective-permute-start | bytes 393224 | tf_op jit(solution)/shard_map/ppermute | solution.py:90
  107.1 3.5 %collective-permute-done.6 = f32[2,128,128]{2,1,0:T(8,128)S(1)} collective-permute-done((f32[2,128,128]{2,1,0:T(8,128)S(1)}, f32[2,128,128]{2,1,0:T(8,128)S(1)}, u32[]{:S(2)}, u32[]{:S(2)}) %collective-permute-start.6) | collective-permute-done | bytes 131104 | tf_op jit(solution)/shard_map/ppermute | solution.py:90
  110.6 6.9 %collective-permute-start.7 = (f32[2,128,128]{2,1,0:T(8,128)S(1)}, f32[2,128,128]{2,1,0:T(8,128)S(1)}, u32[]{:S(2)}, u32[]{:S(2)}) collective-permute-start(f32[2,128,128]{2,1,0:T(8,128)S(1)} %convolution_select_fusion.6), channel_id=1, source_target_pairs={{0,32},{4,36},{8,40},{12,44},{16,48},{20,52},{24,56},{28,60},{32,6... | collective-permute-start | bytes 393224 | tf_op jit(solution)/shard_map/ppermute | solution.py:90
  117.9 3.7 %collective-permute-start.27 = (f32[2,128,128]{2,1,0:T(8,128)S(1)}, f32[2,128,128]{2,1,0:T(8,128)S(1)}, u32[]{:S(2)}, u32[]{:S(2)}) collective-permute-start(f32[2,128,128]{2,1,0:T(8,128)S(1)} %convolution_add_fusion.30), channel_id=1, source_target_pairs={{32,0},{36,4},{40,8},{44,12},{48,16},{52,20},{56,24},{60,28},{64,3... | collective-permute-start | bytes 393224 | tf_op jit(solution)/shard_map/ppermute | solution.py:91
  124.6 4.2 %collective-permute-done.27 = f32[2,128,128]{2,1,0:T(8,128)S(1)} collective-permute-done((f32[2,128,128]{2,1,0:T(8,128)S(1)}, f32[2,128,128]{2,1,0:T(8,128)S(1)}, u32[]{:S(2)}, u32[]{:S(2)}) %collective-permute-start.27) | collective-permute-done | bytes 131104 | tf_op jit(solution)/shard_map/ppermute | solution.py:91
  128.7 3.3 %collective-permute-start.8 = (f32[2,128,128]{2,1,0:T(8,128)S(1)}, f32[2,128,128]{2,1,0:T(8,128)S(1)}, u32[]{:S(2)}, u32[]{:S(2)}) collective-permute-start(f32[2,128,128]{2,1,0:T(8,128)S(1)} %convolution_add_fusion.35), channel_id=1, source_target_pairs={{0,64},{4,68},{8,72},{12,76},{16,80},{20,84},{24,88},{28,92},{32,9... | collective-permute-start | bytes 393224 | tf_op jit(solution)/shard_map/ppermute | solution.py:90
  132.5 4.0 %collective-permute-done.8 = f32[2,128,128]{2,1,0:T(8,128)S(1)} collective-permute-done((f32[2,128,128]{2,1,0:T(8,128)S(1)}, f32[2,128,128]{2,1,0:T(8,128)S(1)}, u32[]{:S(2)}, u32[]{:S(2)}) %collective-permute-start.8) | collective-permute-done | bytes 131104 | tf_op jit(solution)/shard_map/ppermute | solution.py:90
  136.5 3.6 %collective-permute-start.9 = (f32[2,128,128]{2,1,0:T(8,128)S(1)}, f32[2,128,128]{2,1,0:T(8,128)S(1)}, u32[]{:S(2)}, u32[]{:S(2)}) collective-permute-start(f32[2,128,128]{2,1,0:T(8,128)S(1)} %convolution_select_fusion.5), channel_id=1, source_target_pairs={{0,64},{4,68},{8,72},{12,76},{16,80},{20,84},{24,88},{28,92},{32,9... | collective-permute-start | bytes 393224 | tf_op jit(solution)/shard_map/ppermute | solution.py:90
  143.8 3.0 %collective-permute-start.10 = (f32[2,128,128]{2,1,0:T(8,128)S(1)}, f32[2,128,128]{2,1,0:T(8,128)S(1)}, u32[]{:S(2)}, u32[]{:S(2)}) collective-permute-start(f32[2,128,128]{2,1,0:T(8,128)S(1)} %convolution_add_fusion.34), channel_id=1, source_target_pairs={{0,128},{4,132},{8,136},{12,140},{16,144},{20,148},{24,152},{28,15... | collective-permute-start | bytes 393224 | tf_op jit(solution)/shard_map/ppermute | solution.py:87
  152.5 4.9 %collective-permute-done.31 = f32[2,128,128]{2,1,0:T(8,128)S(1)} collective-permute-done((f32[2,128,128]{2,1,0:T(8,128)S(1)}, f32[2,128,128]{2,1,0:T(8,128)S(1)}, u32[]{:S(2)}, u32[]{:S(2)}) %collective-permute-start.31) | collective-permute-done | bytes 131104 | tf_op jit(solution)/shard_map/ppermute | solution.py:88
  166.4 5.4 %while.54 = (s32[]{:T(128)}, f32[2,128,128]{2,1,0:T(8,128)S(1)}, f32[2,2,64,128]{3,2,0,1:T(8,128)S(1)}, f32[2,2,64,128]{3,2,0,1:T(8,128)S(1)}, f32[2,2,64,128]{3...) while((s32[]{:T(128)}, f32[2,128,128]{2,1,0:T(8,128)S(1)}, ...), condition=%wide.region_7.8_spmd, body=%wide.region_6.7_spmd.sunk | while | flops 176275456 | bytes 2367137 | solution.py:70
  185.4 2.4 %collective-permute-start.14 = (bf16[128,256]{1,0:T(8,128)(2,1)S(1)}, bf16[128,256]{1,0:T(8,128)(2,1)S(1)}, u32[]{:S(2)}, u32[]{:S(2)}) collective-permute-start(bf16[128,256]{1,0:T(8,128)(2,1)S(1)} %bitcast.495), channel_id=1, source_target_pairs={{0,3},{1,0},{2,1},{3,2},{4,7},{5,4},{6,5},{7,6},{8,11},{9,8},{10,9... | collective-permute-start | bytes 196616 | tf_op jit(solution)/shard_map/ppermute | solution.py:105
  (244 shorter events, 92.1 us)
Async XLA Ops:
  0.6 29.8 %collective-permute-start.18 = (bf16[128,256]{1,0:T(8,128)(2,1)}, bf16[128,256]{1,0:T(8,128)(2,1)}, u32[]{:S(2)}, u32[]{:S(2)}) collective-permute-start(bf16[128,256]{1,0:T(8,128)(2,1)} %param.17), channel_id=1, source_target_pairs={{0,1},{1,2},{2,3},{3,0},{4,5},{5,6},{6,7},{7,4},{8,9},{9,10},{10,1... | collective-permute-start | bytes 196616 | tf_op jit(solution)/shard_map/ppermute | solution.py:105
  2.2 30.1 %collective-permute-start.19 = (bf16[128,256]{1,0:T(8,128)(2,1)}, bf16[128,256]{1,0:T(8,128)(2,1)}, u32[]{:S(2)}, u32[]{:S(2)}) collective-permute-start(bf16[128,256]{1,0:T(8,128)(2,1)} %param.17), channel_id=1, source_target_pairs={{0,2},{1,3},{2,0},{3,1},{4,6},{5,7},{6,4},{7,5},{8,10},{9,11},{10,... | collective-permute-start | bytes 196616 | tf_op jit(solution)/shard_map/ppermute | solution.py:105
  4.9 28.0 %collective-permute-start.20 = (bf16[128,256]{1,0:T(8,128)(2,1)}, bf16[128,256]{1,0:T(8,128)(2,1)}, u32[]{:S(2)}, u32[]{:S(2)}) collective-permute-start(bf16[128,256]{1,0:T(8,128)(2,1)} %param.17), channel_id=1, source_target_pairs={{0,3},{1,0},{2,1},{3,2},{4,7},{5,4},{6,5},{7,6},{8,11},{9,8},{10,9... | collective-permute-start | bytes 196616 | tf_op jit(solution)/shard_map/ppermute | solution.py:105
  20.5 19.1 %collective-permute-start.22 = (f32[2,128,128]{1,2,0:T(8,128)}, f32[2,128,128]{1,2,0:T(8,128)}, u32[]{:S(2)}, u32[]{:S(2)}) collective-permute-start(f32[2,128,128]{1,2,0:T(8,128)} %get-tuple-element.532), channel_id=1, source_target_pairs={{4,0},{8,4},{12,8},{16,12},{20,16},{24,20},{28,24},{32,28},{36,32}... | collective-permute-start | bytes 393224 | tf_op jit(solution)/shard_map/ppermute | solution.py:91
  26.7 18.4 %collective-permute-start.1 = (f32[2,128,128]{2,1,0:T(8,128)}, f32[2,128,128]{2,1,0:T(8,128)}, u32[]{:S(2)}, u32[]{:S(2)}) collective-permute-start(f32[2,128,128]{2,1,0:T(8,128)} %get-tuple-element.533), channel_id=1, source_target_pairs={{0,4},{4,8},{8,12},{12,16},{16,20},{20,24},{24,28},{28,32},{32,36}... | collective-permute-start | bytes 393224 | tf_op jit(solution)/shard_map/ppermute | solution.py:90
  32.3 153.1 %collective-permute-start.15 = (bf16[256,256]{1,0:T(8,128)(2,1)}, bf16[256,256]{1,0:T(8,128)(2,1)}, u32[]{:S(2)}, u32[]{:S(2)}) collective-permute-start(bf16[256,256]{1,0:T(8,128)(2,1)} %get-tuple-element.528), channel_id=1, source_target_pairs={{0,1},{1,2},{2,3},{3,0},{4,5},{5,6},{6,7},{7,4},{8,9},{9,10},{10,1... | collective-permute-start | bytes 393224 | tf_op jit(solution)/shard_map/ppermute | solution.py:124
  33.0 157.6 %collective-permute-start.16 = (bf16[256,256]{1,0:T(8,128)(2,1)}, bf16[256,256]{1,0:T(8,128)(2,1)}, u32[]{:S(2)}, u32[]{:S(2)}) collective-permute-start(bf16[256,256]{1,0:T(8,128)(2,1)} %get-tuple-element.527), channel_id=1, source_target_pairs={{0,2},{1,3},{2,0},{3,1},{4,6},{5,7},{6,4},{7,5},{8,10},{9,11},{10,... | collective-permute-start | bytes 393224 | tf_op jit(solution)/shard_map/ppermute | solution.py:124
  39.0 151.6 %collective-permute-start.17 = (bf16[256,256]{1,0:T(8,128)(2,1)}, bf16[256,256]{1,0:T(8,128)(2,1)}, u32[]{:S(2)}, u32[]{:S(2)}) collective-permute-start(bf16[256,256]{1,0:T(8,128)(2,1)} %get-tuple-element.526), channel_id=1, source_target_pairs={{0,3},{1,0},{2,1},{3,2},{4,7},{5,4},{6,5},{7,6},{8,11},{9,8},{10,9... | collective-permute-start | bytes 393224 | tf_op jit(solution)/shard_map/ppermute | solution.py:124
  39.6 9.6 %collective-permute-start.21 = (f32[2,128,128]{2,1,0:T(8,128)S(1)}, f32[2,128,128]{2,1,0:T(8,128)S(1)}, u32[]{:S(2)}, u32[]{:S(2)}) collective-permute-start(f32[2,128,128]{2,1,0:T(8,128)S(1)} %convolution_bitcast_fusion.4), channel_id=1, source_target_pairs={{4,0},{8,4},{12,8},{16,12},{20,16},{24,20},{28,24},{32,28},{36,32}... | collective-permute-start | bytes 393224 | tf_op jit(solution)/shard_map/ppermute | solution.py:91
  45.1 15.9 %collective-permute-start.24 = (f32[2,128,128]{1,2,0:T(8,128)S(1)}, f32[2,128,128]{1,2,0:T(8,128)S(1)}, u32[]{:S(2)}, u32[]{:S(2)}) collective-permute-start(f32[2,128,128]{1,2,0:T(8,128)S(1)} %convolution_select_fusion.9), channel_id=1, source_target_pairs={{8,0},{12,4},{16,8},{20,12},{24,16},{28,20},{32,24},{36,28},{40,32... | collective-permute-start | bytes 393224 | tf_op jit(solution)/shard_map/ppermute | solution.py:91
  49.2 9.6 %collective-permute-start.2 = (f32[2,128,128]{2,1,0:T(8,128)S(1)}, f32[2,128,128]{2,1,0:T(8,128)S(1)}, u32[]{:S(2)}, u32[]{:S(2)}) collective-permute-start(f32[2,128,128]{2,1,0:T(8,128)S(1)} %convolution_add_fusion.38), channel_id=1, source_target_pairs={{0,8},{4,12},{8,16},{12,20},{16,24},{20,28},{24,32},{28,36},{32,40... | collective-permute-start | bytes 393224 | tf_op jit(solution)/shard_map/ppermute | solution.py:90
  61.0 12.0 %collective-permute-start.23 = (f32[2,128,128]{2,1,0:T(8,128)S(1)}, f32[2,128,128]{2,1,0:T(8,128)S(1)}, u32[]{:S(2)}, u32[]{:S(2)}) collective-permute-start(f32[2,128,128]{2,1,0:T(8,128)S(1)} %convolution_add_fusion.32), channel_id=1, source_target_pairs={{8,0},{12,4},{16,8},{20,12},{24,16},{28,20},{32,24},{36,28},{40,32... | collective-permute-start | bytes 393224 | tf_op jit(solution)/shard_map/ppermute | solution.py:91
  67.8 17.4 %collective-permute-start.26 = (f32[2,128,128]{1,2,0:T(8,128)S(1)}, f32[2,128,128]{1,2,0:T(8,128)S(1)}, u32[]{:S(2)}, u32[]{:S(2)}) collective-permute-start(f32[2,128,128]{1,2,0:T(8,128)S(1)} %convolution_select_fusion.3), channel_id=1, source_target_pairs={{16,0},{20,4},{24,8},{28,12},{32,16},{36,20},{40,24},{44,28},{48,3... | collective-permute-start | bytes 393224 | tf_op jit(solution)/shard_map/ppermute | solution.py:91
  73.0 10.0 %collective-permute-start.4 = (f32[2,128,128]{2,1,0:T(8,128)S(1)}, f32[2,128,128]{2,1,0:T(8,128)S(1)}, u32[]{:S(2)}, u32[]{:S(2)}) collective-permute-start(f32[2,128,128]{2,1,0:T(8,128)S(1)} %convolution_add_fusion.37), channel_id=1, source_target_pairs={{0,16},{4,20},{8,24},{12,28},{16,32},{20,36},{24,40},{28,44},{32,4... | collective-permute-start | bytes 393224 | tf_op jit(solution)/shard_map/ppermute | solution.py:90
  83.0 13.7 %collective-permute-start.5 = (f32[2,128,128]{2,1,0:T(8,128)S(1)}, f32[2,128,128]{2,1,0:T(8,128)S(1)}, u32[]{:S(2)}, u32[]{:S(2)}) collective-permute-start(f32[2,128,128]{2,1,0:T(8,128)S(1)} %convolution_select_fusion.7), channel_id=1, source_target_pairs={{0,16},{4,20},{8,24},{12,28},{16,32},{20,36},{24,40},{28,44},{32,4... | collective-permute-start | bytes 393224 | tf_op jit(solution)/shard_map/ppermute | solution.py:90
  85.2 13.7 %collective-permute-start.25 = (f32[2,128,128]{2,1,0:T(8,128)S(1)}, f32[2,128,128]{2,1,0:T(8,128)S(1)}, u32[]{:S(2)}, u32[]{:S(2)}) collective-permute-start(f32[2,128,128]{2,1,0:T(8,128)S(1)} %convolution_add_fusion.31), channel_id=1, source_target_pairs={{16,0},{20,4},{24,8},{28,12},{32,16},{36,20},{40,24},{44,28},{48,3... | collective-permute-start | bytes 393224 | tf_op jit(solution)/shard_map/ppermute | solution.py:91
  96.7 21.2 %collective-permute-start.28 = (f32[2,128,128]{1,2,0:T(8,128)S(1)}, f32[2,128,128]{1,2,0:T(8,128)S(1)}, u32[]{:S(2)}, u32[]{:S(2)}) collective-permute-start(f32[2,128,128]{1,2,0:T(8,128)S(1)} %convolution_select_fusion.2), channel_id=1, source_target_pairs={{32,0},{36,4},{40,8},{44,12},{48,16},{52,20},{56,24},{60,28},{64,3... | collective-permute-start | bytes 393224 | tf_op jit(solution)/shard_map/ppermute | solution.py:91
  98.9 11.8 %collective-permute-start.6 = (f32[2,128,128]{2,1,0:T(8,128)S(1)}, f32[2,128,128]{2,1,0:T(8,128)S(1)}, u32[]{:S(2)}, u32[]{:S(2)}) collective-permute-start(f32[2,128,128]{2,1,0:T(8,128)S(1)} %convolution_add_fusion.36), channel_id=1, source_target_pairs={{0,32},{4,36},{8,40},{12,44},{16,48},{20,52},{24,56},{28,60},{32,6... | collective-permute-start | bytes 393224 | tf_op jit(solution)/shard_map/ppermute | solution.py:90
  110.6 11.7 %collective-permute-start.7 = (f32[2,128,128]{2,1,0:T(8,128)S(1)}, f32[2,128,128]{2,1,0:T(8,128)S(1)}, u32[]{:S(2)}, u32[]{:S(2)}) collective-permute-start(f32[2,128,128]{2,1,0:T(8,128)S(1)} %convolution_select_fusion.6), channel_id=1, source_target_pairs={{0,32},{4,36},{8,40},{12,44},{16,48},{20,52},{24,56},{28,60},{32,6... | collective-permute-start | bytes 393224 | tf_op jit(solution)/shard_map/ppermute | solution.py:90
  117.9 10.9 %collective-permute-start.27 = (f32[2,128,128]{2,1,0:T(8,128)S(1)}, f32[2,128,128]{2,1,0:T(8,128)S(1)}, u32[]{:S(2)}, u32[]{:S(2)}) collective-permute-start(f32[2,128,128]{2,1,0:T(8,128)S(1)} %convolution_add_fusion.30), channel_id=1, source_target_pairs={{32,0},{36,4},{40,8},{44,12},{48,16},{52,20},{56,24},{60,28},{64,3... | collective-permute-start | bytes 393224 | tf_op jit(solution)/shard_map/ppermute | solution.py:91
  122.4 18.0 %collective-permute-start.30 = (f32[2,128,128]{1,2,0:T(8,128)S(1)}, f32[2,128,128]{1,2,0:T(8,128)S(1)}, u32[]{:S(2)}, u32[]{:S(2)}) collective-permute-start(f32[2,128,128]{1,2,0:T(8,128)S(1)} %convolution_select_fusion.1), channel_id=1, source_target_pairs={{64,0},{68,4},{72,8},{76,12},{80,16},{84,20},{88,24},{92,28},{96,3... | collective-permute-start | bytes 393224 | tf_op jit(solution)/shard_map/ppermute | solution.py:91
  150.6 9.1 %collective-permute-start.11 = (f32[2,128,128]{2,1,0:T(8,128)S(1)}, f32[2,128,128]{2,1,0:T(8,128)S(1)}, u32[]{:S(2)}, u32[]{:S(2)}) collective-permute-start(f32[2,128,128]{2,1,0:T(8,128)S(1)} %convolution_add_fusion.33), channel_id=1, source_target_pairs={{0,4},{4,8},{8,12},{12,16},{16,20},{20,24},{24,28},{28,32},{32,36}... | collective-permute-start | bytes 393224 | tf_op jit(solution)/shard_map/ppermute | solution.py:98
  163.0 27.6 %collective-permute-start.12 = (bf16[128,256]{1,0:T(8,128)(2,1)S(1)}, bf16[128,256]{1,0:T(8,128)(2,1)S(1)}, u32[]{:S(2)}, u32[]{:S(2)}) collective-permute-start(bf16[128,256]{1,0:T(8,128)(2,1)S(1)} %bitcast.493), channel_id=1, source_target_pairs={{0,1},{1,2},{2,3},{3,0},{4,5},{5,6},{6,7},{7,4},{8,9},{9,10},{10,1... | collective-permute-start | bytes 196616 | tf_op jit(solution)/shard_map/ppermute | solution.py:105
  164.1 26.5 %collective-permute-start.13 = (bf16[128,256]{1,0:T(8,128)(2,1)S(1)}, bf16[128,256]{1,0:T(8,128)(2,1)S(1)}, u32[]{:S(2)}, u32[]{:S(2)}) collective-permute-start(bf16[128,256]{1,0:T(8,128)(2,1)S(1)} %bitcast.494), channel_id=1, source_target_pairs={{0,2},{1,3},{2,0},{3,1},{4,6},{5,7},{6,4},{7,5},{8,10},{9,11},{10,... | collective-permute-start | bytes 196616 | tf_op jit(solution)/shard_map/ppermute | solution.py:105
  (33 other events, 110.7 us)

commit v2 on v1

--- a/solution.py
+++ b/solution.py
@@ -74,29 +74,55 @@
     return jnp.einsum("hij,hjk->hik", left, right, precision=highest)
 
 
+def mm_t(left, right):
+    return jnp.einsum("hji,hjk->hik", left, right, precision=highest)
+
+
 def scan_both(transition, offset, local_adjoint, count, axis):
     place = lax.axis_index(axis)
-    fwd_map, fwd_shift = transition, offset
-    bwd_map, bwd_shift = jnp.swapaxes(transition, 1, 2), local_adjoint
+    width = transition.shape[-1]
+    total_map, total_shift, total_adjoint = transition, offset, local_adjoint
+    entry_map = entry_state = exit_map = exit_adjoint = None
     step = 1
     while step < count:
         last = 2 * step >= count
-        ahead = [(i, i + step) for i in range(count - step)]
-        behind = [(i, i - step) for i in range(step, count)]
+        pairs = [(i, i ^ step) for i in range(count)]
+        upper = (place & step) != 0
         if last:
-            got_shift = lax.ppermute(fwd_shift, axis, ahead)
-            back_shift = lax.ppermute(bwd_shift, axis, behind)
+            sent = jnp.concatenate([total_shift, total_adjoint], -1)
         else:
-            got_map, got_shift = lax.ppermute((fwd_map, fwd_shift), axis, ahead)
-            back_map, back_shift = lax.ppermute((bwd_map, bwd_shift), axis, behind)
-        fwd_shift = fwd_shift + mm(fwd_map, got_shift)
-        bwd_shift = bwd_shift + mm(bwd_map, back_shift)
+            sent = jnp.concatenate([total_map, total_shift, total_adjoint], -1)
+        got = lax.ppermute(sent, axis, pairs)
+        mine = sent
+        low = jnp.where(upper, got, mine)
+        high = jnp.where(upper, mine, got)
+        if last:
+            low_shift = low[..., :width]
+            high_adjoint = high[..., width:]
+        else:
+            low_map, low_shift = low[..., :width], low[..., width : 2 * width]
+            high_map, high_adjoint = high[..., :width], high[..., 2 * width :]
+        if entry_map is None:
+            entry_state = jnp.where(upper, low_shift, jnp.zeros_like(low_shift))
+            exit_adjoint = jnp.where(upper, jnp.zeros_like(high_adjoint), high_adjoint)
+            if not last:
+                eye = jnp.broadcast_to(jnp.eye(width, dtype=jnp.float32), low_map.shape)
+                entry_map = jnp.where(upper, low_map, eye)
+                exit_map = jnp.where(upper, eye, jnp.swapaxes(high_map, 1, 2))
+        else:
+            entry_state = jnp.where(upper, entry_state + mm(entry_map, low_shift), entry_state)
+            exit_adjoint = jnp.where(upper, exit_adjoint, exit_adjoint + mm(exit_map, high_adjoint))
+            if not last:
+                entry_map = jnp.where(upper, mm(entry_map, low_map), entry_map)
+                exit_map = jnp.where(
+                    upper, exit_map, jnp.einsum("hij,hkj->hik", exit_map, high_map, precision=highest)
+                )
         if not last:
-            fwd_map = jnp.where(place >= step, mm(fwd_map, got_map), fwd_map)
-            bwd_map = jnp.where(place + step < count, mm(bwd_map, back_map), bwd_map)
+            joined = mm(high_map, jnp.concatenate([low_map, low_shift], -1))
+            total_map = joined[..., :width]
+            total_shift = joined[..., width:] + high[..., width : 2 * width]
+            total_adjoint = mm_t(low_map, high_adjoint) + low[..., 2 * width :]
         step *= 2
-    entry_state = lax.ppermute(fwd_shift, axis, [(i, i + 1) for i in range(count - 1)])
-    exit_adjoint = lax.ppermute(bwd_shift, axis, [(i, i - 1) for i in range(1, count)])
     return entry_state, exit_adjoint
 
 

time: 196 us -> 144 us (0.73); the launches traced: 193 us -> 143 us
  starting transfers between devices: 94.2 us -> 26.3 us
  waiting for transfers between devices: 43.2 us -> 55.2 us
  local copies, waits for them, and re-layouts: 12.4 us -> 16.6 us
  other arithmetic: 1.71 us -> 5.74 us
    ppermute x24 -> x6, starting transfers between devices: 80.7 us -> 14.6 us  [scan_both(): got = lax.ppermute(sent, axis, pairs)]
    ppermute x24 -> x6, waiting for transfers between devices: 43.2 us -> 53.1 us  [scan_both(): got = lax.ppermute(sent, axis, pairs)]
    unnamed x52 -> x69, local copies, waits for them, and re-layouts: 9.07 us -> 14.1 us
    dot_general x0 -> x9, matrix products: none -> 3.49 us  [the longest x5 1.94 us: mm_t(): return jnp.einsum('hji,hjk->hik', left, right, precision=highest)]
    dot_general x22 -> x19, matrix products: 8.44 us -> 5.5 us  [mm(): return jnp.einsum('hij,hjk->hik', left, right, precision=highest)]
    ppermute x6, starting transfers between devices: 11.4 us -> 8.52 us  [head_ring(): lax.ppermute(part, axis, [(i, (i + k) % count) for i in range(count)])]
    select_n x0 -> x5, other arithmetic: none -> 2.3 us  [scan_both(): high = jnp.where(upper, mine, got)]
    ppermute x6, waiting for transfers between devices: 0.02 us -> 2.12 us  [head_ring(): lax.ppermute(part, axis, [(i, (i + k) % count) for i in range(count)])]
  transfers between devices with their start and end apart: 33 -> 15, of which waited for: 13 -> 7; matrix products, arithmetic and copies ran while one was open for 23% -> 29% of each run, Pallas kernels for 0% -> 0%
where the time goes in v2:
time: 144 us; the launch traced here: 143 us
  waiting for transfers between devices  55.2 us (38%)
  matrix products  37.1 us (26%)
  starting transfers between devices  26.3 us (18%)
  local copies, waits for them, and re-layouts  16.6 us (12%)
  other arithmetic  5.74 us (4%)
  between operations  1.81 us (1%)
    ppermute x6, waiting for transfers between devices, scan_both(): got = lax.ppermute(sent, axis, pairs)  53.1 us
    ppermute x6, starting transfers between devices, scan_both(): got = lax.ppermute(sent, axis, pairs)  14.6 us
    unnamed x69, local copies, waits for them, and re-layouts  14.1 us
    ppermute x6, starting transfers between devices, head_ring(): lax.ppermute(part, axis, [(i, (i + k) % count) for i in range(count)])  8.52 us
    dot_general x19, matrix products, mm(): return jnp.einsum('hij,hjk->hik', left, right, precision=highest)  5.5 us
    dot_general x15, matrix products, block_factors(): jnp.einsum('hnij,hnjk->hnik', power_term, power_term, precision=highest)  4.96 us
    dot_general x15, matrix products, block_factors(): jnp.einsum('hnij,hnjk->hnik', result, power_term, precision=highest)  4.91 us
    ppermute x3, starting transfers between devices, body(): lax.ppermute(block, 'head', [(i, (i + k) % head_devices) for i in range(h...  3.24 us
  transfers between devices with their start and end apart: 15, of which 7 were waited for; matrix products, arithmetic and copies ran while one was open for 29% of the time, Pallas kernels for 0%

profile of v2, /device:TPU:8, one launch (start us, length us, event | category | flops | bytes accessed | tf_op | source)
XLA Modules:
  0.0 143.1 jit_solution(14309871841508740399)
XLA Ops:
  0.6 3.1 %collective-permute-start.1 = (bf16[128,256]{1,0:T(8,128)(2,1)}, bf16[128,256]{1,0:T(8,128)(2,1)}, u32[]{:S(2)}, u32[]{:S(2)}) collective-permute-start(bf16[128,256]{1,0:T(8,128)(2,1)} %param.17), channel_id=1, source_target_pairs={{0,2},{1,3},{2,0},{3,1},{4,6},{5,7},{6,4},{7,5},{8,10},{9,11},{10,... | collective-permute-start | bytes 196616 | tf_op jit(solution)/shard_map/ppermute | solution.py:131
  4.3 2.6 %collective-permute-start.2 = (bf16[128,256]{1,0:T(8,128)(2,1)}, bf16[128,256]{1,0:T(8,128)(2,1)}, u32[]{:S(2)}, u32[]{:S(2)}) collective-permute-start(bf16[128,256]{1,0:T(8,128)(2,1)} %param.17), channel_id=1, source_target_pairs={{0,3},{1,0},{2,1},{3,2},{4,7},{5,4},{6,5},{7,6},{8,11},{9,8},{10,9... | collective-permute-start | bytes 196616 | tf_op jit(solution)/shard_map/ppermute | solution.py:131
  17.5 2.6 %while.52 = (s32[]{:T(128)}, f32[2,128,256]{2,1,0:T(8,128)S(1)}, f32[2,2,64,256]{3,2,0,1:T(8,128)S(1)}, f32[2,2,64,128]{3,2,1,0:T(8,128)S(1)}, f32[2,2,64,256]{3...) while((s32[]{:T(128)}, f32[2,128,256]{2,1,0:T(8,128)S(1)}, ...), condition=%wide.region_3.4_spmd, body=%wide.region_2.3_spmd.sunk | while | flops 176291840 | bytes 2230381 | solution.py:70
  20.9 0.9 constant_dynamic-slice_fusion.7
  21.8 1.2 fusion.84
  24.5 1.8 %collective-permute-done.3 = f32[2,128,384]{2,1,0:T(8,128)} collective-permute-done((f32[2,128,384]{2,1,0:T(8,128)S(1)}, f32[2,128,384]{2,1,0:T(8,128)}, u32[]{:S(2)}, u32[]{:S(2)}) %collective-permute-start.3) | collective-permute-done | bytes 393248 | tf_op jit(solution)/shard_map/ppermute | solution.py:95
  26.3 1.1 broadcast_select_fusion.8
  29.7 1.9 %collective-permute-start.4 = (f32[2,128,384]{2,1,0:T(8,128)}, f32[2,128,384]{2,1,0:T(8,128)}, u32[]{:S(2)}, u32[]{:S(2)}) collective-permute-start(f32[2,128,384]{2,1,0:T(8,128)} %pad_maximum_fusion.1), channel_id=1, source_target_pairs={{0,8},{4,12},{8,0},{12,4},{16,24},{20,28},{24,16},{28,20},{32,40},... | collective-permute-start | bytes 1179656 | tf_op jit(solution)/shard_map/ppermute | solution.py:95
  31.6 3.2 %collective-permute-start.14 = (bf16[256,256]{1,0:T(8,128)(2,1)}, bf16[256,256]{1,0:T(8,128)(2,1)}, u32[]{:S(2)}, u32[]{:S(2)}) collective-permute-start(bf16[256,256]{1,0:T(8,128)(2,1)} %get-tuple-element.540), channel_id=1, source_target_pairs={{0,3},{1,0},{2,1},{3,2},{4,7},{5,4},{6,5},{7,6},{8,11},{9,8},{10,9... | collective-permute-start | bytes 393224 | tf_op jit(solution)/shard_map/ppermute | solution.py:150
  35.5 1.7 %copy.170 = f32[2,128,128]{1,2,0:T(8,128)} copy(f32[2,128,128]{2,1,0:T(8,128)} %get-tuple-element.542) | data formatting | bytes 262144
  37.2 4.1 %collective-permute-done.4 = f32[2,128,384]{2,1,0:T(8,128)} collective-permute-done((f32[2,128,384]{2,1,0:T(8,128)}, f32[2,128,384]{2,1,0:T(8,128)}, u32[]{:S(2)}, u32[]{:S(2)}) %collective-permute-start.4) | collective-permute-done | bytes 393248 | tf_op jit(solution)/shard_map/ppermute | solution.py:95
  41.4 1.1 broadcast_select_fusion.6
  43.9 3.4 %collective-permute-start.5 = (f32[2,128,384]{2,1,0:T(8,128)S(1)}, f32[2,128,384]{2,1,0:T(8,128)S(1)}, u32[]{:S(2)}, u32[]{:S(2)}) collective-permute-start(f32[2,128,384]{2,1,0:T(8,128)S(1)} %pad_maximum_fusion.2), channel_id=1, source_target_pairs={{0,16},{4,20},{8,24},{12,28},{16,0},{20,4},{24,8},{28,12},{32,48},... | collective-permute-start | bytes 1179656 | tf_op jit(solution)/shard_map/ppermute | solution.py:95
  47.9 16.4 %collective-permute-done.5 = f32[2,128,384]{2,1,0:T(8,128)S(1)} collective-permute-done((f32[2,128,384]{2,1,0:T(8,128)S(1)}, f32[2,128,384]{2,1,0:T(8,128)S(1)}, u32[]{:S(2)}, u32[]{:S(2)}) %collective-permute-start.5) | collective-permute-done | bytes 393248 | tf_op jit(solution)/shard_map/ppermute | solution.py:95
  65.8 6.3 %collective-permute-start.6 = (f32[2,128,384]{2,1,0:T(8,128)S(1)}, f32[2,128,384]{2,1,0:T(8,128)S(1)}, u32[]{:S(2)}, u32[]{:S(2)}) collective-permute-start(f32[2,128,384]{2,1,0:T(8,128)S(1)} %pad_maximum_fusion.3), channel_id=1, source_target_pairs={{0,32},{4,36},{8,40},{12,44},{16,48},{20,52},{24,56},{28,60},{32,0... | collective-permute-start | bytes 1179656 | tf_op jit(solution)/shard_map/ppermute | solution.py:95
  72.8 16.7 %collective-permute-done.6 = f32[2,128,384]{2,1,0:T(8,128)S(1)} collective-permute-done((f32[2,128,384]{2,1,0:T(8,128)S(1)}, f32[2,128,384]{2,1,0:T(8,128)S(1)}, u32[]{:S(2)}, u32[]{:S(2)}) %collective-permute-start.6) | collective-permute-done | bytes 393248 | tf_op jit(solution)/shard_map/ppermute | solution.py:95
  92.1 8.9 %collective-permute-done.7 = f32[2,128,384]{2,1,0:T(8,128)S(1)} collective-permute-done((f32[2,128,384]{2,1,0:T(8,128)S(1)}, f32[2,128,384]{2,1,0:T(8,128)S(1)}, u32[]{:S(2)}, u32[]{:S(2)}) %collective-permute-start.7) | collective-permute-done | bytes 393248 | tf_op jit(solution)/shard_map/ppermute | solution.py:95
  102.4 2.3 %collective-permute-start.8 = (f32[2,128,256]{2,1,0:T(8,128)S(1)}, f32[2,128,256]{2,1,0:T(8,128)S(1)}, u32[]{:S(2)}, u32[]{:S(2)}) collective-permute-start(f32[2,128,256]{2,1,0:T(8,128)S(1)} %pad_maximum_fusion.5), channel_id=1, source_target_pairs={{0,128},{4,132},{8,136},{12,140},{16,144},{20,148},{24,152},{28,15... | collective-permute-start | bytes 786440 | tf_op jit(solution)/shard_map/ppermute | solution.py:95
  105.3 5.1 %collective-permute-done.8 = f32[2,128,256]{2,1,0:T(8,128)S(1)} collective-permute-done((f32[2,128,256]{2,1,0:T(8,128)S(1)}, f32[2,128,256]{2,1,0:T(8,128)S(1)}, u32[]{:S(2)}, u32[]{:S(2)}) %collective-permute-start.8) | collective-permute-done | bytes 262176 | tf_op jit(solution)/shard_map/ppermute | solution.py:95
  111.5 2.3 %while.53 = (s32[]{:T(128)}, f32[2,128,128]{2,1,0:T(8,128)S(1)}, bf16[2,2,64,128]{3,2,1,0:T(8,128)(2,1)S(1)}, f32[2,2,128,128]{3,2,1,0:T(8,128)S(1)}, f32[2,2,64...) while((s32[]{:T(128)}, f32[2,128,128]{2,1,0:T(8,128)S(1)}, ...), condition=%wide.region_5.6_spmd, body=%wide.region_4.5_spmd.sunk | while | flops 88145920 | bytes 1575041 | solution.py:70
  114.0 1.4 collective-permute-start.10
  115.7 5.4 %while.54 = (s32[]{:T(128)}, f32[2,128,128]{2,1,0:T(8,128)S(1)}, f32[2,2,64,128]{3,2,0,1:T(8,128)S(1)}, f32[2,2,64,128]{3,2,0,1:T(8,128)S(1)}, f32[2,2,64,128]{3...) while((s32[]{:T(128)}, f32[2,128,128]{2,1,0:T(8,128)S(1)}, ...), condition=%wide.region_7.8_spmd, body=%wide.region_6.7_spmd.sunk | while | flops 176275456 | bytes 2367137 | solution.py:70
  139.0 2.1 %collective-permute-done.9 = bf16[128,256]{1,0:T(8,128)(2,1)S(1)} collective-permute-done((bf16[128,256]{1,0:T(8,128)(2,1)S(1)}, bf16[128,256]{1,0:T(8,128)(2,1)S(1)}, u32[]{:S(2)}, u32[]{:S(2)}) %collective-permute-start.9) | collective-permute-done | bytes 65568 | tf_op jit(solution)/shard_map/ppermute | solution.py:131
  141.1 2.0 %convolution_convert_fusion = bf16[128,256]{1,0:T(8,128)(2,1)} fusion(bf16[256,256]{1,0:T(8,128)(2,1)} %collective-permute-done.14, bf16[256,256]{1,0:T(8,128)(2,1)} %collective-permute-done.13, bf16[256,256]{1,0:T(8,128)(2,1)} %collective-permute-done.12, bf16[256,256]{1,0:T(8,128)(2,1)S(1)} %copy-done.16, bf16[128,256]{1,0:T(8,128)(2,1)} %collective-permute-done.11, ...), kind=kOutput, calls=%fused_computation.147 | convolution fusion | flops 70287360 | bytes 851968 | tf_op jit(solution)/shard_map/dot_general | solution.py:218
  (245 shorter events, 53.6 us)
Async XLA Ops:
  0.6 21.2 %collective-permute-start.1 = (bf16[128,256]{1,0:T(8,128)(2,1)}, bf16[128,256]{1,0:T(8,128)(2,1)}, u32[]{:S(2)}, u32[]{:S(2)}) collective-permute-start(bf16[128,256]{1,0:T(8,128)(2,1)} %param.17), channel_id=1, source_target_pairs={{0,2},{1,3},{2,0},{3,1},{4,6},{5,7},{6,4},{7,5},{8,10},{9,11},{10,... | collective-permute-start | bytes 196616 | tf_op jit(solution)/shard_map/ppermute | solution.py:131
  3.7 18.1 %collective-permute-start = (bf16[128,256]{1,0:T(8,128)(2,1)}, bf16[128,256]{1,0:T(8,128)(2,1)}, u32[]{:S(2)}, u32[]{:S(2)}) collective-permute-start(bf16[128,256]{1,0:T(8,128)(2,1)} %param.17), channel_id=1, source_target_pairs={{0,1},{1,2},{2,3},{3,0},{4,5},{5,6},{6,7},{7,4},{8,9},{9,10},{10,1... | collective-permute-start | bytes 196616 | tf_op jit(solution)/shard_map/ppermute | solution.py:131
  4.3 17.5 %collective-permute-start.2 = (bf16[128,256]{1,0:T(8,128)(2,1)}, bf16[128,256]{1,0:T(8,128)(2,1)}, u32[]{:S(2)}, u32[]{:S(2)}) collective-permute-start(bf16[128,256]{1,0:T(8,128)(2,1)} %param.17), channel_id=1, source_target_pairs={{0,3},{1,0},{2,1},{3,2},{4,7},{5,4},{6,5},{7,6},{8,11},{9,8},{10,9... | collective-permute-start | bytes 196616 | tf_op jit(solution)/shard_map/ppermute | solution.py:131
  7.0 6.3 %copy-start.13 = (f32[64,64]{1,0:T(8,128)}, f32[64,64]{1,0:T(8,128)S(1)}, u32[]{:S(2)}) copy-start(f32[64,64]{1,0:T(8,128)S(1)} %fusion.229) | copy-start | bytes 49156
  7.9 3.6 %copy-start.17 = (pred[64,64]{1,0:T(8,128)(4,1)}, pred[64,64]{1,0:T(8,128)(4,1)S(1)}, u32[]{:S(2)}) copy-start(pred[64,64]{1,0:T(8,128)(4,1)S(1)} %iota_compare_fusion.2) | copy-start | bytes 12292
  10.8 6.2 %copy-start.24 = (f32[2,2,64]{2,1,0:T(2,128)}, f32[2,2,64]{2,1,0:T(2,128)S(1)}, u32[]{:S(2)}) copy-start(f32[2,2,64]{2,1,0:T(2,128)S(1)} %get-tuple-element.555) | copy-start | bytes 3076
  17.5 3.4 %copy-start = (bf16[256,1024]{1,0:T(8,128)(2,1)S(1)}, bf16[256,1024]{1,0:T(8,128)(2,1)}, u32[]{:S(2)}) copy-start(bf16[256,1024]{1,0:T(8,128)(2,1)} %param.16) | copy-start | bytes 1572868
  23.0 1.0 copy-start.20
  24.4 1.9 %collective-permute-start.3 = (f32[2,128,384]{2,1,0:T(8,128)S(1)}, f32[2,128,384]{2,1,0:T(8,128)}, u32[]{:S(2)}, u32[]{:S(2)}) collective-permute-start(f32[2,128,384]{2,1,0:T(8,128)S(1)} %pad_maximum_fusion), channel_id=1, source_target_pairs={{0,4},{4,0},{8,12},{12,8},{16,20},{20,16},{24,28},{28,24},{32,36},... | collective-permute-start | bytes 1179656 | tf_op jit(solution)/shard_map/ppermute | solution.py:95
  29.7 11.7 %collective-permute-start.4 = (f32[2,128,384]{2,1,0:T(8,128)}, f32[2,128,384]{2,1,0:T(8,128)}, u32[]{:S(2)}, u32[]{:S(2)}) collective-permute-start(f32[2,128,384]{2,1,0:T(8,128)} %pad_maximum_fusion.1), channel_id=1, source_target_pairs={{0,8},{4,12},{8,0},{12,4},{16,24},{20,28},{24,16},{28,20},{32,40},... | collective-permute-start | bytes 1179656 | tf_op jit(solution)/shard_map/ppermute | solution.py:95
  31.6 103.8 %collective-permute-start.12 = (bf16[256,256]{1,0:T(8,128)(2,1)}, bf16[256,256]{1,0:T(8,128)(2,1)}, u32[]{:S(2)}, u32[]{:S(2)}) collective-permute-start(bf16[256,256]{1,0:T(8,128)(2,1)} %get-tuple-element.535), channel_id=1, source_target_pairs={{0,1},{1,2},{2,3},{3,0},{4,5},{5,6},{6,7},{7,4},{8,9},{9,10},{10,1... | collective-permute-start | bytes 393224 | tf_op jit(solution)/shard_map/ppermute | solution.py:150
  31.6 107.3 %collective-permute-start.14 = (bf16[256,256]{1,0:T(8,128)(2,1)}, bf16[256,256]{1,0:T(8,128)(2,1)}, u32[]{:S(2)}, u32[]{:S(2)}) collective-permute-start(bf16[256,256]{1,0:T(8,128)(2,1)} %get-tuple-element.540), channel_id=1, source_target_pairs={{0,3},{1,0},{2,1},{3,2},{4,7},{5,4},{6,5},{7,6},{8,11},{9,8},{10,9... | collective-permute-start | bytes 393224 | tf_op jit(solution)/shard_map/ppermute | solution.py:150
  34.9 104.1 %collective-permute-start.13 = (bf16[256,256]{1,0:T(8,128)(2,1)}, bf16[256,256]{1,0:T(8,128)(2,1)}, u32[]{:S(2)}, u32[]{:S(2)}) collective-permute-start(bf16[256,256]{1,0:T(8,128)(2,1)} %get-tuple-element.541), channel_id=1, source_target_pairs={{0,2},{1,3},{2,0},{3,1},{4,6},{5,7},{6,4},{7,5},{8,10},{9,11},{10,... | collective-permute-start | bytes 393224 | tf_op jit(solution)/shard_map/ppermute | solution.py:150
  35.5 5.8 %copy-start.8 = (f32[2,128,128]{2,1,0:T(8,128)S(1)}, f32[2,128,128]{2,1,0:T(8,128)}, u32[]{:S(2)}) copy-start(f32[2,128,128]{2,1,0:T(8,128)} %copy-done.7) | copy-start | bytes 393220
  43.8 3.4 %copy-start.12 = (f32[2,128,128]{1,2,0:T(8,128)S(1)}, f32[2,128,128]{1,2,0:T(8,128)}, u32[]{:S(2)}) copy-start(f32[2,128,128]{1,2,0:T(8,128)} %copy.170) | copy-start | bytes 393220
  43.9 20.5 %collective-permute-start.5 = (f32[2,128,384]{2,1,0:T(8,128)S(1)}, f32[2,128,384]{2,1,0:T(8,128)S(1)}, u32[]{:S(2)}, u32[]{:S(2)}) collective-permute-start(f32[2,128,384]{2,1,0:T(8,128)S(1)} %pad_maximum_fusion.2), channel_id=1, source_target_pairs={{0,16},{4,20},{8,24},{12,28},{16,0},{20,4},{24,8},{28,12},{32,48},... | collective-permute-start | bytes 1179656 | tf_op jit(solution)/shard_map/ppermute | solution.py:95
  65.8 23.7 %collective-permute-start.6 = (f32[2,128,384]{2,1,0:T(8,128)S(1)}, f32[2,128,384]{2,1,0:T(8,128)S(1)}, u32[]{:S(2)}, u32[]{:S(2)}) collective-permute-start(f32[2,128,384]{2,1,0:T(8,128)S(1)} %pad_maximum_fusion.3), channel_id=1, source_target_pairs={{0,32},{4,36},{8,40},{12,44},{16,48},{20,52},{24,56},{28,60},{32,0... | collective-permute-start | bytes 1179656 | tf_op jit(solution)/shard_map/ppermute | solution.py:95
  91.0 10.0 %collective-permute-start.7 = (f32[2,128,384]{2,1,0:T(8,128)S(1)}, f32[2,128,384]{2,1,0:T(8,128)S(1)}, u32[]{:S(2)}, u32[]{:S(2)}) collective-permute-start(f32[2,128,384]{2,1,0:T(8,128)S(1)} %pad_maximum_fusion.4), channel_id=1, source_target_pairs={{0,64},{4,68},{8,72},{12,76},{16,80},{20,84},{24,88},{28,92},{32,9... | collective-permute-start | bytes 1179656 | tf_op jit(solution)/shard_map/ppermute | solution.py:95
  102.4 8.0 %collective-permute-start.8 = (f32[2,128,256]{2,1,0:T(8,128)S(1)}, f32[2,128,256]{2,1,0:T(8,128)S(1)}, u32[]{:S(2)}, u32[]{:S(2)}) collective-permute-start(f32[2,128,256]{2,1,0:T(8,128)S(1)} %pad_maximum_fusion.5), channel_id=1, source_target_pairs={{0,128},{4,132},{8,136},{12,140},{16,144},{20,148},{24,152},{28,15... | collective-permute-start | bytes 786440 | tf_op jit(solution)/shard_map/ppermute | solution.py:95
  113.9 25.1 %collective-permute-start.11 = (bf16[128,256]{1,0:T(8,128)(2,1)S(1)}, bf16[128,256]{1,0:T(8,128)(2,1)}, u32[]{:S(2)}, u32[]{:S(2)}) collective-permute-start(bf16[128,256]{1,0:T(8,128)(2,1)S(1)} %bitcast.470), channel_id=1, source_target_pairs={{0,3},{1,0},{2,1},{3,2},{4,7},{5,4},{6,5},{7,6},{8,11},{9,8},{10,9... | collective-permute-start | bytes 196616 | tf_op jit(solution)/shard_map/ppermute | solution.py:131
  114.0 25.0 %collective-permute-start.10 = (bf16[128,256]{1,0:T(8,128)(2,1)S(1)}, bf16[128,256]{1,0:T(8,128)(2,1)}, u32[]{:S(2)}, u32[]{:S(2)}) collective-permute-start(bf16[128,256]{1,0:T(8,128)(2,1)S(1)} %bitcast.471), channel_id=1, source_target_pairs={{0,2},{1,3},{2,0},{3,1},{4,6},{5,7},{6,4},{7,5},{8,10},{9,11},{10,... | collective-permute-start | bytes 196616 | tf_op jit(solution)/shard_map/ppermute | solution.py:131
  122.2 1.3 copy-start.25
  135.5 5.6 %collective-permute-start.9 = (bf16[128,256]{1,0:T(8,128)(2,1)S(1)}, bf16[128,256]{1,0:T(8,128)(2,1)S(1)}, u32[]{:S(2)}, u32[]{:S(2)}) collective-permute-start(bf16[128,256]{1,0:T(8,128)(2,1)S(1)} %bitcast.472), channel_id=1, source_target_pairs={{0,1},{1,2},{2,3},{3,0},{4,5},{5,6},{6,7},{7,4},{8,9},{9,10},{10,1... | collective-permute-start | bytes 196616 | tf_op jit(solution)/shard_map/ppermute | solution.py:131
  138.3 2.8 %copy-start.16 = (bf16[256,256]{1,0:T(8,128)(2,1)S(1)}, bf16[256,256]{1,0:T(8,128)(2,1)}, u32[]{:S(2)}) copy-start(bf16[256,256]{1,0:T(8,128)(2,1)} %get-tuple-element.536) | copy-start | bytes 393220
  (23 other events, 17.9 us)

commit v3 on v2

--- a/solution.py
+++ b/solution.py
@@ -78,12 +78,27 @@
     return jnp.einsum("hji,hjk->hik", left, right, precision=highest)
 
 
+def pick_head(array, index):
+    return lax.dynamic_slice_in_dim(array, index, 1, 0)
+
+
 def scan_both(transition, offset, local_adjoint, count, axis):
     place = lax.axis_index(axis)
     width = transition.shape[-1]
-    total_map, total_shift, total_adjoint = transition, offset, local_adjoint
+    core = place % 2
+    own = jnp.concatenate([transition, offset, local_adjoint], -1)
+    got = lax.ppermute(pick_head(own, 1 - core), axis, [(i, i ^ 1) for i in range(count)])
+    mine = pick_head(own, core)
+    second = core == 1
+    low = jnp.where(second, got, mine)
+    high = jnp.where(second, mine, got)
+    core_low, core_high = low, high
+    joined = mm(high[..., :width], jnp.concatenate([low[..., :width], low[..., width : 2 * width]], -1))
+    total_map = joined[..., :width]
+    total_shift = joined[..., width:] + high[..., width : 2 * width]
+    total_adjoint = mm_t(low[..., :width], high[..., 2 * width :]) + low[..., 2 * width :]
     entry_map = entry_state = exit_map = exit_adjoint = None
-    step = 1
+    step = 2
     while step < count:
         last = 2 * step >= count
         pairs = [(i, i ^ step) for i in range(count)]
@@ -93,9 +108,8 @@
         else:
             sent = jnp.concatenate([total_map, total_shift, total_adjoint], -1)
         got = lax.ppermute(sent, axis, pairs)
-        mine = sent
-        low = jnp.where(upper, got, mine)
-        high = jnp.where(upper, mine, got)
+        low = jnp.where(upper, got, sent)
+        high = jnp.where(upper, sent, got)
         if last:
             low_shift = low[..., :width]
             high_adjoint = high[..., width:]
@@ -123,7 +137,20 @@
             total_shift = joined[..., width:] + high[..., width : 2 * width]
             total_adjoint = mm_t(low_map, high_adjoint) + low[..., 2 * width :]
         step *= 2
-    return entry_state, exit_adjoint
+    if entry_state is None:
+        entry_state = jnp.zeros_like(total_shift)
+        exit_adjoint = jnp.zeros_like(total_adjoint)
+    entry_second = mm(core_low[..., :width], entry_state) + core_low[..., width : 2 * width]
+    exit_first = mm_t(core_high[..., :width], exit_adjoint) + core_high[..., 2 * width :]
+    mine = jnp.concatenate(
+        [jnp.where(second, entry_second, entry_state), jnp.where(second, exit_adjoint, exit_first)], -1
+    )
+    other = jnp.concatenate(
+        [jnp.where(second, entry_state, entry_second), jnp.where(second, exit_first, exit_adjoint)], -1
+    )
+    back = lax.ppermute(other, axis, [(i, i ^ 1) for i in range(count)])
+    both = jnp.where(second, jnp.concatenate([back, mine], 0), jnp.concatenate([mine, back], 0))
+    return both[..., :width], both[..., width:]
 
 
 def head_ring(part, count, axis):

time: 144 us -> 119 us (0.83)
  waiting for transfers between devices: 55.2 us -> 33.5 us
  matrix products: 37.1 us -> 34.4 us
  starting transfers between devices: 26.3 us -> 28 us
  local copies, waits for them, and re-layouts: 16.6 us -> 15.1 us
    ppermute x6 -> x5, waiting for transfers between devices: 53.1 us -> 29.7 us  [scan_both(): got = lax.ppermute(sent, axis, pairs)]
    unnamed x69 -> x53, local copies, waits for them, and re-layouts: 14.1 us -> 10.3 us
    while x0 -> x8, local copies, waits for them, and re-layouts: none -> 2.32 us
    dot_general x19 -> x17, matrix products: 5.5 us -> 3.77 us  [mm(): return jnp.einsum('hij,hjk->hik', left, right, precision=highest)]
    ppermute x6 -> x5, starting transfers between devices: 14.6 us -> 14.7 us  [scan_both(): got = lax.ppermute(sent, axis, pairs)]
  transfers between devices with their start and end apart: 15 -> 16, of which waited for: 7 -> 7; matrix products, arithmetic and copies ran while one was open for 29% -> 27% of each run, Pallas kernels for 0% -> 0%
where the time goes in v3:
time: 119 us; the launch traced here: 118 us
  matrix products  34.4 us (29%)
  waiting for transfers between devices  33.5 us (28%)
  starting transfers between devices  28 us (24%)
  local copies, waits for them, and re-layouts  15.1 us (13%)
  other arithmetic  4.6 us (4%)
  between operations  1.71 us (1%)
    ppermute x5, waiting for transfers between devices, scan_both(): got = lax.ppermute(sent, axis, pairs)  29.7 us
    ppermute x5, starting transfers between devices, scan_both(): got = lax.ppermute(sent, axis, pairs)  14.7 us
    unnamed x53, local copies, waits for them, and re-layouts  10.3 us
    ppermute x6, starting transfers between devices, head_ring(): lax.ppermute(part, axis, [(i, (i + k) % count) for i in range(count)])  9.08 us
    dot_general x15, matrix products, block_factors(): jnp.einsum('hnij,hnjk->hnik', power_term, power_term, precision=highest)  4.97 us
    dot_general x15, matrix products, block_factors(): jnp.einsum('hnij,hnjk->hnik', result, power_term, precision=highest)  4.92 us
    ppermute x3, starting transfers between devices, body(): lax.ppermute(block, 'head', [(i, (i + k) % head_devices) for i in range(h...  3.96 us
    dot_general x17, matrix products, mm(): return jnp.einsum('hij,hjk->hik', left, right, precision=highest)  3.77 us
  transfers between devices with their start and end apart: 16, of which 7 were waited for; matrix products, arithmetic and copies ran while one was open for 27% of the time, Pallas kernels for 0%

profile of v3, /device:TPU:8, one launch (start us, length us, event | category | flops | bytes accessed | tf_op | source)
XLA Modules:
  0.0 117.6 jit_solution(2252190822278349835)
XLA Ops:
  0.6 2.8 %collective-permute-start.2 = (bf16[128,256]{1,0:T(8,128)(2,1)}, bf16[128,256]{1,0:T(8,128)(2,1)}, u32[]{:S(2)}, u32[]{:S(2)}) collective-permute-start(bf16[128,256]{1,0:T(8,128)(2,1)} %param.17), channel_id=1, source_target_pairs={{0,3},{1,0},{2,1},{3,2},{4,7},{5,4},{6,5},{7,6},{8,11},{9,8},{10,9... | collective-permute-start | bytes 196616 | tf_op jit(solution)/shard_map/ppermute | solution.py:158
  4.3 0.9 collective-permute-start
  15.5 5.0 %while.52 = (s32[]{:T(128)}, f32[2,128,256]{2,1,0:T(8,128)S(1)}, f32[2,2,64,256]{3,2,0,1:T(8,128)}, f32[2,2,64,128]{3,2,1,0:T(8,128)S(1)}, f32[2,2,64,256]{3,2,0...) while((s32[]{:T(128)}, f32[2,128,256]{2,1,0:T(8,128)S(1)}, ...), condition=%wide.region_3.4_spmd, body=%wide.region_2.3_spmd.sunk | while | flops 176291840 | bytes 4327589 | solution.py:70
  20.4 0.9 constant_dynamic-slice_fusion.7
  21.3 1.2 %fusion.105 = f32[128,256]{1,0:T(8,128)S(1)} fusion(bf16[256,256]{1,0:T(8,128)(2,1)S(1)} %get-tuple-element.529, bf16[256,256]{1,0:T(8,128)(2,1)S(1)} %get-tuple-element.530, bf16[256,256]{1,0:T(8,128)(2,1)S(1)} %get-tuple-element.531, bf16[256,256]{1,0:T(8,128)(2,1)S(1)} %get-tuple-element.526, bf16[128,256]{1,0:T(8,128)(2,1)} %collective-permute-done.2, ...), kind=kOutput, calls=%fused_computation.173 | convolution fusion | flops 70254592 | bytes 917504 | tf_op jit(solution)/shard_map/dot_general | solution.py:227
  24.1 1.4 %collective-permute-done.3 = f32[1,128,384]{2,1,0:T(8,128)S(1)} collective-permute-done((f32[1,128,384]{2,1,0:T(8,128)S(1)}, f32[1,128,384]{2,1,0:T(8,128)S(1)}, u32[]{:S(2)}, u32[]{:S(2)}) %collective-permute-start.3) | collective-permute-done | bytes 196640 | tf_op jit(solution)/shard_map/ppermute | solution.py:90
  26.1 2.0 %collective-permute-start.4 = (f32[1,128,384]{2,1,0:T(8,128)S(1)}, f32[1,128,384]{2,1,0:T(8,128)}, u32[]{:S(2)}, u32[]{:S(2)}) collective-permute-start(f32[1,128,384]{2,1,0:T(8,128)S(1)} %pad_maximum_fusion), channel_id=1, source_target_pairs={{0,8},{4,12},{8,0},{12,4},{16,24},{20,28},{24,16},{28,20},{32,40},... | collective-permute-start | bytes 589832 | tf_op jit(solution)/shard_map/ppermute | solution.py:110
  28.1 5.3 %collective-permute-done.4 = f32[1,128,384]{2,1,0:T(8,128)} collective-permute-done((f32[1,128,384]{2,1,0:T(8,128)S(1)}, f32[1,128,384]{2,1,0:T(8,128)}, u32[]{:S(2)}, u32[]{:S(2)}) %collective-permute-start.4) | collective-permute-done | bytes 196640 | tf_op jit(solution)/shard_map/ppermute | solution.py:110
  33.4 1.0 broadcast_select_fusion.8
  36.3 3.3 %collective-permute-start.5 = (f32[1,128,384]{2,1,0:T(8,128)}, f32[1,128,384]{2,1,0:T(8,128)}, u32[]{:S(2)}, u32[]{:S(2)}) collective-permute-start(f32[1,128,384]{2,1,0:T(8,128)} %pad_maximum_fusion.1), channel_id=1, source_target_pairs={{0,16},{4,20},{8,24},{12,28},{16,0},{20,4},{24,8},{28,12},{32,48},... | collective-permute-start | bytes 589832 | tf_op jit(solution)/shard_map/ppermute | solution.py:110
  39.7 9.0 %collective-permute-done.5 = f32[1,128,384]{2,1,0:T(8,128)} collective-permute-done((f32[1,128,384]{2,1,0:T(8,128)}, f32[1,128,384]{2,1,0:T(8,128)}, u32[]{:S(2)}, u32[]{:S(2)}) %collective-permute-start.5) | collective-permute-done | bytes 196640 | tf_op jit(solution)/shard_map/ppermute | solution.py:110
  48.6 1.0 broadcast_select_fusion.5
  50.9 6.5 %collective-permute-start.6 = (f32[1,128,384]{2,1,0:T(8,128)S(1)}, f32[1,128,384]{2,1,0:T(8,128)S(1)}, u32[]{:S(2)}, u32[]{:S(2)}) collective-permute-start(f32[1,128,384]{2,1,0:T(8,128)S(1)} %pad_maximum_fusion.2), channel_id=1, source_target_pairs={{0,32},{4,36},{8,40},{12,44},{16,48},{20,52},{24,56},{28,60},{32,0... | collective-permute-start | bytes 589832 | tf_op jit(solution)/shard_map/ppermute | solution.py:110
  57.6 7.4 %collective-permute-done.6 = f32[1,128,384]{2,1,0:T(8,128)S(1)} collective-permute-done((f32[1,128,384]{2,1,0:T(8,128)S(1)}, f32[1,128,384]{2,1,0:T(8,128)S(1)}, u32[]{:S(2)}, u32[]{:S(2)}) %collective-permute-start.6) | collective-permute-done | bytes 196640 | tf_op jit(solution)/shard_map/ppermute | solution.py:110
  67.0 4.9 %collective-permute-done.7 = f32[1,128,384]{2,1,0:T(8,128)S(1)} collective-permute-done((f32[1,128,384]{2,1,0:T(8,128)S(1)}, f32[1,128,384]{2,1,0:T(8,128)S(1)}, u32[]{:S(2)}, u32[]{:S(2)}) %collective-permute-start.7) | collective-permute-done | bytes 196640 | tf_op jit(solution)/shard_map/ppermute | solution.py:110
  72.5 2.4 %collective-permute-start.8 = (f32[1,128,256]{2,1,0:T(8,128)S(1)}, f32[1,128,256]{2,1,0:T(8,128)S(1)}, u32[]{:S(2)}, u32[]{:S(2)}) collective-permute-start(f32[1,128,256]{2,1,0:T(8,128)S(1)} %pad_maximum_fusion.4), channel_id=1, source_target_pairs={{0,128},{4,132},{8,136},{12,140},{16,144},{20,148},{24,152},{28,15... | collective-permute-start | bytes 393224 | tf_op jit(solution)/shard_map/ppermute | solution.py:110
  75.9 3.2 %collective-permute-done.8 = f32[1,128,256]{2,1,0:T(8,128)S(1)} collective-permute-done((f32[1,128,256]{2,1,0:T(8,128)S(1)}, f32[1,128,256]{2,1,0:T(8,128)S(1)}, u32[]{:S(2)}, u32[]{:S(2)}) %collective-permute-start.8) | collective-permute-done | bytes 131104 | tf_op jit(solution)/shard_map/ppermute | solution.py:110
  80.2 2.5 %collective-permute-start.15 = (bf16[256,256]{1,0:T(8,128)(2,1)}, bf16[256,256]{1,0:T(8,128)(2,1)S(1)}, u32[]{:S(2)}, u32[]{:S(2)}) collective-permute-start(bf16[256,256]{1,0:T(8,128)(2,1)} %get-tuple-element.532), channel_id=1, source_target_pairs={{0,3},{1,0},{2,1},{3,2},{4,7},{5,4},{6,5},{7,6},{8,11},{9,8},{10,9... | collective-permute-start | bytes 393224 | tf_op jit(solution)/shard_map/ppermute | solution.py:177
  82.6 1.5 %collective-permute-start.14 = (bf16[256,256]{1,0:T(8,128)(2,1)}, bf16[256,256]{1,0:T(8,128)(2,1)}, u32[]{:S(2)}, u32[]{:S(2)}) collective-permute-start(bf16[256,256]{1,0:T(8,128)(2,1)} %get-tuple-element.533), channel_id=1, source_target_pairs={{0,2},{1,3},{2,0},{3,1},{4,6},{5,7},{6,4},{7,5},{8,10},{9,11},{10,... | collective-permute-start | bytes 393224 | tf_op jit(solution)/shard_map/ppermute | solution.py:177
  84.2 2.3 %while.53 = (s32[]{:T(128)}, f32[2,128,128]{2,1,0:T(8,128)S(1)}, bf16[2,2,64,128]{3,2,1,0:T(8,128)(2,1)S(1)}, f32[2,2,128,128]{3,2,1,0:T(8,128)S(1)}, f32[2,2,64...) while((s32[]{:T(128)}, f32[2,128,128]{2,1,0:T(8,128)S(1)}, ...), condition=%wide.region_5.6_spmd, body=%wide.region_4.5_spmd.sunk | while | flops 88145920 | bytes 1575041 | solution.py:70
  86.6 3.3 %collective-permute-start.12 = (bf16[128,256]{1,0:T(8,128)(2,1)S(1)}, bf16[128,256]{1,0:T(8,128)(2,1)S(1)}, u32[]{:S(2)}, u32[]{:S(2)}) collective-permute-start(bf16[128,256]{1,0:T(8,128)(2,1)S(1)} %bitcast.711), channel_id=1, source_target_pairs={{0,3},{1,0},{2,1},{3,2},{4,7},{5,4},{6,5},{7,6},{8,11},{9,8},{10,9... | collective-permute-start | bytes 196616 | tf_op jit(solution)/shard_map/ppermute | solution.py:158
  90.9 5.4 %while.54 = (s32[]{:T(128)}, f32[2,128,128]{2,1,0:T(8,128)S(1)}, f32[2,2,64,128]{3,2,0,1:T(8,128)S(1)}, f32[2,2,64,128]{3,2,0,1:T(8,128)S(1)}, f32[2,2,64,128]{3...) while((s32[]{:T(128)}, f32[2,128,128]{2,1,0:T(8,128)S(1)}, ...), condition=%wide.region_7.8_spmd, body=%wide.region_6.7_spmd.sunk | while | flops 176275456 | bytes 2367145 | solution.py:70
  113.4 2.3 %collective-permute-done.10 = bf16[128,256]{1,0:T(8,128)(2,1)S(1)} collective-permute-done((bf16[128,256]{1,0:T(8,128)(2,1)S(1)}, bf16[128,256]{1,0:T(8,128)(2,1)S(1)}, u32[]{:S(2)}, u32[]{:S(2)}) %collective-permute-start.10) | collective-permute-done | bytes 65568 | tf_op jit(solution)/shard_map/ppermute | solution.py:158
  115.8 1.9 %convolution_convert_fusion = bf16[128,256]{1,0:T(8,128)(2,1)} fusion(bf16[256,256]{1,0:T(8,128)(2,1)S(1)} %collective-permute-done.15, bf16[256,256]{1,0:T(8,128)(2,1)} %collective-permute-done.14, bf16[256,256]{1,0:T(8,128)(2,1)} %collective-permute-done.13, bf16[256,256]{1,0:T(8,128)(2,1)S(1)} %copy-done.10, ...), kind=kOutput, calls=%fused_computation.118 | convolution fusion | flops 70287360 | bytes 851968 | tf_op jit(solution)/shard_map/dot_general | solution.py:245
  (241 shorter events, 51.0 us)
Async XLA Ops:
  0.6 20.7 %collective-permute-start.2 = (bf16[128,256]{1,0:T(8,128)(2,1)}, bf16[128,256]{1,0:T(8,128)(2,1)}, u32[]{:S(2)}, u32[]{:S(2)}) collective-permute-start(bf16[128,256]{1,0:T(8,128)(2,1)} %param.17), channel_id=1, source_target_pairs={{0,3},{1,0},{2,1},{3,2},{4,7},{5,4},{6,5},{7,6},{8,11},{9,8},{10,9... | collective-permute-start | bytes 196616 | tf_op jit(solution)/shard_map/ppermute | solution.py:158
  3.5 17.9 %collective-permute-start.1 = (bf16[128,256]{1,0:T(8,128)(2,1)}, bf16[128,256]{1,0:T(8,128)(2,1)}, u32[]{:S(2)}, u32[]{:S(2)}) collective-permute-start(bf16[128,256]{1,0:T(8,128)(2,1)} %param.17), channel_id=1, source_target_pairs={{0,2},{1,3},{2,0},{3,1},{4,6},{5,7},{6,4},{7,5},{8,10},{9,11},{10,... | collective-permute-start | bytes 196616 | tf_op jit(solution)/shard_map/ppermute | solution.py:158
  4.3 17.1 %collective-permute-start = (bf16[128,256]{1,0:T(8,128)(2,1)}, bf16[128,256]{1,0:T(8,128)(2,1)}, u32[]{:S(2)}, u32[]{:S(2)}) collective-permute-start(bf16[128,256]{1,0:T(8,128)(2,1)} %param.17), channel_id=1, source_target_pairs={{0,1},{1,2},{2,3},{3,0},{4,5},{5,6},{6,7},{7,4},{8,9},{9,10},{10,1... | collective-permute-start | bytes 196616 | tf_op jit(solution)/shard_map/ppermute | solution.py:158
  5.2 5.3 %copy-start.7 = (f32[64,64]{1,0:T(8,128)}, f32[64,64]{1,0:T(8,128)S(1)}, u32[]{:S(2)}) copy-start(f32[64,64]{1,0:T(8,128)S(1)} %fusion.226) | copy-start | bytes 49156
  8.2 6.8 %copy-start.19 = (f32[2,2,64]{2,1,0:T(2,128)}, f32[2,2,64]{2,1,0:T(2,128)S(1)}, u32[]{:S(2)}) copy-start(f32[2,2,64]{2,1,0:T(2,128)S(1)} %get-tuple-element.561) | copy-start | bytes 3076
  15.4 5.0 %copy-start = (bf16[256,1024]{1,0:T(8,128)(2,1)S(1)}, bf16[256,1024]{1,0:T(8,128)(2,1)}, u32[]{:S(2)}) copy-start(bf16[256,1024]{1,0:T(8,128)(2,1)} %param.16) | copy-start | bytes 1572868
  16.0 1.0 copy-start.13
  18.5 1.0 copy-start.13
  22.6 1.0 copy-start.15
  24.0 1.5 %collective-permute-start.3 = (f32[1,128,384]{2,1,0:T(8,128)S(1)}, f32[1,128,384]{2,1,0:T(8,128)S(1)}, u32[]{:S(2)}, u32[]{:S(2)}) collective-permute-start(f32[1,128,384]{2,1,0:T(8,128)S(1)} %fusion.134), channel_id=1, source_target_pairs={{0,4},{4,0},{8,12},{12,8},{16,20},{20,16},{24,28},{28,24},{32,36},... | collective-permute-start | bytes 589832 | tf_op jit(solution)/shard_map/ppermute | solution.py:90
  26.1 7.3 %collective-permute-start.4 = (f32[1,128,384]{2,1,0:T(8,128)S(1)}, f32[1,128,384]{2,1,0:T(8,128)}, u32[]{:S(2)}, u32[]{:S(2)}) collective-permute-start(f32[1,128,384]{2,1,0:T(8,128)S(1)} %pad_maximum_fusion), channel_id=1, source_target_pairs={{0,8},{4,12},{8,0},{12,4},{16,24},{20,28},{24,16},{28,20},{32,40},... | collective-permute-start | bytes 589832 | tf_op jit(solution)/shard_map/ppermute | solution.py:110
  35.6 4.0 %copy-start.9 = (f32[1,128,128]{2,1,0:T(8,128)S(1)}, f32[1,128,128]{2,1,0:T(8,128)}, u32[]{:S(2)}) copy-start(f32[1,128,128]{2,1,0:T(8,128)} %get-tuple-element.544) | copy-start | bytes 196612
  36.3 12.3 %collective-permute-start.5 = (f32[1,128,384]{2,1,0:T(8,128)}, f32[1,128,384]{2,1,0:T(8,128)}, u32[]{:S(2)}, u32[]{:S(2)}) collective-permute-start(f32[1,128,384]{2,1,0:T(8,128)} %pad_maximum_fusion.1), channel_id=1, source_target_pairs={{0,16},{4,20},{8,24},{12,28},{16,0},{20,4},{24,8},{28,12},{32,48},... | collective-permute-start | bytes 589832 | tf_op jit(solution)/shard_map/ppermute | solution.py:110
  50.9 14.1 %collective-permute-start.6 = (f32[1,128,384]{2,1,0:T(8,128)S(1)}, f32[1,128,384]{2,1,0:T(8,128)S(1)}, u32[]{:S(2)}, u32[]{:S(2)}) collective-permute-start(f32[1,128,384]{2,1,0:T(8,128)S(1)} %pad_maximum_fusion.2), channel_id=1, source_target_pairs={{0,32},{4,36},{8,40},{12,44},{16,48},{20,52},{24,56},{28,60},{32,0... | collective-permute-start | bytes 589832 | tf_op jit(solution)/shard_map/ppermute | solution.py:110
  66.1 5.8 %collective-permute-start.7 = (f32[1,128,384]{2,1,0:T(8,128)S(1)}, f32[1,128,384]{2,1,0:T(8,128)S(1)}, u32[]{:S(2)}, u32[]{:S(2)}) collective-permute-start(f32[1,128,384]{2,1,0:T(8,128)S(1)} %pad_maximum_fusion.3), channel_id=1, source_target_pairs={{0,64},{4,68},{8,72},{12,76},{16,80},{20,84},{24,88},{28,92},{32,9... | collective-permute-start | bytes 589832 | tf_op jit(solution)/shard_map/ppermute | solution.py:110
  72.5 6.6 %collective-permute-start.8 = (f32[1,128,256]{2,1,0:T(8,128)S(1)}, f32[1,128,256]{2,1,0:T(8,128)S(1)}, u32[]{:S(2)}, u32[]{:S(2)}) collective-permute-start(f32[1,128,256]{2,1,0:T(8,128)S(1)} %pad_maximum_fusion.4), channel_id=1, source_target_pairs={{0,128},{4,132},{8,136},{12,140},{16,144},{20,148},{24,152},{28,15... | collective-permute-start | bytes 393224 | tf_op jit(solution)/shard_map/ppermute | solution.py:110
  80.1 4.1 %collective-permute-start.9 = (f32[1,128,256]{2,1,0:T(8,128)S(1)}, f32[1,128,256]{2,1,0:T(8,128)S(1)}, u32[]{:S(2)}, u32[]{:S(2)}) collective-permute-start(f32[1,128,256]{2,1,0:T(8,128)S(1)} %pad_maximum_fusion.5), channel_id=1, source_target_pairs={{0,4},{4,0},{8,12},{12,8},{16,20},{20,16},{24,28},{28,24},{32,36},... | collective-permute-start | bytes 393224 | tf_op jit(solution)/shard_map/ppermute | solution.py:151
  80.2 30.0 %collective-permute-start.15 = (bf16[256,256]{1,0:T(8,128)(2,1)}, bf16[256,256]{1,0:T(8,128)(2,1)S(1)}, u32[]{:S(2)}, u32[]{:S(2)}) collective-permute-start(bf16[256,256]{1,0:T(8,128)(2,1)} %get-tuple-element.532), channel_id=1, source_target_pairs={{0,3},{1,0},{2,1},{3,2},{4,7},{5,4},{6,5},{7,6},{8,11},{9,8},{10,9... | collective-permute-start | bytes 393224 | tf_op jit(solution)/shard_map/ppermute | solution.py:177
  82.6 30.8 %collective-permute-start.14 = (bf16[256,256]{1,0:T(8,128)(2,1)}, bf16[256,256]{1,0:T(8,128)(2,1)}, u32[]{:S(2)}, u32[]{:S(2)}) collective-permute-start(bf16[256,256]{1,0:T(8,128)(2,1)} %get-tuple-element.533), channel_id=1, source_target_pairs={{0,2},{1,3},{2,0},{3,1},{4,6},{5,7},{6,4},{7,5},{8,10},{9,11},{10,... | collective-permute-start | bytes 393224 | tf_op jit(solution)/shard_map/ppermute | solution.py:177
  84.1 29.3 %collective-permute-start.13 = (bf16[256,256]{1,0:T(8,128)(2,1)}, bf16[256,256]{1,0:T(8,128)(2,1)}, u32[]{:S(2)}, u32[]{:S(2)}) collective-permute-start(bf16[256,256]{1,0:T(8,128)(2,1)} %get-tuple-element.527), channel_id=1, source_target_pairs={{0,1},{1,2},{2,3},{3,0},{4,5},{5,6},{6,7},{7,4},{8,9},{9,10},{10,1... | collective-permute-start | bytes 393224 | tf_op jit(solution)/shard_map/ppermute | solution.py:177
  86.6 26.8 %collective-permute-start.12 = (bf16[128,256]{1,0:T(8,128)(2,1)S(1)}, bf16[128,256]{1,0:T(8,128)(2,1)S(1)}, u32[]{:S(2)}, u32[]{:S(2)}) collective-permute-start(bf16[128,256]{1,0:T(8,128)(2,1)S(1)} %bitcast.711), channel_id=1, source_target_pairs={{0,3},{1,0},{2,1},{3,2},{4,7},{5,4},{6,5},{7,6},{8,11},{9,8},{10,9... | collective-permute-start | bytes 196616 | tf_op jit(solution)/shard_map/ppermute | solution.py:158
  89.9 23.5 %collective-permute-start.11 = (bf16[128,256]{1,0:T(8,128)(2,1)S(1)}, bf16[128,256]{1,0:T(8,128)(2,1)}, u32[]{:S(2)}, u32[]{:S(2)}) collective-permute-start(bf16[128,256]{1,0:T(8,128)(2,1)S(1)} %bitcast.712), channel_id=1, source_target_pairs={{0,2},{1,3},{2,0},{3,1},{4,6},{5,7},{6,4},{7,5},{8,10},{9,11},{10,... | collective-permute-start | bytes 196616 | tf_op jit(solution)/shard_map/ppermute | solution.py:158
  110.2 5.6 %collective-permute-start.10 = (bf16[128,256]{1,0:T(8,128)(2,1)S(1)}, bf16[128,256]{1,0:T(8,128)(2,1)S(1)}, u32[]{:S(2)}, u32[]{:S(2)}) collective-permute-start(bf16[128,256]{1,0:T(8,128)(2,1)S(1)} %bitcast.713), channel_id=1, source_target_pairs={{0,1},{1,2},{2,3},{3,0},{4,5},{5,6},{6,7},{7,4},{8,9},{9,10},{10,1... | collective-permute-start | bytes 196616 | tf_op jit(solution)/shard_map/ppermute | solution.py:158
  112.0 3.7 %copy-start.10 = (bf16[256,256]{1,0:T(8,128)(2,1)S(1)}, bf16[256,256]{1,0:T(8,128)(2,1)}, u32[]{:S(2)}) copy-start(bf16[256,256]{1,0:T(8,128)(2,1)} %get-tuple-element.528) | copy-start | bytes 393220
  (20 other events, 14.6 us)

commit v4 on v3

--- a/solution.py
+++ b/solution.py
@@ -31,22 +31,40 @@
     return block_outputs.transpose(0, 2, 1, 3).reshape(block_count * size, head_count * head_width)
 
 
-def block_factors(query_blocks, key_blocks, value_blocks, rate_parts):
-    unit_query = unit_rows(query_blocks)
-    unit_key = unit_rows(key_blocks)
-    size = unit_key.shape[-2]
-    identity_block = jnp.eye(size, dtype=jnp.float32)
-    key_gram = jnp.einsum(
-        "hncd,hnsd->hncs", unit_key * rate_parts[..., None], unit_key, precision=highest
-    )
-    strict_lower = jnp.tril(key_gram, -1)
-    result = identity_block - strict_lower
+@jax.custom_vjp
+def unit_lower_inverse(strict_lower):
+    return unit_lower_inverse_fwd(strict_lower)[0]
+
+
+def unit_lower_inverse_fwd(strict_lower):
+    size = strict_lower.shape[-1]
+    result = jnp.eye(size, dtype=jnp.float32) - strict_lower
     power_term = strict_lower
     span_done = 2
     while span_done < size:
         power_term = jnp.einsum("hnij,hnjk->hnik", power_term, power_term, precision=highest)
         result = result + jnp.einsum("hnij,hnjk->hnik", result, power_term, precision=highest)
         span_done = span_done * 2
+    return result, result
+
+
+def unit_lower_inverse_bwd(result, grad):
+    inner = jnp.einsum("hnji,hnjk->hnik", result, grad, precision=highest)
+    outer = jnp.einsum("hnij,hnkj->hnik", inner, result, precision=highest)
+    return (jnp.tril(-outer, -1),)
+
+
+unit_lower_inverse.defvjp(unit_lower_inverse_fwd, unit_lower_inverse_bwd)
+
+
+def block_factors(query_blocks, key_blocks, value_blocks, rate_parts):
+    unit_query = unit_rows(query_blocks)
+    unit_key = unit_rows(key_blocks)
+    key_gram = jnp.einsum(
+        "hncd,hnsd->hncs", unit_key * rate_parts[..., None], unit_key, precision=highest
+    )
+    strict_lower = jnp.tril(key_gram, -1)
+    result = unit_lower_inverse(strict_lower)
     scaled = result * rate_parts[..., None, :]
     key_mix = jnp.einsum("hncs,hnsd->hncd", scaled, unit_key, precision=highest)
     value_mix = jnp.einsum("hncs,hnsd->hncd", scaled, value_blocks, precision=highest)
@@ -168,19 +186,22 @@
         width = queries.shape[1]
         here = lax.axis_index("head")
 
+        rows = out_grad.shape[0]
         weight_cols = [lax.dynamic_slice_in_dim(out_weight, here * width, width, 1)]
+        grad_parts = [out_grad]
         for k in range(1, head_devices):
             block = lax.dynamic_slice_in_dim(
                 out_weight, ((here + k) % head_devices) * width, width, 1
             )
-            weight_cols.append(
-                lax.ppermute(
-                    block, "head", [(i, (i + k) % head_devices) for i in range(head_devices)]
-                )
+            moved = lax.ppermute(
+                jnp.concatenate([out_grad, block], 0),
+                "head",
+                [(i, (i + k) % head_devices) for i in range(head_devices)],
             )
+            grad_parts.append(moved[:rows])
+            weight_cols.append(moved[rows:])
         weight_mine = jnp.concatenate(weight_cols, 0)
 
-        grad_parts = head_ring(out_grad, head_devices, "head")
         weight_rows = jnp.concatenate(
             [
                 lax.dynamic_slice_in_dim(

time: 119 us -> 98.3 us (0.83)
  matrix products: 34.4 us -> 25.8 us
  starting transfers between devices: 28 us -> 23.6 us
  other arithmetic: 4.6 us -> 1.52 us
  local copies, waits for them, and re-layouts: 15.1 us -> 12.2 us
  waiting for transfers between devices: 33.5 us -> 32 us
    dot_general x30 -> x12, matrix products: 9.89 us -> 3.29 us  [the longest x5 1.28 us: unit_lower_inverse_fwd(): jnp.einsum('hnij,hnjk->hnik', result, power_term, precision=highest)]
    ppermute x6 -> x3, starting transfers between devices: 9.08 us -> 4.03 us  [head_ring(): lax.ppermute(part, axis, [(i, (i + k) % count) for i in range(count)])]
    unnamed x53 -> x31, local copies, waits for them, and re-layouts: 10.3 us -> 6.05 us
    ppermute x6 -> x3, waiting for transfers between devices: 2.34 us -> 0.01 us  [head_ring(): lax.ppermute(part, axis, [(i, (i + k) % count) for i in range(count)])]
    dynamic_slice x1, local copies, waits for them, and re-layouts: 0.88 us -> 2.15 us  [body(): lax.dynamic_slice_in_dim(out_weight, (here - k) % head_devices * width, w...]
    ppermute x1, waiting for transfers between devices: 0.01 us -> 1.26 us  [scan_both(): back = lax.ppermute(other, axis, [(i, i ^ 1) for i in range(count)])]
  transfers between devices with their start and end apart: 16 -> 13, of which waited for: 7 -> 7; matrix products, arithmetic and copies ran while one was open for 27% -> 22% of each run, Pallas kernels for 0% -> 0%
where the time goes in v4:
time: 98.3 us; the launch traced here: 97.2 us
  waiting for transfers between devices  32 us (33%)
  matrix products  25.8 us (26%)
  starting transfers between devices  23.6 us (24%)
  local copies, waits for them, and re-layouts  12.2 us (12%)
  between operations  1.74 us (2%)
  other arithmetic  1.52 us (2%)
    ppermute x5, waiting for transfers between devices, scan_both(): got = lax.ppermute(sent, axis, pairs)  29.3 us
    ppermute x5, starting transfers between devices, scan_both(): got = lax.ppermute(sent, axis, pairs)  14.8 us
    unnamed x31, local copies, waits for them, and re-layouts  6.05 us
    ppermute x3, starting transfers between devices, body(): lax.ppermute(jnp.concatenate([out_grad, block], 0), 'head', [(i, (i + k)...  4.52 us
    ppermute x3, starting transfers between devices, head_ring(): lax.ppermute(part, axis, [(i, (i + k) % count) for i in range(count)])  4.03 us
    dot_general x17, matrix products, mm(): return jnp.einsum('hij,hjk->hik', left, right, precision=highest)  3.77 us
    dot_general x8, matrix products, advance_block(): jnp.einsum('hcd,hce->hde', unit_key, innovation, precision=highest)  2.93 us
    dot_general x8, matrix products, advance_block(): jnp.einsum('hcd,hde->hce', key_mix, state, precision=highest)  2.54 us
  transfers between devices with their start and end apart: 13, of which 7 were waited for; matrix products, arithmetic and copies ran while one was open for 22% of the time, Pallas kernels for 0%

profile of v4, /device:TPU:8, one launch (start us, length us, event | category | flops | bytes accessed | tf_op | source)
XLA Modules:
  0.0 97.2 jit_solution(10029193429609487029)
XLA Ops:
  0.8 2.2 %constant_dynamic-slice_fusion.4 = (bf16[256,256]{1,0:T(8,128)(2,1)S(1)}, bf16[256,256]{1,0:T(8,128)(2,1)}, bf16[256,256]{1,0:T(8,128)(2,1)}, bf16[256,256]{1,0:...) fusion(bf16[256,1024]{1,0:T(8,128)(2,1)} %param.16, ...), kind=kLoop, calls=%fused_computation.375 | loop fusion | bytes 2097184 | tf_op jit(solution)/shard_map/dynamic_slice | solution.py:207
  3.0 2.8 %collective-permute-start.2 = (bf16[384,256]{1,0:T(8,128)(2,1)S(1)}, bf16[384,256]{1,0:T(8,128)(2,1)S(1)}, u32[]{:S(2)}, u32[]{:S(2)}) collective-permute-start(bf16[384,256]{1,0:T(8,128)(2,1)S(1)} %get-tuple-element.559), channel_id=1, source_target_pairs={{0,3},{1,0},{2,1},{3,2},{4,7},{5,4},{6,5},{7,6},{8,11},{9,8},{10,9... | collective-permute-start | bytes 589832 | tf_op jit(solution)/shard_map/ppermute | solution.py:196
  5.8 0.8 collective-permute-start.1
  6.6 0.9 collective-permute-start
  7.7 0.8 copy-done.11
  15.0 5.0 %while.52 = (s32[]{:T(128)}, f32[2,128,256]{2,1,0:T(8,128)S(1)}, f32[2,2,64,256]{3,2,0,1:T(8,128)}, f32[2,2,64,128]{3,2,1,0:T(8,128)S(1)}, f32[2,2,64,256]{3,2,0...) while((s32[]{:T(128)}, f32[2,128,256]{2,1,0:T(8,128)S(1)}, ...), condition=%wide.region_3.4_spmd, body=%wide.region_2.3_spmd.sunk | while | flops 176291840 | bytes 4327589 | solution.py:88
  20.1 0.9 copy-done.6
  21.6 0.9 copy-done.9
  23.0 1.4 %collective-permute-done.3 = f32[1,128,384]{2,1,0:T(8,128)S(1)} collective-permute-done((f32[1,128,384]{2,1,0:T(8,128)S(1)}, f32[1,128,384]{2,1,0:T(8,128)S(1)}, u32[]{:S(2)}, u32[]{:S(2)}) %collective-permute-start.3) | collective-permute-done | bytes 196640 | tf_op jit(solution)/shard_map/ppermute | solution.py:108
  25.1 2.0 %collective-permute-start.4 = (f32[1,128,384]{2,1,0:T(8,128)S(1)}, f32[1,128,384]{2,1,0:T(8,128)S(1)}, u32[]{:S(2)}, u32[]{:S(2)}) collective-permute-start(f32[1,128,384]{2,1,0:T(8,128)S(1)} %pad_maximum_fusion.3), channel_id=1, source_target_pairs={{0,8},{4,12},{8,0},{12,4},{16,24},{20,28},{24,16},{28,20},{32,40},... | collective-permute-start | bytes 589832 | tf_op jit(solution)/shard_map/ppermute | solution.py:128
  27.1 5.2 %collective-permute-done.4 = f32[1,128,384]{2,1,0:T(8,128)S(1)} collective-permute-done((f32[1,128,384]{2,1,0:T(8,128)S(1)}, f32[1,128,384]{2,1,0:T(8,128)S(1)}, u32[]{:S(2)}, u32[]{:S(2)}) %collective-permute-start.4) | collective-permute-done | bytes 196640 | tf_op jit(solution)/shard_map/ppermute | solution.py:128
  32.9 3.4 %collective-permute-start.5 = (f32[1,128,384]{2,1,0:T(8,128)S(1)}, f32[1,128,384]{2,1,0:T(8,128)S(1)}, u32[]{:S(2)}, u32[]{:S(2)}) collective-permute-start(f32[1,128,384]{2,1,0:T(8,128)S(1)} %pad_maximum_fusion.4), channel_id=1, source_target_pairs={{0,16},{4,20},{8,24},{12,28},{16,0},{20,4},{24,8},{28,12},{32,48},... | collective-permute-start | bytes 589832 | tf_op jit(solution)/shard_map/ppermute | solution.py:128
  36.4 8.6 %collective-permute-done.5 = f32[1,128,384]{2,1,0:T(8,128)S(1)} collective-permute-done((f32[1,128,384]{2,1,0:T(8,128)S(1)}, f32[1,128,384]{2,1,0:T(8,128)S(1)}, u32[]{:S(2)}, u32[]{:S(2)}) %collective-permute-start.5) | collective-permute-done | bytes 196640 | tf_op jit(solution)/shard_map/ppermute | solution.py:128
  46.4 6.5 %collective-permute-start.6 = (f32[1,128,384]{2,1,0:T(8,128)S(1)}, f32[1,128,384]{2,1,0:T(8,128)S(1)}, u32[]{:S(2)}, u32[]{:S(2)}) collective-permute-start(f32[1,128,384]{2,1,0:T(8,128)S(1)} %pad_maximum_fusion.5), channel_id=1, source_target_pairs={{0,32},{4,36},{8,40},{12,44},{16,48},{20,52},{24,56},{28,60},{32,0... | collective-permute-start | bytes 589832 | tf_op jit(solution)/shard_map/ppermute | solution.py:128
  53.1 7.4 %collective-permute-done.6 = f32[1,128,384]{2,1,0:T(8,128)S(1)} collective-permute-done((f32[1,128,384]{2,1,0:T(8,128)S(1)}, f32[1,128,384]{2,1,0:T(8,128)S(1)}, u32[]{:S(2)}, u32[]{:S(2)}) %collective-permute-start.6) | collective-permute-done | bytes 196640 | tf_op jit(solution)/shard_map/ppermute | solution.py:128
  62.6 4.8 %collective-permute-done.7 = f32[1,128,384]{2,1,0:T(8,128)S(1)} collective-permute-done((f32[1,128,384]{2,1,0:T(8,128)S(1)}, f32[1,128,384]{2,1,0:T(8,128)S(1)}, u32[]{:S(2)}, u32[]{:S(2)}) %collective-permute-start.7) | collective-permute-done | bytes 196640 | tf_op jit(solution)/shard_map/ppermute | solution.py:128
  68.0 2.4 %collective-permute-start.8 = (f32[1,128,256]{2,1,0:T(8,128)S(1)}, f32[1,128,256]{2,1,0:T(8,128)S(1)}, u32[]{:S(2)}, u32[]{:S(2)}) collective-permute-start(f32[1,128,256]{2,1,0:T(8,128)S(1)} %pad_maximum_fusion.7), channel_id=1, source_target_pairs={{0,128},{4,132},{8,136},{12,140},{16,144},{20,148},{24,152},{28,15... | collective-permute-start | bytes 393224 | tf_op jit(solution)/shard_map/ppermute | solution.py:128
  71.3 3.2 %collective-permute-done.8 = f32[1,128,256]{2,1,0:T(8,128)S(1)} collective-permute-done((f32[1,128,256]{2,1,0:T(8,128)S(1)}, f32[1,128,256]{2,1,0:T(8,128)S(1)}, u32[]{:S(2)}, u32[]{:S(2)}) %collective-permute-start.8) | collective-permute-done | bytes 131104 | tf_op jit(solution)/shard_map/ppermute | solution.py:128
  75.7 1.3 %collective-permute-done.9 = f32[1,128,256]{2,1,0:T(8,128)S(1)} collective-permute-done((f32[1,128,256]{2,1,0:T(8,128)S(1)}, f32[1,128,256]{2,1,0:T(8,128)S(1)}, u32[]{:S(2)}, u32[]{:S(2)}) %collective-permute-start.9) | collective-permute-done | bytes 131104 | tf_op jit(solution)/shard_map/ppermute | solution.py:169
  77.0 2.3 %while.53 = (s32[]{:T(128)}, f32[2,128,128]{2,1,0:T(8,128)S(1)}, bf16[2,2,64,128]{3,2,1,0:T(8,128)(2,1)S(1)}, f32[2,2,128,128]{3,2,1,0:T(8,128)S(1)}, f32[2,2,64...) while((s32[]{:T(128)}, f32[2,128,128]{2,1,0:T(8,128)S(1)}, ...), condition=%wide.region_5.6_spmd, body=%wide.region_4.5_spmd.sunk | while | flops 88145920 | bytes 1575041 | solution.py:88
  79.4 2.5 %collective-permute-start.12 = (bf16[128,256]{1,0:T(8,128)(2,1)S(1)}, bf16[128,256]{1,0:T(8,128)(2,1)S(1)}, u32[]{:S(2)}, u32[]{:S(2)}) collective-permute-start(bf16[128,256]{1,0:T(8,128)(2,1)S(1)} %bitcast.676), channel_id=1, source_target_pairs={{0,3},{1,0},{2,1},{3,2},{4,7},{5,4},{6,5},{7,6},{8,11},{9,8},{10,9... | collective-permute-start | bytes 196616 | tf_op jit(solution)/shard_map/ppermute | solution.py:176
  81.9 1.5 %collective-permute-start.11 = (bf16[128,256]{1,0:T(8,128)(2,1)S(1)}, bf16[128,256]{1,0:T(8,128)(2,1)S(1)}, u32[]{:S(2)}, u32[]{:S(2)}) collective-permute-start(bf16[128,256]{1,0:T(8,128)(2,1)S(1)} %bitcast.677), channel_id=1, source_target_pairs={{0,2},{1,3},{2,0},{3,1},{4,6},{5,7},{6,4},{7,5},{8,10},{9,11},{10,... | collective-permute-start | bytes 196616 | tf_op jit(solution)/shard_map/ppermute | solution.py:176
  83.6 5.4 %while.54 = (s32[]{:T(128)}, f32[2,128,128]{2,1,0:T(8,128)S(1)}, f32[2,2,64,128]{3,2,0,1:T(8,128)S(1)}, f32[2,2,64,128]{3,2,0,1:T(8,128)S(1)}, f32[2,2,64,128]{3...) while((s32[]{:T(128)}, f32[2,128,128]{2,1,0:T(8,128)S(1)}, ...), condition=%wide.region_7.8_spmd, body=%wide.region_6.7_spmd.sunk | while | flops 176275456 | bytes 2367145 | solution.py:88
  96.3 0.9 convolution_convert_fusion
  (205 shorter events, 34.8 us)
Async XLA Ops:
  0.7 2.2 %copy-start.12 = (bf16[128,256]{1,0:T(8,128)(2,1)S(1)}, bf16[128,256]{1,0:T(8,128)(2,1)}, u32[]{:S(2)}) copy-start(bf16[128,256]{1,0:T(8,128)(2,1)} %param.17) | copy-start | bytes 196612
  3.0 4.6 %copy-start.10 = (bf16[128,256]{1,0:T(8,128)(2,1)S(1)}, bf16[128,256]{1,0:T(8,128)(2,1)}, u32[]{:S(2)}) copy-start(bf16[128,256]{1,0:T(8,128)(2,1)} %param.13) | copy-start | bytes 196612
  3.0 17.0 %collective-permute-start.2 = (bf16[384,256]{1,0:T(8,128)(2,1)S(1)}, bf16[384,256]{1,0:T(8,128)(2,1)S(1)}, u32[]{:S(2)}, u32[]{:S(2)}) collective-permute-start(bf16[384,256]{1,0:T(8,128)(2,1)S(1)} %get-tuple-element.559), channel_id=1, source_target_pairs={{0,3},{1,0},{2,1},{3,2},{4,7},{5,4},{6,5},{7,6},{8,11},{9,8},{10,9... | collective-permute-start | bytes 589832 | tf_op jit(solution)/shard_map/ppermute | solution.py:196
  5.8 14.2 %collective-permute-start.1 = (bf16[384,256]{1,0:T(8,128)(2,1)S(1)}, bf16[384,256]{1,0:T(8,128)(2,1)S(1)}, u32[]{:S(2)}, u32[]{:S(2)}) collective-permute-start(bf16[384,256]{1,0:T(8,128)(2,1)S(1)} %get-tuple-element.558), channel_id=1, source_target_pairs={{0,2},{1,3},{2,0},{3,1},{4,6},{5,7},{6,4},{7,5},{8,10},{9,11},{10,... | collective-permute-start | bytes 589832 | tf_op jit(solution)/shard_map/ppermute | solution.py:196
  6.6 13.4 %collective-permute-start = (bf16[384,256]{1,0:T(8,128)(2,1)S(1)}, bf16[384,256]{1,0:T(8,128)(2,1)S(1)}, u32[]{:S(2)}, u32[]{:S(2)}) collective-permute-start(bf16[384,256]{1,0:T(8,128)(2,1)S(1)} %get-tuple-element.557), channel_id=1, source_target_pairs={{0,1},{1,2},{2,3},{3,0},{4,5},{5,6},{6,7},{7,4},{8,9},{9,10},{10,1... | collective-permute-start | bytes 589832 | tf_op jit(solution)/shard_map/ppermute | solution.py:196
  20.0 55.7 %copy-start = (bf16[384,256]{1,0:T(8,128)(2,1)}, bf16[384,256]{1,0:T(8,128)(2,1)S(1)}, u32[]{:S(2)}) copy-start(bf16[384,256]{1,0:T(8,128)(2,1)S(1)} %collective-permute-done.2) | copy-start | bytes 589828
  20.0 1.2 %copy-start.4 = (bf16[256,256]{1,0:T(8,128)(2,1)S(1)}, bf16[256,256]{1,0:T(8,128)(2,1)}, u32[]{:S(2)}) copy-start(bf16[256,256]{1,0:T(8,128)(2,1)} %get-tuple-element.527) | copy-start | bytes 393220
  20.0 1.2 %copy-start.5 = (bf16[256,256]{1,0:T(8,128)(2,1)S(1)}, bf16[256,256]{1,0:T(8,128)(2,1)}, u32[]{:S(2)}) copy-start(bf16[256,256]{1,0:T(8,128)(2,1)} %get-tuple-element.528) | copy-start | bytes 393220
  20.0 55.7 %copy-start.1 = (bf16[384,256]{1,0:T(8,128)(2,1)}, bf16[384,256]{1,0:T(8,128)(2,1)S(1)}, u32[]{:S(2)}) copy-start(bf16[384,256]{1,0:T(8,128)(2,1)S(1)} %collective-permute-done.1) | copy-start | bytes 589828
  20.1 55.6 %copy-start.2 = (bf16[384,256]{1,0:T(8,128)(2,1)}, bf16[384,256]{1,0:T(8,128)(2,1)S(1)}, u32[]{:S(2)}) copy-start(bf16[384,256]{1,0:T(8,128)(2,1)S(1)} %collective-permute-done) | copy-start | bytes 589828
  22.9 1.5 %collective-permute-start.3 = (f32[1,128,384]{2,1,0:T(8,128)S(1)}, f32[1,128,384]{2,1,0:T(8,128)S(1)}, u32[]{:S(2)}, u32[]{:S(2)}) collective-permute-start(f32[1,128,384]{2,1,0:T(8,128)S(1)} %fusion.133), channel_id=1, source_target_pairs={{0,4},{4,0},{8,12},{12,8},{16,20},{20,16},{24,28},{28,24},{32,36},... | collective-permute-start | bytes 589832 | tf_op jit(solution)/shard_map/ppermute | solution.py:108
  25.1 7.2 %collective-permute-start.4 = (f32[1,128,384]{2,1,0:T(8,128)S(1)}, f32[1,128,384]{2,1,0:T(8,128)S(1)}, u32[]{:S(2)}, u32[]{:S(2)}) collective-permute-start(f32[1,128,384]{2,1,0:T(8,128)S(1)} %pad_maximum_fusion.3), channel_id=1, source_target_pairs={{0,8},{4,12},{8,0},{12,4},{16,24},{20,28},{24,16},{28,20},{32,40},... | collective-permute-start | bytes 589832 | tf_op jit(solution)/shard_map/ppermute | solution.py:128
  32.9 12.1 %collective-permute-start.5 = (f32[1,128,384]{2,1,0:T(8,128)S(1)}, f32[1,128,384]{2,1,0:T(8,128)S(1)}, u32[]{:S(2)}, u32[]{:S(2)}) collective-permute-start(f32[1,128,384]{2,1,0:T(8,128)S(1)} %pad_maximum_fusion.4), channel_id=1, source_target_pairs={{0,16},{4,20},{8,24},{12,28},{16,0},{20,4},{24,8},{28,12},{32,48},... | collective-permute-start | bytes 589832 | tf_op jit(solution)/shard_map/ppermute | solution.py:128
  46.4 14.0 %collective-permute-start.6 = (f32[1,128,384]{2,1,0:T(8,128)S(1)}, f32[1,128,384]{2,1,0:T(8,128)S(1)}, u32[]{:S(2)}, u32[]{:S(2)}) collective-permute-start(f32[1,128,384]{2,1,0:T(8,128)S(1)} %pad_maximum_fusion.5), channel_id=1, source_target_pairs={{0,32},{4,36},{8,40},{12,44},{16,48},{20,52},{24,56},{28,60},{32,0... | collective-permute-start | bytes 589832 | tf_op jit(solution)/shard_map/ppermute | solution.py:128
  61.6 5.8 %collective-permute-start.7 = (f32[1,128,384]{2,1,0:T(8,128)S(1)}, f32[1,128,384]{2,1,0:T(8,128)S(1)}, u32[]{:S(2)}, u32[]{:S(2)}) collective-permute-start(f32[1,128,384]{2,1,0:T(8,128)S(1)} %pad_maximum_fusion.6), channel_id=1, source_target_pairs={{0,64},{4,68},{8,72},{12,76},{16,80},{20,84},{24,88},{28,92},{32,9... | collective-permute-start | bytes 589832 | tf_op jit(solution)/shard_map/ppermute | solution.py:128
  68.0 6.6 %collective-permute-start.8 = (f32[1,128,256]{2,1,0:T(8,128)S(1)}, f32[1,128,256]{2,1,0:T(8,128)S(1)}, u32[]{:S(2)}, u32[]{:S(2)}) collective-permute-start(f32[1,128,256]{2,1,0:T(8,128)S(1)} %pad_maximum_fusion.7), channel_id=1, source_target_pairs={{0,128},{4,132},{8,136},{12,140},{16,144},{20,148},{24,152},{28,15... | collective-permute-start | bytes 393224 | tf_op jit(solution)/shard_map/ppermute | solution.py:128
  75.5 1.4 %collective-permute-start.9 = (f32[1,128,256]{2,1,0:T(8,128)S(1)}, f32[1,128,256]{2,1,0:T(8,128)S(1)}, u32[]{:S(2)}, u32[]{:S(2)}) collective-permute-start(f32[1,128,256]{2,1,0:T(8,128)S(1)} %pad_maximum_fusion.8), channel_id=1, source_target_pairs={{0,4},{4,0},{8,12},{12,8},{16,20},{20,16},{24,28},{28,24},{32,36},... | collective-permute-start | bytes 393224 | tf_op jit(solution)/shard_map/ppermute | solution.py:169
  79.4 16.8 %collective-permute-start.12 = (bf16[128,256]{1,0:T(8,128)(2,1)S(1)}, bf16[128,256]{1,0:T(8,128)(2,1)S(1)}, u32[]{:S(2)}, u32[]{:S(2)}) collective-permute-start(bf16[128,256]{1,0:T(8,128)(2,1)S(1)} %bitcast.676), channel_id=1, source_target_pairs={{0,3},{1,0},{2,1},{3,2},{4,7},{5,4},{6,5},{7,6},{8,11},{9,8},{10,9... | collective-permute-start | bytes 196616 | tf_op jit(solution)/shard_map/ppermute | solution.py:176
  81.9 14.3 %collective-permute-start.11 = (bf16[128,256]{1,0:T(8,128)(2,1)S(1)}, bf16[128,256]{1,0:T(8,128)(2,1)S(1)}, u32[]{:S(2)}, u32[]{:S(2)}) collective-permute-start(bf16[128,256]{1,0:T(8,128)(2,1)S(1)} %bitcast.677), channel_id=1, source_target_pairs={{0,2},{1,3},{2,0},{3,1},{4,6},{5,7},{6,4},{7,5},{8,10},{9,11},{10,... | collective-permute-start | bytes 196616 | tf_op jit(solution)/shard_map/ppermute | solution.py:176
  83.5 12.8 %collective-permute-start.10 = (bf16[128,256]{1,0:T(8,128)(2,1)S(1)}, bf16[128,256]{1,0:T(8,128)(2,1)S(1)}, u32[]{:S(2)}, u32[]{:S(2)}) collective-permute-start(bf16[128,256]{1,0:T(8,128)(2,1)S(1)} %bitcast.678), channel_id=1, source_target_pairs={{0,1},{1,2},{2,3},{3,0},{4,5},{5,6},{6,7},{7,4},{8,9},{9,10},{10,1... | collective-permute-start | bytes 196616 | tf_op jit(solution)/shard_map/ppermute | solution.py:176
  93.3 3.0 %copy-start.3 = (bf16[256,256]{1,0:T(8,128)(2,1)S(1)}, bf16[256,256]{1,0:T(8,128)(2,1)}, u32[]{:S(2)}) copy-start(bf16[256,256]{1,0:T(8,128)(2,1)} %get-tuple-element.532) | copy-start | bytes 393220
  94.2 2.0 %slice-start.2 = ((bf16[384,256]{1,0:T(8,128)(2,1)}), bf16[256,256]{1,0:T(8,128)(2,1)S(1)}, s32[]{:S(2)}) async-start(bf16[384,256]{1,0:T(8,128)(2,1)} %copy-done.2), calls=%async_computation.2 | async-start | bytes 262144 | tf_op jit(solution)/shard_map/slice | solution.py:202
  94.9 1.4 %slice-start = ((bf16[384,256]{1,0:T(8,128)(2,1)}), bf16[256,256]{1,0:T(8,128)(2,1)S(1)}, s32[]{:S(2)}) async-start(bf16[384,256]{1,0:T(8,128)(2,1)} %copy-done), calls=%async_computation | async-start | bytes 262144 | tf_op jit(solution)/shard_map/slice | solution.py:202
  94.9 1.4 %slice-start.1 = ((bf16[384,256]{1,0:T(8,128)(2,1)}), bf16[256,256]{1,0:T(8,128)(2,1)S(1)}, s32[]{:S(2)}) async-start(bf16[384,256]{1,0:T(8,128)(2,1)} %copy-done.1), calls=%async_computation.1 | async-start | bytes 262144 | tf_op jit(solution)/shard_map/slice | solution.py:202
  (9 other events, 7.7 us)

commit v5 on v4

--- a/solution.py
+++ b/solution.py
@@ -85,7 +85,7 @@
         state = state + jnp.einsum("hcd,hce->hde", unit_key, innovation, precision=highest)
         return (state, block_out)
 
-    return lax.scan(advance_block, start_state, moved)
+    return lax.scan(advance_block, start_state, moved, unroll=True)
 
 
 def mm(left, right):

time: 98.3 us -> 96.7 us (0.984)
  local copies, waits for them, and re-layouts: 12.2 us -> 16 us
  waiting for transfers between devices: 32 us -> 28.7 us
  matrix products: 25.8 us -> 23.6 us
    ppermute x5, waiting for transfers between devices: 29.3 us -> 26.3 us  [scan_both(): got = lax.ppermute(sent, axis, pairs)]
    slice x6 -> x4, local copies, waits for them, and re-layouts: 0.01 us -> 2.64 us  [body(): weight_cols.append(moved[rows:])]
    while x12 -> x0, local copies, waits for them, and re-layouts: 2.37 us -> none
    slice x3, local copies, waits for them, and re-layouts: 0.02 us -> 1.84 us  [body(): grad_parts.append(moved[:rows])]
    unnamed x31 -> x49, local copies, waits for them, and re-layouts: 6.05 us -> 7.47 us
    ppermute x3, starting transfers between devices: 4.03 us -> 2.72 us  [head_ring(): lax.ppermute(part, axis, [(i, (i + k) % count) for i in range(count)])]
    ppermute x3, starting transfers between devices: 4.52 us -> 5.73 us  [body(): lax.ppermute(jnp.concatenate([out_grad, block], 0), 'head', [(i, (i + k)...]
    dot_general x8 -> x7, matrix products: 2.93 us -> 2.4 us  [advance_block(): jnp.einsum('hcd,hce->hde', unit_key, innovation, precision=highest)]
  transfers between devices with their start and end apart: 13 -> 13, of which waited for: 7 -> 7; matrix products, arithmetic and copies ran while one was open for 22% -> 20% of each run, Pallas kernels for 0% -> 0%
where the time goes in v5:
time: 96.7 us; the launch traced here: 95 us
  waiting for transfers between devices  28.7 us (30%)
  matrix products  23.6 us (24%)
  starting transfers between devices  23.4 us (24%)
  local copies, waits for them, and re-layouts  16 us (17%)
  between operations  1.87 us (2%)
  other arithmetic  1.43 us (1%)
    ppermute x5, waiting for transfers between devices, scan_both(): got = lax.ppermute(sent, axis, pairs)  26.3 us
    ppermute x5, starting transfers between devices, scan_both(): got = lax.ppermute(sent, axis, pairs)  14.7 us
    unnamed x49, local copies, waits for them, and re-layouts  7.47 us
    ppermute x3, starting transfers between devices, body(): lax.ppermute(jnp.concatenate([out_grad, block], 0), 'head', [(i, (i + k)...  5.73 us
    dot_general x17, matrix products, mm(): return jnp.einsum('hij,hjk->hik', left, right, precision=highest)  3.76 us
    ppermute x3, starting transfers between devices, head_ring(): lax.ppermute(part, axis, [(i, (i + k) % count) for i in range(count)])  2.72 us
    slice x4, local copies, waits for them, and re-layouts, body(): weight_cols.append(moved[rows:])  2.64 us
    dot_general x7, matrix products, advance_block(): jnp.einsum('hcd,hce->hde', unit_key, innovation, precision=highest)  2.4 us
  transfers between devices with their start and end apart: 13, of which 7 were waited for; matrix products, arithmetic and copies ran while one was open for 20% of the time, Pallas kernels for 0%

profile of v5, /device:TPU:8, one launch (start us, length us, event | category | flops | bytes accessed | tf_op | source)
XLA Modules:
  0.0 95.0 jit_solution(12973685289790336906)
XLA Ops:
  0.8 2.2 %constant_dynamic-slice_fusion.4 = (bf16[256,256]{1,0:T(8,128)(2,1)S(1)}, bf16[256,256]{1,0:T(8,128)(2,1)}, bf16[256,256]{1,0:T(8,128)(2,1)}, bf16[256,256]{1,0:...) fusion(bf16[256,1024]{1,0:T(8,128)(2,1)} %param.10, ...), kind=kLoop, calls=%fused_computation.351 | loop fusion | bytes 2097184 | tf_op jit(solution)/shard_map/dynamic_slice | solution.py:207
  3.0 1.6 %collective-permute-start = (bf16[384,256]{1,0:T(8,128)(2,1)S(1)}, bf16[384,256]{1,0:T(8,128)(2,1)S(1)}, u32[]{:S(2)}, u32[]{:S(2)}) collective-permute-start(bf16[384,256]{1,0:T(8,128)(2,1)S(1)} %get-tuple-element.40), channel_id=1, source_target_pairs={{0,1},{1,2},{2,3},{3,0},{4,5},{5,6},{6,7},{7,4},{8,9},{9,10},{10,1... | collective-permute-start | bytes 589832 | tf_op jit(solution)/shard_map/ppermute | solution.py:196
  4.5 2.7 %collective-permute-start.1 = (bf16[384,256]{1,0:T(8,128)(2,1)S(1)}, bf16[384,256]{1,0:T(8,128)(2,1)}, u32[]{:S(2)}, u32[]{:S(2)}) collective-permute-start(bf16[384,256]{1,0:T(8,128)(2,1)S(1)} %get-tuple-element.41), channel_id=1, source_target_pairs={{0,2},{1,3},{2,0},{3,1},{4,6},{5,7},{6,4},{7,5},{8,10},{9,11},{10,... | collective-permute-start | bytes 589832 | tf_op jit(solution)/shard_map/ppermute | solution.py:196
  7.3 1.4 %collective-permute-start.2 = (bf16[384,256]{1,0:T(8,128)(2,1)S(1)}, bf16[384,256]{1,0:T(8,128)(2,1)}, u32[]{:S(2)}, u32[]{:S(2)}) collective-permute-start(bf16[384,256]{1,0:T(8,128)(2,1)S(1)} %get-tuple-element.42), channel_id=1, source_target_pairs={{0,3},{1,0},{2,1},{3,2},{4,7},{5,4},{6,5},{7,6},{8,11},{9,8},{10,9... | collective-permute-start | bytes 589832 | tf_op jit(solution)/shard_map/ppermute | solution.py:196
  9.6 0.8 copy-done.6
  11.3 0.7 copy-done.7
  19.4 1.0 %slice.293 = bf16[128,256]{1,0:T(8,128)(2,1)S(1)} slice(bf16[384,256]{1,0:T(8,128)(2,1)} %collective-permute-done.1), slice={[0:128], [0:256]} | slice | bytes 131072 | tf_op jit(solution)/shard_map/slice | solution.py:201
  20.4 0.8 slice.294
  22.2 1.4 %collective-permute-done.3 = f32[1,128,384]{2,1,0:T(8,128)S(1)} collective-permute-done((f32[1,128,384]{2,1,0:T(8,128)S(1)}, f32[1,128,384]{2,1,0:T(8,128)S(1)}, u32[]{:S(2)}, u32[]{:S(2)}) %collective-permute-start.3) | collective-permute-done | bytes 196640 | tf_op jit(solution)/shard_map/ppermute | solution.py:108
  24.3 2.0 %collective-permute-start.4 = (f32[1,128,384]{2,1,0:T(8,128)S(1)}, f32[1,128,384]{2,1,0:T(8,128)S(1)}, u32[]{:S(2)}, u32[]{:S(2)}) collective-permute-start(f32[1,128,384]{2,1,0:T(8,128)S(1)} %pad_maximum_fusion.3), channel_id=1, source_target_pairs={{0,8},{4,12},{8,0},{12,4},{16,24},{20,28},{24,16},{28,20},{32,40},... | collective-permute-start | bytes 589832 | tf_op jit(solution)/shard_map/ppermute | solution.py:128
  26.3 5.2 %collective-permute-done.4 = f32[1,128,384]{2,1,0:T(8,128)S(1)} collective-permute-done((f32[1,128,384]{2,1,0:T(8,128)S(1)}, f32[1,128,384]{2,1,0:T(8,128)S(1)}, u32[]{:S(2)}, u32[]{:S(2)}) %collective-permute-start.4) | collective-permute-done | bytes 196640 | tf_op jit(solution)/shard_map/ppermute | solution.py:128
  32.2 3.3 %collective-permute-start.5 = (f32[1,128,384]{2,1,0:T(8,128)S(1)}, f32[1,128,384]{2,1,0:T(8,128)S(1)}, u32[]{:S(2)}, u32[]{:S(2)}) collective-permute-start(f32[1,128,384]{2,1,0:T(8,128)S(1)} %pad_maximum_fusion.4), channel_id=1, source_target_pairs={{0,16},{4,20},{8,24},{12,28},{16,0},{20,4},{24,8},{28,12},{32,48},... | collective-permute-start | bytes 589832 | tf_op jit(solution)/shard_map/ppermute | solution.py:128
  36.2 0.9 slice.344
  37.1 1.6 %slice.345 = bf16[256,256]{1,0:T(8,128)(2,1)} slice(bf16[384,256]{1,0:T(8,128)(2,1)} %collective-permute-done.2), slice={[128:384], [0:256]} | slice | bytes 262144 | tf_op jit(solution)/shard_map/slice | solution.py:202
  38.7 5.6 %collective-permute-done.5 = f32[1,128,384]{2,1,0:T(8,128)S(1)} collective-permute-done((f32[1,128,384]{2,1,0:T(8,128)S(1)}, f32[1,128,384]{2,1,0:T(8,128)S(1)}, u32[]{:S(2)}, u32[]{:S(2)}) %collective-permute-start.5) | collective-permute-done | bytes 196640 | tf_op jit(solution)/shard_map/ppermute | solution.py:128
  45.6 6.5 %collective-permute-start.6 = (f32[1,128,384]{2,1,0:T(8,128)S(1)}, f32[1,128,384]{2,1,0:T(8,128)S(1)}, u32[]{:S(2)}, u32[]{:S(2)}) collective-permute-start(f32[1,128,384]{2,1,0:T(8,128)S(1)} %pad_maximum_fusion.5), channel_id=1, source_target_pairs={{0,32},{4,36},{8,40},{12,44},{16,48},{20,52},{24,56},{28,60},{32,0... | collective-permute-start | bytes 589832 | tf_op jit(solution)/shard_map/ppermute | solution.py:128
  52.3 7.4 %collective-permute-done.6 = f32[1,128,384]{2,1,0:T(8,128)S(1)} collective-permute-done((f32[1,128,384]{2,1,0:T(8,128)S(1)}, f32[1,128,384]{2,1,0:T(8,128)S(1)}, u32[]{:S(2)}, u32[]{:S(2)}) %collective-permute-start.6) | collective-permute-done | bytes 196640 | tf_op jit(solution)/shard_map/ppermute | solution.py:128
  61.8 4.8 %collective-permute-done.7 = f32[1,128,384]{2,1,0:T(8,128)S(1)} collective-permute-done((f32[1,128,384]{2,1,0:T(8,128)S(1)}, f32[1,128,384]{2,1,0:T(8,128)S(1)}, u32[]{:S(2)}, u32[]{:S(2)}) %collective-permute-start.7) | collective-permute-done | bytes 196640 | tf_op jit(solution)/shard_map/ppermute | solution.py:128
  67.2 2.4 %collective-permute-start.8 = (f32[1,128,256]{2,1,0:T(8,128)S(1)}, f32[1,128,256]{2,1,0:T(8,128)S(1)}, u32[]{:S(2)}, u32[]{:S(2)}) collective-permute-start(f32[1,128,256]{2,1,0:T(8,128)S(1)} %pad_maximum_fusion.7), channel_id=1, source_target_pairs={{0,128},{4,132},{8,136},{12,140},{16,144},{20,148},{24,152},{28,15... | collective-permute-start | bytes 393224 | tf_op jit(solution)/shard_map/ppermute | solution.py:128
  70.5 3.3 %collective-permute-done.8 = f32[1,128,256]{2,1,0:T(8,128)S(1)} collective-permute-done((f32[1,128,256]{2,1,0:T(8,128)S(1)}, f32[1,128,256]{2,1,0:T(8,128)S(1)}, u32[]{:S(2)}, u32[]{:S(2)}) %collective-permute-start.8) | collective-permute-done | bytes 131104 | tf_op jit(solution)/shard_map/ppermute | solution.py:128
  75.1 1.0 %collective-permute-done.9 = f32[1,128,256]{2,1,0:T(8,128)S(1)} collective-permute-done((f32[1,128,256]{2,1,0:T(8,128)S(1)}, f32[1,128,256]{2,1,0:T(8,128)S(1)}, u32[]{:S(2)}, u32[]{:S(2)}) %collective-permute-start.9) | collective-permute-done | bytes 131104 | tf_op jit(solution)/shard_map/ppermute | solution.py:169
  83.2 2.6 %collective-permute-start.11 = (bf16[128,256]{1,0:T(8,128)(2,1)S(1)}, bf16[128,256]{1,0:T(8,128)(2,1)S(1)}, u32[]{:S(2)}, u32[]{:S(2)}) collective-permute-start(bf16[128,256]{1,0:T(8,128)(2,1)S(1)} %bitcast.573), channel_id=1, source_target_pairs={{0,2},{1,3},{2,0},{3,1},{4,6},{5,7},{6,4},{7,5},{8,10},{9,11},{10,... | collective-permute-start | bytes 196616 | tf_op jit(solution)/shard_map/ppermute | solution.py:176
  90.2 0.7 copy-done.20
  94.1 0.9 convolution_convert_fusion
  (193 shorter events, 32.3 us)
Async XLA Ops:
  0.8 2.2 %copy-start.8 = (bf16[128,256]{1,0:T(8,128)(2,1)S(1)}, bf16[128,256]{1,0:T(8,128)(2,1)}, u32[]{:S(2)}) copy-start(bf16[128,256]{1,0:T(8,128)(2,1)} %param.11) | copy-start | bytes 196612
  3.0 16.4 %collective-permute-start = (bf16[384,256]{1,0:T(8,128)(2,1)S(1)}, bf16[384,256]{1,0:T(8,128)(2,1)S(1)}, u32[]{:S(2)}, u32[]{:S(2)}) collective-permute-start(bf16[384,256]{1,0:T(8,128)(2,1)S(1)} %get-tuple-element.40), channel_id=1, source_target_pairs={{0,1},{1,2},{2,3},{3,0},{4,5},{5,6},{6,7},{7,4},{8,9},{9,10},{10,1... | collective-permute-start | bytes 589832 | tf_op jit(solution)/shard_map/ppermute | solution.py:196
  4.5 14.9 %collective-permute-start.1 = (bf16[384,256]{1,0:T(8,128)(2,1)S(1)}, bf16[384,256]{1,0:T(8,128)(2,1)}, u32[]{:S(2)}, u32[]{:S(2)}) collective-permute-start(bf16[384,256]{1,0:T(8,128)(2,1)S(1)} %get-tuple-element.41), channel_id=1, source_target_pairs={{0,2},{1,3},{2,0},{3,1},{4,6},{5,7},{6,4},{7,5},{8,10},{9,11},{10,... | collective-permute-start | bytes 589832 | tf_op jit(solution)/shard_map/ppermute | solution.py:196
  7.3 13.2 %collective-permute-start.2 = (bf16[384,256]{1,0:T(8,128)(2,1)S(1)}, bf16[384,256]{1,0:T(8,128)(2,1)}, u32[]{:S(2)}, u32[]{:S(2)}) collective-permute-start(bf16[384,256]{1,0:T(8,128)(2,1)S(1)} %get-tuple-element.42), channel_id=1, source_target_pairs={{0,3},{1,0},{2,1},{3,2},{4,7},{5,4},{6,5},{7,6},{8,11},{9,8},{10,9... | collective-permute-start | bytes 589832 | tf_op jit(solution)/shard_map/ppermute | solution.py:196
  9.5 6.3 %copy-start.11 = (f32[2,64,2]{1,0,2:T(2,128)}, f32[2,64,2]{1,0,2:T(2,128)S(1)}, u32[]{:S(2)}) copy-start(f32[2,64,2]{1,0,2:T(2,128)S(1)} %reshape.252) | copy-start | bytes 3076
  9.5 3.4 %copy-start.14 = (f32[2,2,64]{2,0,1:T(2,128)}, f32[2,2,64]{2,0,1:T(2,128)S(1)}, u32[]{:S(2)}) copy-start(f32[2,2,64]{2,0,1:T(2,128)S(1)} %copy.264) | copy-start | bytes 3076
  18.9 2.4 %copy-start.9 = (bf16[128,256]{1,0:T(8,128)(2,1)S(1)}, bf16[128,256]{1,0:T(8,128)(2,1)}, u32[]{:S(2)}) copy-start(bf16[128,256]{1,0:T(8,128)(2,1)} %param.11) | copy-start | bytes 196612
  19.4 16.8 %copy-start = (bf16[384,256]{1,0:T(8,128)(2,1)}, bf16[384,256]{1,0:T(8,128)(2,1)S(1)}, u32[]{:S(2)}) copy-start(bf16[384,256]{1,0:T(8,128)(2,1)S(1)} %collective-permute-done) | copy-start | bytes 589828
  19.4 1.9 %copy-start.4 = (bf16[256,256]{1,0:T(8,128)(2,1)S(1)}, bf16[256,256]{1,0:T(8,128)(2,1)}, u32[]{:S(2)}) copy-start(bf16[256,256]{1,0:T(8,128)(2,1)} %get-tuple-element.18) | copy-start | bytes 393220
  19.4 1.9 %copy-start.2 = (bf16[256,256]{1,0:T(8,128)(2,1)S(1)}, bf16[256,256]{1,0:T(8,128)(2,1)}, u32[]{:S(2)}) copy-start(bf16[256,256]{1,0:T(8,128)(2,1)} %get-tuple-element.12) | copy-start | bytes 393220
  19.4 1.9 %copy-start.3 = (bf16[256,256]{1,0:T(8,128)(2,1)S(1)}, bf16[256,256]{1,0:T(8,128)(2,1)}, u32[]{:S(2)}) copy-start(bf16[256,256]{1,0:T(8,128)(2,1)} %get-tuple-element.13) | copy-start | bytes 393220
  22.1 1.5 %collective-permute-start.3 = (f32[1,128,384]{2,1,0:T(8,128)S(1)}, f32[1,128,384]{2,1,0:T(8,128)S(1)}, u32[]{:S(2)}, u32[]{:S(2)}) collective-permute-start(f32[1,128,384]{2,1,0:T(8,128)S(1)} %fusion.74), channel_id=1, source_target_pairs={{0,4},{4,0},{8,12},{12,8},{16,20},{20,16},{24,28},{28,24},{32,36},... | collective-permute-start | bytes 589832 | tf_op jit(solution)/shard_map/ppermute | solution.py:108
  24.3 7.2 %collective-permute-start.4 = (f32[1,128,384]{2,1,0:T(8,128)S(1)}, f32[1,128,384]{2,1,0:T(8,128)S(1)}, u32[]{:S(2)}, u32[]{:S(2)}) collective-permute-start(f32[1,128,384]{2,1,0:T(8,128)S(1)} %pad_maximum_fusion.3), channel_id=1, source_target_pairs={{0,8},{4,12},{8,0},{12,4},{16,24},{20,28},{24,16},{28,20},{32,40},... | collective-permute-start | bytes 589832 | tf_op jit(solution)/shard_map/ppermute | solution.py:128
  32.2 3.4 %copy-start.12 = (f32[2,64,2]{1,0,2:T(2,128)S(1)}, f32[2,64,2]{1,0,2:T(2,128)}, u32[]{:S(2)}) copy-start(f32[2,64,2]{1,0,2:T(2,128)} %copy-done.11) | copy-start | bytes 3076
  32.2 12.1 %collective-permute-start.5 = (f32[1,128,384]{2,1,0:T(8,128)S(1)}, f32[1,128,384]{2,1,0:T(8,128)S(1)}, u32[]{:S(2)}, u32[]{:S(2)}) collective-permute-start(f32[1,128,384]{2,1,0:T(8,128)S(1)} %pad_maximum_fusion.4), channel_id=1, source_target_pairs={{0,16},{4,20},{8,24},{12,28},{16,0},{20,4},{24,8},{28,12},{32,48},... | collective-permute-start | bytes 589832 | tf_op jit(solution)/shard_map/ppermute | solution.py:128
  45.6 14.1 %collective-permute-start.6 = (f32[1,128,384]{2,1,0:T(8,128)S(1)}, f32[1,128,384]{2,1,0:T(8,128)S(1)}, u32[]{:S(2)}, u32[]{:S(2)}) collective-permute-start(f32[1,128,384]{2,1,0:T(8,128)S(1)} %pad_maximum_fusion.5), channel_id=1, source_target_pairs={{0,32},{4,36},{8,40},{12,44},{16,48},{20,52},{24,56},{28,60},{32,0... | collective-permute-start | bytes 589832 | tf_op jit(solution)/shard_map/ppermute | solution.py:128
  60.8 5.8 %collective-permute-start.7 = (f32[1,128,384]{2,1,0:T(8,128)S(1)}, f32[1,128,384]{2,1,0:T(8,128)S(1)}, u32[]{:S(2)}, u32[]{:S(2)}) collective-permute-start(f32[1,128,384]{2,1,0:T(8,128)S(1)} %pad_maximum_fusion.6), channel_id=1, source_target_pairs={{0,64},{4,68},{8,72},{12,76},{16,80},{20,84},{24,88},{28,92},{32,9... | collective-permute-start | bytes 589832 | tf_op jit(solution)/shard_map/ppermute | solution.py:128
  67.2 6.6 %collective-permute-start.8 = (f32[1,128,256]{2,1,0:T(8,128)S(1)}, f32[1,128,256]{2,1,0:T(8,128)S(1)}, u32[]{:S(2)}, u32[]{:S(2)}) collective-permute-start(f32[1,128,256]{2,1,0:T(8,128)S(1)} %pad_maximum_fusion.7), channel_id=1, source_target_pairs={{0,128},{4,132},{8,136},{12,140},{16,144},{20,148},{24,152},{28,15... | collective-permute-start | bytes 393224 | tf_op jit(solution)/shard_map/ppermute | solution.py:128
  74.8 1.4 %collective-permute-start.9 = (f32[1,128,256]{2,1,0:T(8,128)S(1)}, f32[1,128,256]{2,1,0:T(8,128)S(1)}, u32[]{:S(2)}, u32[]{:S(2)}) collective-permute-start(f32[1,128,256]{2,1,0:T(8,128)S(1)} %pad_maximum_fusion.10), channel_id=1, source_target_pairs={{0,4},{4,0},{8,12},{12,8},{16,20},{20,16},{24,28},{28,24},{32,36},... | collective-permute-start | bytes 393224 | tf_op jit(solution)/shard_map/ppermute | solution.py:169
  83.1 10.8 %collective-permute-start.12 = (bf16[128,256]{1,0:T(8,128)(2,1)S(1)}, bf16[128,256]{1,0:T(8,128)(2,1)S(1)}, u32[]{:S(2)}, u32[]{:S(2)}) collective-permute-start(bf16[128,256]{1,0:T(8,128)(2,1)S(1)} %bitcast.572), channel_id=1, source_target_pairs={{0,3},{1,0},{2,1},{3,2},{4,7},{5,4},{6,5},{7,6},{8,11},{9,8},{10,9... | collective-permute-start | bytes 196616 | tf_op jit(solution)/shard_map/ppermute | solution.py:176
  83.2 10.7 %collective-permute-start.11 = (bf16[128,256]{1,0:T(8,128)(2,1)S(1)}, bf16[128,256]{1,0:T(8,128)(2,1)S(1)}, u32[]{:S(2)}, u32[]{:S(2)}) collective-permute-start(bf16[128,256]{1,0:T(8,128)(2,1)S(1)} %bitcast.573), channel_id=1, source_target_pairs={{0,2},{1,3},{2,0},{3,1},{4,6},{5,7},{6,4},{7,5},{8,10},{9,11},{10,... | collective-permute-start | bytes 196616 | tf_op jit(solution)/shard_map/ppermute | solution.py:176
  85.8 8.1 %collective-permute-start.10 = (bf16[128,256]{1,0:T(8,128)(2,1)S(1)}, bf16[128,256]{1,0:T(8,128)(2,1)S(1)}, u32[]{:S(2)}, u32[]{:S(2)}) collective-permute-start(bf16[128,256]{1,0:T(8,128)(2,1)S(1)} %bitcast.574), channel_id=1, source_target_pairs={{0,1},{1,2},{2,3},{3,0},{4,5},{5,6},{6,7},{7,4},{8,9},{9,10},{10,1... | collective-permute-start | bytes 196616 | tf_op jit(solution)/shard_map/ppermute | solution.py:176
  91.9 2.0 %copy-start.5 = (bf16[256,256]{1,0:T(8,128)(2,1)S(1)}, bf16[256,256]{1,0:T(8,128)(2,1)}, u32[]{:S(2)}) copy-start(bf16[256,256]{1,0:T(8,128)(2,1)} %slice.345) | copy-start | bytes 393220
  93.2 1.0 %copy-start.1 = (bf16[256,256]{1,0:T(8,128)(2,1)S(1)}, bf16[256,256]{1,0:T(8,128)(2,1)}, u32[]{:S(2)}) copy-start(bf16[256,256]{1,0:T(8,128)(2,1)} %get-tuple-element.17) | copy-start | bytes 393220
  (12 other events, 8.7 us)

commit v6 on v5

--- a/solution.py
+++ b/solution.py
@@ -39,11 +39,17 @@
 def unit_lower_inverse_fwd(strict_lower):
     size = strict_lower.shape[-1]
     result = jnp.eye(size, dtype=jnp.float32) - strict_lower
-    power_term = strict_lower
+    power_term = jnp.einsum("hnij,hnjk->hnik", strict_lower, strict_lower, precision=highest)
     span_done = 2
     while span_done < size:
-        power_term = jnp.einsum("hnij,hnjk->hnik", power_term, power_term, precision=highest)
-        result = result + jnp.einsum("hnij,hnjk->hnik", result, power_term, precision=highest)
+        both = jnp.einsum(
+            "hnij,hnjk->hnik",
+            jnp.concatenate([power_term, result], -2),
+            power_term,
+            precision=highest,
+        )
+        power_term = both[..., :size, :]
+        result = result + both[..., size:, :]
         span_done = span_done * 2
     return result, result
 
@@ -193,13 +199,17 @@
             block = lax.dynamic_slice_in_dim(
                 out_weight, ((here + k) % head_devices) * width, width, 1
             )
-            moved = lax.ppermute(
-                jnp.concatenate([out_grad, block], 0),
-                "head",
-                [(i, (i + k) % head_devices) for i in range(head_devices)],
-            )
-            grad_parts.append(moved[:rows])
-            weight_cols.append(moved[rows:])
+            pairs = [(i, (i + k) % head_devices) for i in range(head_devices)]
+            if block.shape[0] % rows == 0:
+                moved = lax.ppermute(
+                    jnp.concatenate([out_grad[None], block.reshape(-1, rows, width)], 0), "head", pairs
+                )
+                grad_parts.append(moved[0])
+                weight_cols.append(moved[1:].reshape(-1, width))
+            else:
+                moved = lax.ppermute(jnp.concatenate([out_grad, block], 0), "head", pairs)
+                grad_parts.append(moved[:rows])
+                weight_cols.append(moved[rows:])
         weight_mine = jnp.concatenate(weight_cols, 0)
 
         weight_rows = jnp.concatenate(

time: 96.7 us -> 96.6 us (level)
    squeeze x0 -> x3, local copies, waits for them, and re-layouts: none -> 1.84 us  [body(): grad_parts.append(moved[0])]
    slice x7 -> x4, local copies, waits for them, and re-layouts: 4.48 us -> 2.65 us  [body(): weight_cols.append(moved[1:].reshape(-1, width))]
    dot_general x10 -> x6, matrix products: 2.57 us -> 2.02 us  [the longest x5 1.75 us: unit_lower_inverse_fwd(): jnp.einsum('hnij,hnjk->hnik', jnp.concatenate([power_term, result], -2),...]
where the time goes in v6:
time: 96.6 us; the launch traced here: 95 us
  waiting for transfers between devices  28.7 us (30%)
  starting transfers between devices  23.5 us (24%)
  matrix products  23.3 us (24%)
  local copies, waits for them, and re-layouts  15.8 us (16%)
  between operations  1.86 us (2%)
  other arithmetic  1.77 us (2%)
    ppermute x5, waiting for transfers between devices, scan_both(): got = lax.ppermute(sent, axis, pairs)  26.2 us
    ppermute x5, starting transfers between devices, scan_both(): got = lax.ppermute(sent, axis, pairs)  14.8 us
    unnamed x49, local copies, waits for them, and re-layouts  7.29 us
    ppermute x3, starting transfers between devices, body(): lax.ppermute(jnp.concatenate([out_grad[None], block.reshape(-1, rows, wid...  5.73 us
    dot_general x17, matrix products, mm(): return jnp.einsum('hij,hjk->hik', left, right, precision=highest)  3.76 us
    ppermute x3, starting transfers between devices, head_ring(): lax.ppermute(part, axis, [(i, (i + k) % count) for i in range(count)])  2.71 us
    slice x4, local copies, waits for them, and re-layouts, body(): weight_cols.append(moved[1:].reshape(-1, width))  2.65 us
    dot_general x7, matrix products, advance_block(): jnp.einsum('hcd,hce->hde', unit_key, innovation, precision=highest)  2.41 us
  transfers between devices with their start and end apart: 13, of which 7 were waited for; matrix products, arithmetic and copies ran while one was open for 20% of the time, Pallas kernels for 0%

profile of v6, /device:TPU:8, one launch (start us, length us, event | category | flops | bytes accessed | tf_op | source)
XLA Modules:
  0.0 95.0 jit_solution(12454424752585842603)
XLA Ops:
  0.8 2.2 %constant_dynamic-slice_fusion.4 = (bf16[256,256]{1,0:T(8,128)(2,1)S(1)}, bf16[256,256]{1,0:T(8,128)(2,1)}, bf16[256,256]{1,0:T(8,128)(2,1)}, bf16[256,256]{1,0:...) fusion(bf16[256,1024]{1,0:T(8,128)(2,1)} %param.10, ...), kind=kLoop, calls=%fused_computation.371 | loop fusion | bytes 2097184 | tf_op jit(solution)/shard_map/dynamic_slice | solution.py:217
  3.0 1.6 %collective-permute-start = (bf16[3,128,256]{2,1,0:T(8,128)(2,1)S(1)}, bf16[3,128,256]{2,1,0:T(8,128)(2,1)S(1)}, u32[]{:S(2)}, u32[]{:S(2)}) collective-permute-start(bf16[3,128,256]{2,1,0:T(8,128)(2,1)S(1)} %get-tuple-element.48), channel_id=1, source_target_pairs={{0,1},{1,2},{2,3},{3,0},{4,5},{5,6},{6,7},{7,4},{8,9},{9,10},{10,1... | collective-permute-start | bytes 589832 | tf_op jit(solution)/shard_map/ppermute | solution.py:204
  4.5 2.7 %collective-permute-start.1 = (bf16[3,128,256]{2,1,0:T(8,128)(2,1)S(1)}, bf16[3,128,256]{2,1,0:T(8,128)(2,1)}, u32[]{:S(2)}, u32[]{:S(2)}) collective-permute-start(bf16[3,128,256]{2,1,0:T(8,128)(2,1)S(1)} %get-tuple-element.49), channel_id=1, source_target_pairs={{0,2},{1,3},{2,0},{3,1},{4,6},{5,7},{6,4},{7,5},{8,10},{9,11},{10,... | collective-permute-start | bytes 589832 | tf_op jit(solution)/shard_map/ppermute | solution.py:204
  7.3 1.4 %collective-permute-start.2 = (bf16[3,128,256]{2,1,0:T(8,128)(2,1)S(1)}, bf16[3,128,256]{2,1,0:T(8,128)(2,1)}, u32[]{:S(2)}, u32[]{:S(2)}) collective-permute-start(bf16[3,128,256]{2,1,0:T(8,128)(2,1)S(1)} %get-tuple-element.50), channel_id=1, source_target_pairs={{0,3},{1,0},{2,1},{3,2},{4,7},{5,4},{6,5},{7,6},{8,11},{9,8},{10,9... | collective-permute-start | bytes 589832 | tf_op jit(solution)/shard_map/ppermute | solution.py:204
  8.8 0.7 copy-done.21
  9.6 0.8 copy-done.6
  11.3 0.7 copy-done.7
  19.6 1.0 %slice_bitcast_fusion.34 = bf16[128,256]{1,0:T(8,128)(2,1)S(1)} fusion(bf16[3,128,256]{2,1,0:T(8,128)(2,1)} %collective-permute-done.1), kind=kLoop, calls=%fused_computation.296 | loop fusion | bytes 131072 | tf_op jit(solution)/shard_map/squeeze | solution.py:207
  20.6 0.8 slice_bitcast_fusion.33
  22.4 1.4 %collective-permute-done.3 = f32[1,128,384]{2,1,0:T(8,128)S(1)} collective-permute-done((f32[1,128,384]{2,1,0:T(8,128)S(1)}, f32[1,128,384]{2,1,0:T(8,128)S(1)}, u32[]{:S(2)}, u32[]{:S(2)}) %collective-permute-start.3) | collective-permute-done | bytes 196640 | tf_op jit(solution)/shard_map/ppermute | solution.py:114
  24.5 2.0 %collective-permute-start.4 = (f32[1,128,384]{2,1,0:T(8,128)S(1)}, f32[1,128,384]{2,1,0:T(8,128)S(1)}, u32[]{:S(2)}, u32[]{:S(2)}) collective-permute-start(f32[1,128,384]{2,1,0:T(8,128)S(1)} %pad_maximum_fusion.3), channel_id=1, source_target_pairs={{0,8},{4,12},{8,0},{12,4},{16,24},{20,28},{24,16},{28,20},{32,40},... | collective-permute-start | bytes 589832 | tf_op jit(solution)/shard_map/ppermute | solution.py:134
  26.5 5.2 %collective-permute-done.4 = f32[1,128,384]{2,1,0:T(8,128)S(1)} collective-permute-done((f32[1,128,384]{2,1,0:T(8,128)S(1)}, f32[1,128,384]{2,1,0:T(8,128)S(1)}, u32[]{:S(2)}, u32[]{:S(2)}) %collective-permute-start.4) | collective-permute-done | bytes 196640 | tf_op jit(solution)/shard_map/ppermute | solution.py:134
  32.3 3.4 %collective-permute-start.5 = (f32[1,128,384]{2,1,0:T(8,128)S(1)}, f32[1,128,384]{2,1,0:T(8,128)S(1)}, u32[]{:S(2)}, u32[]{:S(2)}) collective-permute-start(f32[1,128,384]{2,1,0:T(8,128)S(1)} %pad_maximum_fusion.4), channel_id=1, source_target_pairs={{0,16},{4,20},{8,24},{12,28},{16,0},{20,4},{24,8},{28,12},{32,48},... | collective-permute-start | bytes 589832 | tf_op jit(solution)/shard_map/ppermute | solution.py:134
  36.3 0.9 slice.389
  37.2 1.6 %slice.390 = bf16[2,128,256]{2,1,0:T(8,128)(2,1)} slice(bf16[3,128,256]{2,1,0:T(8,128)(2,1)} %collective-permute-done.2), slice={[1:3], [0:128], [0:256]} | slice | bytes 262144 | tf_op jit(solution)/shard_map/slice | solution.py:208
  38.9 5.6 %collective-permute-done.5 = f32[1,128,384]{2,1,0:T(8,128)S(1)} collective-permute-done((f32[1,128,384]{2,1,0:T(8,128)S(1)}, f32[1,128,384]{2,1,0:T(8,128)S(1)}, u32[]{:S(2)}, u32[]{:S(2)}) %collective-permute-start.5) | collective-permute-done | bytes 196640 | tf_op jit(solution)/shard_map/ppermute | solution.py:134
  45.8 6.5 %collective-permute-start.6 = (f32[1,128,384]{2,1,0:T(8,128)S(1)}, f32[1,128,384]{2,1,0:T(8,128)S(1)}, u32[]{:S(2)}, u32[]{:S(2)}) collective-permute-start(f32[1,128,384]{2,1,0:T(8,128)S(1)} %pad_maximum_fusion.5), channel_id=1, source_target_pairs={{0,32},{4,36},{8,40},{12,44},{16,48},{20,52},{24,56},{28,60},{32,0... | collective-permute-start | bytes 589832 | tf_op jit(solution)/shard_map/ppermute | solution.py:134
  52.5 7.4 %collective-permute-done.6 = f32[1,128,384]{2,1,0:T(8,128)S(1)} collective-permute-done((f32[1,128,384]{2,1,0:T(8,128)S(1)}, f32[1,128,384]{2,1,0:T(8,128)S(1)}, u32[]{:S(2)}, u32[]{:S(2)}) %collective-permute-start.6) | collective-permute-done | bytes 196640 | tf_op jit(solution)/shard_map/ppermute | solution.py:134
  61.9 4.8 %collective-permute-done.7 = f32[1,128,384]{2,1,0:T(8,128)S(1)} collective-permute-done((f32[1,128,384]{2,1,0:T(8,128)S(1)}, f32[1,128,384]{2,1,0:T(8,128)S(1)}, u32[]{:S(2)}, u32[]{:S(2)}) %collective-permute-start.7) | collective-permute-done | bytes 196640 | tf_op jit(solution)/shard_map/ppermute | solution.py:134
  67.4 2.4 %collective-permute-start.8 = (f32[1,128,256]{2,1,0:T(8,128)S(1)}, f32[1,128,256]{2,1,0:T(8,128)S(1)}, u32[]{:S(2)}, u32[]{:S(2)}) collective-permute-start(f32[1,128,256]{2,1,0:T(8,128)S(1)} %pad_maximum_fusion.7), channel_id=1, source_target_pairs={{0,128},{4,132},{8,136},{12,140},{16,144},{20,148},{24,152},{28,15... | collective-permute-start | bytes 393224 | tf_op jit(solution)/shard_map/ppermute | solution.py:134
  70.7 3.2 %collective-permute-done.8 = f32[1,128,256]{2,1,0:T(8,128)S(1)} collective-permute-done((f32[1,128,256]{2,1,0:T(8,128)S(1)}, f32[1,128,256]{2,1,0:T(8,128)S(1)}, u32[]{:S(2)}, u32[]{:S(2)}) %collective-permute-start.8) | collective-permute-done | bytes 131104 | tf_op jit(solution)/shard_map/ppermute | solution.py:134
  75.2 1.1 %collective-permute-done.9 = f32[1,128,256]{2,1,0:T(8,128)S(1)} collective-permute-done((f32[1,128,256]{2,1,0:T(8,128)S(1)}, f32[1,128,256]{2,1,0:T(8,128)S(1)}, u32[]{:S(2)}, u32[]{:S(2)}) %collective-permute-start.9) | collective-permute-done | bytes 131104 | tf_op jit(solution)/shard_map/ppermute | solution.py:175
  83.3 2.6 %collective-permute-start.11 = (bf16[128,256]{1,0:T(8,128)(2,1)S(1)}, bf16[128,256]{1,0:T(8,128)(2,1)S(1)}, u32[]{:S(2)}, u32[]{:S(2)}) collective-permute-start(bf16[128,256]{1,0:T(8,128)(2,1)S(1)} %bitcast.581), channel_id=1, source_target_pairs={{0,2},{1,3},{2,0},{3,1},{4,6},{5,7},{6,4},{7,5},{8,10},{9,11},{10,... | collective-permute-start | bytes 196616 | tf_op jit(solution)/shard_map/ppermute | solution.py:182
  94.1 0.9 convolution_convert_fusion
  (192 shorter events, 32.2 us)
Async XLA Ops:
  0.8 2.2 %copy-start.8 = (bf16[128,256]{1,0:T(8,128)(2,1)S(1)}, bf16[128,256]{1,0:T(8,128)(2,1)}, u32[]{:S(2)}) copy-start(bf16[128,256]{1,0:T(8,128)(2,1)} %param.11) | copy-start | bytes 196612
  3.0 16.6 %collective-permute-start = (bf16[3,128,256]{2,1,0:T(8,128)(2,1)S(1)}, bf16[3,128,256]{2,1,0:T(8,128)(2,1)S(1)}, u32[]{:S(2)}, u32[]{:S(2)}) collective-permute-start(bf16[3,128,256]{2,1,0:T(8,128)(2,1)S(1)} %get-tuple-element.48), channel_id=1, source_target_pairs={{0,1},{1,2},{2,3},{3,0},{4,5},{5,6},{6,7},{7,4},{8,9},{9,10},{10,1... | collective-permute-start | bytes 589832 | tf_op jit(solution)/shard_map/ppermute | solution.py:204
  4.5 15.1 %collective-permute-start.1 = (bf16[3,128,256]{2,1,0:T(8,128)(2,1)S(1)}, bf16[3,128,256]{2,1,0:T(8,128)(2,1)}, u32[]{:S(2)}, u32[]{:S(2)}) collective-permute-start(bf16[3,128,256]{2,1,0:T(8,128)(2,1)S(1)} %get-tuple-element.49), channel_id=1, source_target_pairs={{0,2},{1,3},{2,0},{3,1},{4,6},{5,7},{6,4},{7,5},{8,10},{9,11},{10,... | collective-permute-start | bytes 589832 | tf_op jit(solution)/shard_map/ppermute | solution.py:204
  7.3 13.3 %collective-permute-start.2 = (bf16[3,128,256]{2,1,0:T(8,128)(2,1)S(1)}, bf16[3,128,256]{2,1,0:T(8,128)(2,1)}, u32[]{:S(2)}, u32[]{:S(2)}) collective-permute-start(bf16[3,128,256]{2,1,0:T(8,128)(2,1)S(1)} %get-tuple-element.50), channel_id=1, source_target_pairs={{0,3},{1,0},{2,1},{3,2},{4,7},{5,4},{6,5},{7,6},{8,11},{9,8},{10,9... | collective-permute-start | bytes 589832 | tf_op jit(solution)/shard_map/ppermute | solution.py:204
  9.5 6.0 %copy-start.11 = (f32[2,64,2]{1,0,2:T(2,128)}, f32[2,64,2]{1,0,2:T(2,128)S(1)}, u32[]{:S(2)}) copy-start(f32[2,64,2]{1,0,2:T(2,128)S(1)} %reshape.270) | copy-start | bytes 3076
  9.5 3.3 %copy-start.14 = (f32[2,2,64]{2,0,1:T(2,128)}, f32[2,2,64]{2,0,1:T(2,128)S(1)}, u32[]{:S(2)}) copy-start(f32[2,2,64]{2,0,1:T(2,128)S(1)} %copy.312) | copy-start | bytes 3076
  19.1 2.4 %copy-start.9 = (bf16[128,256]{1,0:T(8,128)(2,1)S(1)}, bf16[128,256]{1,0:T(8,128)(2,1)}, u32[]{:S(2)}) copy-start(bf16[128,256]{1,0:T(8,128)(2,1)} %param.11) | copy-start | bytes 196612
  19.6 16.7 %copy-start = (bf16[3,128,256]{2,1,0:T(8,128)(2,1)}, bf16[3,128,256]{2,1,0:T(8,128)(2,1)S(1)}, u32[]{:S(2)}) copy-start(bf16[3,128,256]{2,1,0:T(8,128)(2,1)S(1)} %collective-permute-done) | copy-start | bytes 589828
  19.6 1.9 %copy-start.4 = (bf16[256,256]{1,0:T(8,128)(2,1)S(1)}, bf16[256,256]{1,0:T(8,128)(2,1)}, u32[]{:S(2)}) copy-start(bf16[256,256]{1,0:T(8,128)(2,1)} %get-tuple-element.18) | copy-start | bytes 393220
  19.6 1.9 %copy-start.2 = (bf16[256,256]{1,0:T(8,128)(2,1)S(1)}, bf16[256,256]{1,0:T(8,128)(2,1)}, u32[]{:S(2)}) copy-start(bf16[256,256]{1,0:T(8,128)(2,1)} %get-tuple-element.12) | copy-start | bytes 393220
  19.6 1.9 %copy-start.3 = (bf16[256,256]{1,0:T(8,128)(2,1)S(1)}, bf16[256,256]{1,0:T(8,128)(2,1)}, u32[]{:S(2)}) copy-start(bf16[256,256]{1,0:T(8,128)(2,1)} %get-tuple-element.13) | copy-start | bytes 393220
  22.3 1.5 %collective-permute-start.3 = (f32[1,128,384]{2,1,0:T(8,128)S(1)}, f32[1,128,384]{2,1,0:T(8,128)S(1)}, u32[]{:S(2)}, u32[]{:S(2)}) collective-permute-start(f32[1,128,384]{2,1,0:T(8,128)S(1)} %fusion.74), channel_id=1, source_target_pairs={{0,4},{4,0},{8,12},{12,8},{16,20},{20,16},{24,28},{28,24},{32,36},... | collective-permute-start | bytes 589832 | tf_op jit(solution)/shard_map/ppermute | solution.py:114
  24.5 7.2 %collective-permute-start.4 = (f32[1,128,384]{2,1,0:T(8,128)S(1)}, f32[1,128,384]{2,1,0:T(8,128)S(1)}, u32[]{:S(2)}, u32[]{:S(2)}) collective-permute-start(f32[1,128,384]{2,1,0:T(8,128)S(1)} %pad_maximum_fusion.3), channel_id=1, source_target_pairs={{0,8},{4,12},{8,0},{12,4},{16,24},{20,28},{24,16},{28,20},{32,40},... | collective-permute-start | bytes 589832 | tf_op jit(solution)/shard_map/ppermute | solution.py:134
  32.3 3.4 %copy-start.12 = (f32[2,64,2]{1,0,2:T(2,128)S(1)}, f32[2,64,2]{1,0,2:T(2,128)}, u32[]{:S(2)}) copy-start(f32[2,64,2]{1,0,2:T(2,128)} %copy-done.11) | copy-start | bytes 3076
  32.3 12.1 %collective-permute-start.5 = (f32[1,128,384]{2,1,0:T(8,128)S(1)}, f32[1,128,384]{2,1,0:T(8,128)S(1)}, u32[]{:S(2)}, u32[]{:S(2)}) collective-permute-start(f32[1,128,384]{2,1,0:T(8,128)S(1)} %pad_maximum_fusion.4), channel_id=1, source_target_pairs={{0,16},{4,20},{8,24},{12,28},{16,0},{20,4},{24,8},{28,12},{32,48},... | collective-permute-start | bytes 589832 | tf_op jit(solution)/shard_map/ppermute | solution.py:134
  45.8 14.1 %collective-permute-start.6 = (f32[1,128,384]{2,1,0:T(8,128)S(1)}, f32[1,128,384]{2,1,0:T(8,128)S(1)}, u32[]{:S(2)}, u32[]{:S(2)}) collective-permute-start(f32[1,128,384]{2,1,0:T(8,128)S(1)} %pad_maximum_fusion.5), channel_id=1, source_target_pairs={{0,32},{4,36},{8,40},{12,44},{16,48},{20,52},{24,56},{28,60},{32,0... | collective-permute-start | bytes 589832 | tf_op jit(solution)/shard_map/ppermute | solution.py:134
  60.9 5.8 %collective-permute-start.7 = (f32[1,128,384]{2,1,0:T(8,128)S(1)}, f32[1,128,384]{2,1,0:T(8,128)S(1)}, u32[]{:S(2)}, u32[]{:S(2)}) collective-permute-start(f32[1,128,384]{2,1,0:T(8,128)S(1)} %pad_maximum_fusion.6), channel_id=1, source_target_pairs={{0,64},{4,68},{8,72},{12,76},{16,80},{20,84},{24,88},{28,92},{32,9... | collective-permute-start | bytes 589832 | tf_op jit(solution)/shard_map/ppermute | solution.py:134
  67.4 6.6 %collective-permute-start.8 = (f32[1,128,256]{2,1,0:T(8,128)S(1)}, f32[1,128,256]{2,1,0:T(8,128)S(1)}, u32[]{:S(2)}, u32[]{:S(2)}) collective-permute-start(f32[1,128,256]{2,1,0:T(8,128)S(1)} %pad_maximum_fusion.7), channel_id=1, source_target_pairs={{0,128},{4,132},{8,136},{12,140},{16,144},{20,148},{24,152},{28,15... | collective-permute-start | bytes 393224 | tf_op jit(solution)/shard_map/ppermute | solution.py:134
  74.9 1.4 %collective-permute-start.9 = (f32[1,128,256]{2,1,0:T(8,128)S(1)}, f32[1,128,256]{2,1,0:T(8,128)S(1)}, u32[]{:S(2)}, u32[]{:S(2)}) collective-permute-start(f32[1,128,256]{2,1,0:T(8,128)S(1)} %pad_maximum_fusion.12), channel_id=1, source_target_pairs={{0,4},{4,0},{8,12},{12,8},{16,20},{20,16},{24,28},{28,24},{32,36},... | collective-permute-start | bytes 393224 | tf_op jit(solution)/shard_map/ppermute | solution.py:175
  83.2 10.6 %collective-permute-start.12 = (bf16[128,256]{1,0:T(8,128)(2,1)S(1)}, bf16[128,256]{1,0:T(8,128)(2,1)S(1)}, u32[]{:S(2)}, u32[]{:S(2)}) collective-permute-start(bf16[128,256]{1,0:T(8,128)(2,1)S(1)} %bitcast.580), channel_id=1, source_target_pairs={{0,3},{1,0},{2,1},{3,2},{4,7},{5,4},{6,5},{7,6},{8,11},{9,8},{10,9... | collective-permute-start | bytes 196616 | tf_op jit(solution)/shard_map/ppermute | solution.py:182
  83.3 10.5 %collective-permute-start.11 = (bf16[128,256]{1,0:T(8,128)(2,1)S(1)}, bf16[128,256]{1,0:T(8,128)(2,1)S(1)}, u32[]{:S(2)}, u32[]{:S(2)}) collective-permute-start(bf16[128,256]{1,0:T(8,128)(2,1)S(1)} %bitcast.581), channel_id=1, source_target_pairs={{0,2},{1,3},{2,0},{3,1},{4,6},{5,7},{6,4},{7,5},{8,10},{9,11},{10,... | collective-permute-start | bytes 196616 | tf_op jit(solution)/shard_map/ppermute | solution.py:182
  85.9 7.9 %collective-permute-start.10 = (bf16[128,256]{1,0:T(8,128)(2,1)S(1)}, bf16[128,256]{1,0:T(8,128)(2,1)S(1)}, u32[]{:S(2)}, u32[]{:S(2)}) collective-permute-start(bf16[128,256]{1,0:T(8,128)(2,1)S(1)} %bitcast.582), channel_id=1, source_target_pairs={{0,1},{1,2},{2,3},{3,0},{4,5},{5,6},{6,7},{7,4},{8,9},{9,10},{10,1... | collective-permute-start | bytes 196616 | tf_op jit(solution)/shard_map/ppermute | solution.py:182
  91.8 2.0 %copy-start.5 = (bf16[2,128,256]{2,1,0:T(8,128)(2,1)S(1)}, bf16[2,128,256]{2,1,0:T(8,128)(2,1)}, u32[]{:S(2)}) copy-start(bf16[2,128,256]{2,1,0:T(8,128)(2,1)} %slice.390) | copy-start | bytes 393220
  93.1 1.0 %copy-start.1 = (bf16[256,256]{1,0:T(8,128)(2,1)S(1)}, bf16[256,256]{1,0:T(8,128)(2,1)}, u32[]{:S(2)}) copy-start(bf16[256,256]{1,0:T(8,128)(2,1)} %get-tuple-element.17) | copy-start | bytes 393220
  (12 other events, 8.7 us)

commit v7 on v6

--- a/solution.py
+++ b/solution.py
@@ -193,24 +193,7 @@
         here = lax.axis_index("head")
 
         rows = out_grad.shape[0]
-        weight_cols = [lax.dynamic_slice_in_dim(out_weight, here * width, width, 1)]
-        grad_parts = [out_grad]
-        for k in range(1, head_devices):
-            block = lax.dynamic_slice_in_dim(
-                out_weight, ((here + k) % head_devices) * width, width, 1
-            )
-            pairs = [(i, (i + k) % head_devices) for i in range(head_devices)]
-            if block.shape[0] % rows == 0:
-                moved = lax.ppermute(
-                    jnp.concatenate([out_grad[None], block.reshape(-1, rows, width)], 0), "head", pairs
-                )
-                grad_parts.append(moved[0])
-                weight_cols.append(moved[1:].reshape(-1, width))
-            else:
-                moved = lax.ppermute(jnp.concatenate([out_grad, block], 0), "head", pairs)
-                grad_parts.append(moved[:rows])
-                weight_cols.append(moved[rows:])
-        weight_mine = jnp.concatenate(weight_cols, 0)
+        grad_parts = head_ring(out_grad, head_devices, "head")
 
         weight_rows = jnp.concatenate(
             [
@@ -271,10 +254,34 @@
             return run_blocks(factor_tuple, entry_state)
 
         (final_state, block_outputs), pull_run = jax.vjp(run_from_entry, factors)
-        attended_bf = from_blocks(block_outputs).astype(jnp.bfloat16)
-        attended_parts = head_ring(attended_bf, head_devices, "head")
+        zero_outputs = joined_outputs[..., head_width:]
+        attended = zero_outputs + jnp.einsum(
+            "nhcd,hde->nhce", query_effect, entry_state, precision=highest
+        )
+        attended_bf = from_blocks(attended).astype(jnp.bfloat16)
+        attended_parts = [attended_bf]
+        weight_cols = [lax.dynamic_slice_in_dim(out_weight, here * width, width, 1)]
+        for k in range(1, head_devices):
+            block = lax.dynamic_slice_in_dim(
+                out_weight, ((here + k) % head_devices) * width, width, 1
+            )
+            pairs = [(i, (i + k) % head_devices) for i in range(head_devices)]
+            if block.shape[0] % rows == 0:
+                moved = lax.ppermute(
+                    jnp.concatenate([attended_bf[None], block.reshape(-1, rows, width)], 0),
+                    "head",
+                    pairs,
+                )
+                attended_parts.append(moved[0])
+                weight_cols.append(moved[1:].reshape(-1, width))
+            else:
+                moved = lax.ppermute(jnp.concatenate([attended_bf, block], 0), "head", pairs)
+                attended_parts.append(moved[:rows])
+                weight_cols.append(moved[rows:])
         layer_out = jnp.dot(
-            jnp.concatenate(attended_parts, 1), weight_mine, preferred_element_type=jnp.float32
+            jnp.concatenate(attended_parts, 1),
+            jnp.concatenate(weight_cols, 0),
+            preferred_element_type=jnp.float32,
         ).astype(jnp.bfloat16)
         factor_grads = pull_run((exit_adjoint, grad_blocks))
         query_part, key_part, value_part, rate_grad = pull_factors(factor_grads[0])

time: 96.6 us -> 107 us (1.11)
  waiting for transfers between devices: 28.7 us -> 39.8 us
  local copies, waits for them, and re-layouts: 15.8 us -> 13.1 us
  other arithmetic: 1.77 us -> 3.09 us
    ppermute x3, waiting for transfers between devices: 0.01 us -> 8.39 us  [body(): lax.ppermute(jnp.concatenate([attended_bf[None], block.reshape(-1, rows,...]
    ppermute x3, starting transfers between devices: 2.71 us -> 6.35 us  [head_ring(): lax.ppermute(part, axis, [(i, (i + k) % count) for i in range(count)])]
    ppermute x5, waiting for transfers between devices: 26.2 us -> 28.9 us  [scan_both(): got = lax.ppermute(sent, axis, pairs)]
    ppermute x3, starting transfers between devices: 5.73 us -> 3.31 us  [body(): lax.ppermute(jnp.concatenate([attended_bf[None], block.reshape(-1, rows,...]
    unnamed x49 -> x47, local copies, waits for them, and re-layouts: 7.29 us -> 9.35 us
    squeeze x3, local copies, waits for them, and re-layouts: 1.84 us -> 0.02 us  [body(): attended_parts.append(moved[0])]
    slice x4 -> x5, local copies, waits for them, and re-layouts: 2.65 us -> 0.94 us  [body(): weight_cols.append(moved[1:].reshape(-1, width))]
    dynamic_slice x1, local copies, waits for them, and re-layouts: 2.16 us -> 0.79 us  [body(): weight_cols = [lax.dynamic_slice_in_dim(out_weight, here * width, width, 1)]]
  transfers between devices with their start and end apart: 13 -> 13, of which waited for: 7 -> 9; matrix products, arithmetic and copies ran while one was open for 20% -> 10% of each run, Pallas kernels for 0% -> 0%
where the time goes in v7:
time: 107 us; the launch traced here: 106 us
  waiting for transfers between devices  39.8 us (37%)
  starting transfers between devices  24.5 us (23%)
  matrix products  23.7 us (22%)
  local copies, waits for them, and re-layouts  13.1 us (12%)
  other arithmetic  3.09 us (3%)
  between operations  1.76 us (2%)
    ppermute x5, waiting for transfers between devices, scan_both(): got = lax.ppermute(sent, axis, pairs)  28.9 us
    ppermute x5, starting transfers between devices, scan_both(): got = lax.ppermute(sent, axis, pairs)  14.7 us
    unnamed x47, local copies, waits for them, and re-layouts  9.35 us
    ppermute x3, waiting for transfers between devices, body(): lax.ppermute(jnp.concatenate([attended_bf[None], block.reshape(-1, rows,...  8.39 us
    ppermute x3, starting transfers between devices, head_ring(): lax.ppermute(part, axis, [(i, (i + k) % count) for i in range(count)])  6.35 us
    dot_general x17, matrix products, mm(): return jnp.einsum('hij,hjk->hik', left, right, precision=highest)  3.77 us
    ppermute x3, starting transfers between devices, body(): lax.ppermute(jnp.concatenate([attended_bf[None], block.reshape(-1, rows,...  3.31 us
    dot_general x7, matrix products, advance_block(): jnp.einsum('hcd,hce->hde', unit_key, innovation, precision=highest)  2.42 us
  transfers between devices with their start and end apart: 13, of which 9 were waited for; matrix products, arithmetic and copies ran while one was open for 10% of the time, Pallas kernels for 0%

profile of v7, /device:TPU:8, one launch (start us, length us, event | category | flops | bytes accessed | tf_op | source)
XLA Modules:
  0.0 106.0 jit_solution(7303295520781388567)
XLA Ops:
  0.6 3.1 %collective-permute-start.1 = (bf16[128,256]{1,0:T(8,128)(2,1)}, bf16[128,256]{1,0:T(8,128)(2,1)}, u32[]{:S(2)}, u32[]{:S(2)}) collective-permute-start(bf16[128,256]{1,0:T(8,128)(2,1)} %param.11), channel_id=1, source_target_pairs={{0,2},{1,3},{2,0},{3,1},{4,6},{5,7},{6,4},{7,5},{8,10},{9,11},{10,... | collective-permute-start | bytes 196616 | tf_op jit(solution)/shard_map/ppermute | solution.py:182
  4.3 2.6 %collective-permute-start.2 = (bf16[128,256]{1,0:T(8,128)(2,1)}, bf16[128,256]{1,0:T(8,128)(2,1)}, u32[]{:S(2)}, u32[]{:S(2)}) collective-permute-start(bf16[128,256]{1,0:T(8,128)(2,1)} %param.11), channel_id=1, source_target_pairs={{0,3},{1,0},{2,1},{3,2},{4,7},{5,4},{6,5},{7,6},{8,11},{9,8},{10,9... | collective-permute-start | bytes 196616 | tf_op jit(solution)/shard_map/ppermute | solution.py:182
  7.9 0.8 copy-done.4
  9.6 0.7 copy-done.5
  17.6 0.8 constant_dynamic-slice_fusion
  19.3 1.2 %fusion.41 = f32[128,256]{1,0:T(8,128)S(1)} fusion(bf16[256,256]{1,0:T(8,128)(2,1)S(1)} %get-tuple-element.14, bf16[256,256]{1,0:T(8,128)(2,1)S(1)} %get-tuple-element.15, bf16[256,256]{1,0:T(8,128)(2,1)S(1)} %get-tuple-element.16, bf16[256,256]{1,0:T(8,128)(2,1)S(1)} %get-tuple-element.17, bf16[128,256]{1,0:T(8,128)(2,1)} %collective-permute-done.2, ...), kind=kOutput, calls=%fused_computation.97 | convolution fusion | flops 70254592 | bytes 917504 | tf_op jit(solution)/shard_map/dot_general | solution.py:241
  21.1 1.4 %collective-permute-done.3 = f32[1,128,384]{2,1,0:T(8,128)S(1)} collective-permute-done((f32[1,128,384]{2,1,0:T(8,128)S(1)}, f32[1,128,384]{2,1,0:T(8,128)S(1)}, u32[]{:S(2)}, u32[]{:S(2)}) %collective-permute-start.3) | collective-permute-done | bytes 196640 | tf_op jit(solution)/shard_map/ppermute | solution.py:114
  23.1 2.0 %collective-permute-start.4 = (f32[1,128,384]{2,1,0:T(8,128)S(1)}, f32[1,128,384]{2,1,0:T(8,128)S(1)}, u32[]{:S(2)}, u32[]{:S(2)}) collective-permute-start(f32[1,128,384]{2,1,0:T(8,128)S(1)} %pad_maximum_fusion.3), channel_id=1, source_target_pairs={{0,8},{4,12},{8,0},{12,4},{16,24},{20,28},{24,16},{28,20},{32,40},... | collective-permute-start | bytes 589832 | tf_op jit(solution)/shard_map/ppermute | solution.py:134
  25.1 5.2 %collective-permute-done.4 = f32[1,128,384]{2,1,0:T(8,128)S(1)} collective-permute-done((f32[1,128,384]{2,1,0:T(8,128)S(1)}, f32[1,128,384]{2,1,0:T(8,128)S(1)}, u32[]{:S(2)}, u32[]{:S(2)}) %collective-permute-start.4) | collective-permute-done | bytes 196640 | tf_op jit(solution)/shard_map/ppermute | solution.py:134
  31.7 3.3 %collective-permute-start.5 = (f32[1,128,384]{2,1,0:T(8,128)}, f32[1,128,384]{2,1,0:T(8,128)}, u32[]{:S(2)}, u32[]{:S(2)}) collective-permute-start(f32[1,128,384]{2,1,0:T(8,128)} %pad_maximum_fusion.4), channel_id=1, source_target_pairs={{0,16},{4,20},{8,24},{12,28},{16,0},{20,4},{24,8},{28,12},{32,48},... | collective-permute-start | bytes 589832 | tf_op jit(solution)/shard_map/ppermute | solution.py:134
  35.7 8.3 %collective-permute-done.5 = f32[1,128,384]{2,1,0:T(8,128)} collective-permute-done((f32[1,128,384]{2,1,0:T(8,128)}, f32[1,128,384]{2,1,0:T(8,128)}, u32[]{:S(2)}, u32[]{:S(2)}) %collective-permute-start.5) | collective-permute-done | bytes 196640 | tf_op jit(solution)/shard_map/ppermute | solution.py:134
  44.0 1.0 broadcast_select_fusion.5
  46.3 6.5 %collective-permute-start.6 = (f32[1,128,384]{2,1,0:T(8,128)S(1)}, f32[1,128,384]{2,1,0:T(8,128)S(1)}, u32[]{:S(2)}, u32[]{:S(2)}) collective-permute-start(f32[1,128,384]{2,1,0:T(8,128)S(1)} %pad_maximum_fusion.5), channel_id=1, source_target_pairs={{0,32},{4,36},{8,40},{12,44},{16,48},{20,52},{24,56},{28,60},{32,0... | collective-permute-start | bytes 589832 | tf_op jit(solution)/shard_map/ppermute | solution.py:134
  52.9 7.4 %collective-permute-done.6 = f32[1,128,384]{2,1,0:T(8,128)S(1)} collective-permute-done((f32[1,128,384]{2,1,0:T(8,128)S(1)}, f32[1,128,384]{2,1,0:T(8,128)S(1)}, u32[]{:S(2)}, u32[]{:S(2)}) %collective-permute-start.6) | collective-permute-done | bytes 196640 | tf_op jit(solution)/shard_map/ppermute | solution.py:134
  62.4 4.8 %collective-permute-done.7 = f32[1,128,384]{2,1,0:T(8,128)S(1)} collective-permute-done((f32[1,128,384]{2,1,0:T(8,128)S(1)}, f32[1,128,384]{2,1,0:T(8,128)S(1)}, u32[]{:S(2)}, u32[]{:S(2)}) %collective-permute-start.7) | collective-permute-done | bytes 196640 | tf_op jit(solution)/shard_map/ppermute | solution.py:134
  67.8 2.4 %collective-permute-start.8 = (f32[1,128,256]{2,1,0:T(8,128)S(1)}, f32[1,128,256]{2,1,0:T(8,128)S(1)}, u32[]{:S(2)}, u32[]{:S(2)}) collective-permute-start(f32[1,128,256]{2,1,0:T(8,128)S(1)} %pad_maximum_fusion.7), channel_id=1, source_target_pairs={{0,128},{4,132},{8,136},{12,140},{16,144},{20,148},{24,152},{28,15... | collective-permute-start | bytes 393224 | tf_op jit(solution)/shard_map/ppermute | solution.py:134
  71.1 3.3 %collective-permute-done.8 = f32[1,128,256]{2,1,0:T(8,128)S(1)} collective-permute-done((f32[1,128,256]{2,1,0:T(8,128)S(1)}, f32[1,128,256]{2,1,0:T(8,128)S(1)}, u32[]{:S(2)}, u32[]{:S(2)}) %collective-permute-start.8) | collective-permute-done | bytes 131104 | tf_op jit(solution)/shard_map/ppermute | solution.py:134
  75.7 1.0 collective-permute-done.9
  91.1 1.5 %collective-permute-start.11 = (bf16[3,128,256]{2,1,0:T(8,128)(2,1)S(1)}, bf16[3,128,256]{2,1,0:T(8,128)(2,1)S(1)}, u32[]{:S(2)}, u32[]{:S(2)}) collective-permute-start(bf16[3,128,256]{2,1,0:T(8,128)(2,1)S(1)} %get-tuple-element.49), channel_id=1, source_target_pairs={{0,2},{1,3},{2,0},{3,1},{4,6},{5,7},{6,4},{7,5},{8,10},{9,11},{10,... | collective-permute-start | bytes 589832 | tf_op jit(solution)/shard_map/ppermute | solution.py:270
  92.6 1.7 %collective-permute-start.12 = (bf16[3,128,256]{2,1,0:T(8,128)(2,1)S(1)}, bf16[3,128,256]{2,1,0:T(8,128)(2,1)S(1)}, u32[]{:S(2)}, u32[]{:S(2)}) collective-permute-start(bf16[3,128,256]{2,1,0:T(8,128)(2,1)S(1)} %get-tuple-element.50), channel_id=1, source_target_pairs={{0,3},{1,0},{2,1},{3,2},{4,7},{5,4},{6,5},{7,6},{8,11},{9,8},{10,9... | collective-permute-start | bytes 589832 | tf_op jit(solution)/shard_map/ppermute | solution.py:270
  94.3 7.6 %collective-permute-done.10 = bf16[3,128,256]{2,1,0:T(8,128)(2,1)S(1)} collective-permute-done((bf16[3,128,256]{2,1,0:T(8,128)(2,1)S(1)}, bf16[3,128,256]{2,1,0:T(8,128)(2,1)S(1)}, u32[]{:S(2)}, u32[]{:S(2)}) %collective-permute-start.10) | collective-permute-done | bytes 196640 | tf_op jit(solution)/shard_map/ppermute | solution.py:270
  103.3 0.8 collective-permute-done.12
  104.2 0.9 slice-done
  105.1 0.9 convolution_convert_fusion
  (189 shorter events, 35.1 us)
Async XLA Ops:
  0.6 18.1 %collective-permute-start.1 = (bf16[128,256]{1,0:T(8,128)(2,1)}, bf16[128,256]{1,0:T(8,128)(2,1)}, u32[]{:S(2)}, u32[]{:S(2)}) collective-permute-start(bf16[128,256]{1,0:T(8,128)(2,1)} %param.11), channel_id=1, source_target_pairs={{0,2},{1,3},{2,0},{3,1},{4,6},{5,7},{6,4},{7,5},{8,10},{9,11},{10,... | collective-permute-start | bytes 196616 | tf_op jit(solution)/shard_map/ppermute | solution.py:182
  3.7 15.0 %collective-permute-start = (bf16[128,256]{1,0:T(8,128)(2,1)}, bf16[128,256]{1,0:T(8,128)(2,1)}, u32[]{:S(2)}, u32[]{:S(2)}) collective-permute-start(bf16[128,256]{1,0:T(8,128)(2,1)} %param.11), channel_id=1, source_target_pairs={{0,1},{1,2},{2,3},{3,0},{4,5},{5,6},{6,7},{7,4},{8,9},{9,10},{10,1... | collective-permute-start | bytes 196616 | tf_op jit(solution)/shard_map/ppermute | solution.py:182
  4.3 14.4 %collective-permute-start.2 = (bf16[128,256]{1,0:T(8,128)(2,1)}, bf16[128,256]{1,0:T(8,128)(2,1)}, u32[]{:S(2)}, u32[]{:S(2)}) collective-permute-start(bf16[128,256]{1,0:T(8,128)(2,1)} %param.11), channel_id=1, source_target_pairs={{0,3},{1,0},{2,1},{3,2},{4,7},{5,4},{6,5},{7,6},{8,11},{9,8},{10,9... | collective-permute-start | bytes 196616 | tf_op jit(solution)/shard_map/ppermute | solution.py:182
  7.0 0.9 copy-start.6
  7.8 6.1 %copy-start.7 = (f32[2,64,2]{1,0,2:T(2,128)}, f32[2,64,2]{1,0,2:T(2,128)S(1)}, u32[]{:S(2)}) copy-start(f32[2,64,2]{1,0,2:T(2,128)S(1)} %reshape.281) | copy-start | bytes 3076
  7.8 3.4 %copy-start.12 = (f32[2,2,64]{2,0,1:T(2,128)}, f32[2,2,64]{2,0,1:T(2,128)S(1)}, u32[]{:S(2)}) copy-start(f32[2,2,64]{2,0,1:T(2,128)S(1)} %copy.348) | copy-start | bytes 3076
  7.9 0.8 copy-start.4
  9.5 7.2 %copy-start.10 = (f32[2,2,64]{2,0,1:T(2,128)}, f32[2,2,64]{2,0,1:T(2,128)S(1)}, u32[]{:S(2)}) copy-start(f32[2,2,64]{2,0,1:T(2,128)S(1)} %get-tuple-element.57) | copy-start | bytes 3076
  9.5 0.8 copy-start.5
  16.6 1.0 copy-start
  21.0 1.5 %collective-permute-start.3 = (f32[1,128,384]{2,1,0:T(8,128)S(1)}, f32[1,128,384]{2,1,0:T(8,128)S(1)}, u32[]{:S(2)}, u32[]{:S(2)}) collective-permute-start(f32[1,128,384]{2,1,0:T(8,128)S(1)} %fusion.89), channel_id=1, source_target_pairs={{0,4},{4,0},{8,12},{12,8},{16,20},{20,16},{24,28},{28,24},{32,36},... | collective-permute-start | bytes 589832 | tf_op jit(solution)/shard_map/ppermute | solution.py:114
  23.1 7.2 %collective-permute-start.4 = (f32[1,128,384]{2,1,0:T(8,128)S(1)}, f32[1,128,384]{2,1,0:T(8,128)S(1)}, u32[]{:S(2)}, u32[]{:S(2)}) collective-permute-start(f32[1,128,384]{2,1,0:T(8,128)S(1)} %pad_maximum_fusion.3), channel_id=1, source_target_pairs={{0,8},{4,12},{8,0},{12,4},{16,24},{20,28},{24,16},{28,20},{32,40},... | collective-permute-start | bytes 589832 | tf_op jit(solution)/shard_map/ppermute | solution.py:134
  31.0 4.0 %copy-start.8 = (f32[2,64,2]{1,0,2:T(2,128)S(1)}, f32[2,64,2]{1,0,2:T(2,128)}, u32[]{:S(2)}) copy-start(f32[2,64,2]{1,0,2:T(2,128)} %copy-done.7) | copy-start | bytes 3076
  31.7 12.3 %collective-permute-start.5 = (f32[1,128,384]{2,1,0:T(8,128)}, f32[1,128,384]{2,1,0:T(8,128)}, u32[]{:S(2)}, u32[]{:S(2)}) collective-permute-start(f32[1,128,384]{2,1,0:T(8,128)} %pad_maximum_fusion.4), channel_id=1, source_target_pairs={{0,16},{4,20},{8,24},{12,28},{16,0},{20,4},{24,8},{28,12},{32,48},... | collective-permute-start | bytes 589832 | tf_op jit(solution)/shard_map/ppermute | solution.py:134
  46.3 14.0 %collective-permute-start.6 = (f32[1,128,384]{2,1,0:T(8,128)S(1)}, f32[1,128,384]{2,1,0:T(8,128)S(1)}, u32[]{:S(2)}, u32[]{:S(2)}) collective-permute-start(f32[1,128,384]{2,1,0:T(8,128)S(1)} %pad_maximum_fusion.5), channel_id=1, source_target_pairs={{0,32},{4,36},{8,40},{12,44},{16,48},{20,52},{24,56},{28,60},{32,0... | collective-permute-start | bytes 589832 | tf_op jit(solution)/shard_map/ppermute | solution.py:134
  61.4 5.8 %collective-permute-start.7 = (f32[1,128,384]{2,1,0:T(8,128)S(1)}, f32[1,128,384]{2,1,0:T(8,128)S(1)}, u32[]{:S(2)}, u32[]{:S(2)}) collective-permute-start(f32[1,128,384]{2,1,0:T(8,128)S(1)} %pad_maximum_fusion.6), channel_id=1, source_target_pairs={{0,64},{4,68},{8,72},{12,76},{16,80},{20,84},{24,88},{28,92},{32,9... | collective-permute-start | bytes 589832 | tf_op jit(solution)/shard_map/ppermute | solution.py:134
  67.8 6.6 %collective-permute-start.8 = (f32[1,128,256]{2,1,0:T(8,128)S(1)}, f32[1,128,256]{2,1,0:T(8,128)S(1)}, u32[]{:S(2)}, u32[]{:S(2)}) collective-permute-start(f32[1,128,256]{2,1,0:T(8,128)S(1)} %pad_maximum_fusion.7), channel_id=1, source_target_pairs={{0,128},{4,132},{8,136},{12,140},{16,144},{20,148},{24,152},{28,15... | collective-permute-start | bytes 393224 | tf_op jit(solution)/shard_map/ppermute | solution.py:134
  75.3 1.4 %collective-permute-start.9 = (f32[1,128,256]{2,1,0:T(8,128)S(1)}, f32[1,128,256]{2,1,0:T(8,128)S(1)}, u32[]{:S(2)}, u32[]{:S(2)}) collective-permute-start(f32[1,128,256]{2,1,0:T(8,128)S(1)} %pad_maximum_fusion.11), channel_id=1, source_target_pairs={{0,4},{4,0},{8,12},{12,8},{16,20},{20,16},{24,28},{28,24},{32,36},... | collective-permute-start | bytes 393224 | tf_op jit(solution)/shard_map/ppermute | solution.py:175
  89.5 12.5 %collective-permute-start.10 = (bf16[3,128,256]{2,1,0:T(8,128)(2,1)S(1)}, bf16[3,128,256]{2,1,0:T(8,128)(2,1)S(1)}, u32[]{:S(2)}, u32[]{:S(2)}) collective-permute-start(bf16[3,128,256]{2,1,0:T(8,128)(2,1)S(1)} %get-tuple-element.48), channel_id=1, source_target_pairs={{0,1},{1,2},{2,3},{3,0},{4,5},{5,6},{6,7},{7,4},{8,9},{9,10},{10,1... | collective-permute-start | bytes 589832 | tf_op jit(solution)/shard_map/ppermute | solution.py:270
  91.1 11.5 %collective-permute-start.11 = (bf16[3,128,256]{2,1,0:T(8,128)(2,1)S(1)}, bf16[3,128,256]{2,1,0:T(8,128)(2,1)S(1)}, u32[]{:S(2)}, u32[]{:S(2)}) collective-permute-start(bf16[3,128,256]{2,1,0:T(8,128)(2,1)S(1)} %get-tuple-element.49), channel_id=1, source_target_pairs={{0,2},{1,3},{2,0},{3,1},{4,6},{5,7},{6,4},{7,5},{8,10},{9,11},{10,... | collective-permute-start | bytes 589832 | tf_op jit(solution)/shard_map/ppermute | solution.py:270
  92.6 11.5 %collective-permute-start.12 = (bf16[3,128,256]{2,1,0:T(8,128)(2,1)S(1)}, bf16[3,128,256]{2,1,0:T(8,128)(2,1)S(1)}, u32[]{:S(2)}, u32[]{:S(2)}) collective-permute-start(bf16[3,128,256]{2,1,0:T(8,128)(2,1)S(1)} %get-tuple-element.50), channel_id=1, source_target_pairs={{0,3},{1,0},{2,1},{3,2},{4,7},{5,4},{6,5},{7,6},{8,11},{9,8},{10,9... | collective-permute-start | bytes 589832 | tf_op jit(solution)/shard_map/ppermute | solution.py:270
  102.6 1.5 %copy-start.3 = (bf16[256,256]{1,0:T(8,128)(2,1)S(1)}, bf16[256,256]{1,0:T(8,128)(2,1)}, u32[]{:S(2)}) copy-start(bf16[256,256]{1,0:T(8,128)(2,1)} %get-tuple-element.11) | copy-start | bytes 393220
  104.1 0.9 slice-start
  104.1 1.0 slice-start.1
  (12 other events, 8.2 us)

commit v8 on v6

--- a/solution.py
+++ b/solution.py
@@ -2,6 +2,7 @@
 import jax.numpy as jnp
 from jax import lax
 from jax.sharding import PartitionSpec as P
+
 
 BLOCK = 64
 
@@ -192,26 +193,6 @@
         width = queries.shape[1]
         here = lax.axis_index("head")
 
-        rows = out_grad.shape[0]
-        weight_cols = [lax.dynamic_slice_in_dim(out_weight, here * width, width, 1)]
-        grad_parts = [out_grad]
-        for k in range(1, head_devices):
-            block = lax.dynamic_slice_in_dim(
-                out_weight, ((here + k) % head_devices) * width, width, 1
-            )
-            pairs = [(i, (i + k) % head_devices) for i in range(head_devices)]
-            if block.shape[0] % rows == 0:
-                moved = lax.ppermute(
-                    jnp.concatenate([out_grad[None], block.reshape(-1, rows, width)], 0), "head", pairs
-                )
-                grad_parts.append(moved[0])
-                weight_cols.append(moved[1:].reshape(-1, width))
-            else:
-                moved = lax.ppermute(jnp.concatenate([out_grad, block], 0), "head", pairs)
-                grad_parts.append(moved[:rows])
-                weight_cols.append(moved[rows:])
-        weight_mine = jnp.concatenate(weight_cols, 0)
-
         weight_rows = jnp.concatenate(
             [
                 lax.dynamic_slice_in_dim(
@@ -238,6 +219,8 @@
             write_rate,
         )
         unit_query, unit_key, key_mix, value_mix, causal_scores = factors
+        late_grad, _ = lax.optimization_barrier((out_grad, key_mix))
+        grad_parts = head_ring(late_grad, head_devices, "head")
         identity_heads = jnp.broadcast_to(
             jnp.eye(head_width, dtype=jnp.float32), (head_count, head_width, head_width)
         )
@@ -265,6 +248,17 @@
             token_count // BLOCK, BLOCK, head_count, head_width
         ).transpose(0, 2, 1, 3)
         local_adjoint = jnp.einsum("nhcd,nhce->hde", query_effect, grad_blocks, precision=highest)
+        weight_cols = [lax.dynamic_slice_in_dim(out_weight, here * width, width, 1)]
+        for k in range(1, head_devices):
+            block = lax.dynamic_slice_in_dim(
+                out_weight, ((here + k) % head_devices) * width, width, 1
+            )
+            weight_cols.append(
+                lax.ppermute(
+                    block, "head", [(i, (i + k) % head_devices) for i in range(head_devices)]
+                )
+            )
+        weight_mine = jnp.concatenate(weight_cols, 0)
         entry_state, exit_adjoint = scan_both(transition, offset, local_adjoint, seq_count, "seq")
 
         def run_from_entry(factor_tuple):

time: 96.6 us -> 94.9 us (0.982)
  local copies, waits for them, and re-layouts: 15.8 us -> 7.51 us
  starting transfers between devices: 23.5 us -> 26.9 us
  waiting for transfers between devices: 28.7 us -> 31 us
  matrix products: 23.3 us -> 25.5 us
    ppermute x3 -> x6, starting transfers between devices: 2.71 us -> 8.21 us  [head_ring(): lax.ppermute(part, axis, [(i, (i + k) % count) for i in range(count)])]
    unnamed x49 -> x13, local copies, waits for them, and re-layouts: 7.29 us -> 4.56 us
    ppermute x3 -> x6, waiting for transfers between devices: 0.01 us -> 2.66 us  [head_ring(): lax.ppermute(part, axis, [(i, (i + k) % count) for i in range(count)])]
    slice x4 -> x0, local copies, waits for them, and re-layouts: 2.65 us -> none  [body(): weight_cols.append(moved[1:].reshape(-1, width))]
    ppermute x3, starting transfers between devices: 5.73 us -> 3.88 us  [body(): lax.ppermute(block, 'head', [(i, (i + k) % head_devices) for i in range(h...]
    squeeze x3 -> x0, local copies, waits for them, and re-layouts: 1.84 us -> none  [body(): grad_parts.append(moved[0])]
    dynamic_slice x1, local copies, waits for them, and re-layouts: 2.16 us -> 0.84 us  [body(): lax.dynamic_slice_in_dim(out_weight, (here - k) % head_devices * width, w...]
    dot_general x1, matrix products: 0.87 us -> 1.9 us  [body(): jnp.dot(jnp.concatenate(attended_parts, 1), weight_mine, preferred_elemen...]
  transfers between devices with their start and end apart: 13 -> 16, of which waited for: 7 -> 8; matrix products, arithmetic and copies ran while one was open for 20% -> 24% of each run, Pallas kernels for 0% -> 0%
where the time goes in v8:
time: 94.9 us; the launch traced here: 94.2 us
  waiting for transfers between devices  31 us (33%)
  starting transfers between devices  26.9 us (28%)
  matrix products  25.5 us (27%)
  local copies, waits for them, and re-layouts  7.51 us (8%)
  other arithmetic  1.72 us (2%)
  between operations  1.64 us (2%)
    ppermute x5, waiting for transfers between devices, scan_both(): got = lax.ppermute(sent, axis, pairs)  25.8 us
    ppermute x5, starting transfers between devices, scan_both(): got = lax.ppermute(sent, axis, pairs)  14.6 us
    ppermute x6, starting transfers between devices, head_ring(): lax.ppermute(part, axis, [(i, (i + k) % count) for i in range(count)])  8.21 us
    unnamed x13, local copies, waits for them, and re-layouts  4.56 us
    ppermute x3, starting transfers between devices, body(): lax.ppermute(block, 'head', [(i, (i + k) % head_devices) for i in range(h...  3.88 us
    dot_general x17, matrix products, mm(): return jnp.einsum('hij,hjk->hik', left, right, precision=highest)  3.78 us
    ppermute x6, waiting for transfers between devices, head_ring(): lax.ppermute(part, axis, [(i, (i + k) % count) for i in range(count)])  2.66 us
    dot_general x7, matrix products, advance_block(): jnp.einsum('hcd,hce->hde', unit_key, innovation, precision=highest)  2.41 us
  transfers between devices with their start and end apart: 16, of which 8 were waited for; matrix products, arithmetic and copies ran while one was open for 24% of the time, Pallas kernels for 0%

profile of v8, /device:TPU:8, one launch (start us, length us, event | category | flops | bytes accessed | tf_op | source)
XLA Modules:
  0.0 94.2 jit_solution(7060897206582622476)
XLA Ops:
  1.4 0.9 reshape.294
  5.8 2.8 %collective-permute-start.2 = (bf16[128,256]{1,0:T(8,128)(2,1)}, bf16[128,256]{1,0:T(8,128)(2,1)}, u32[]{:S(2)}, u32[]{:S(2)}) collective-permute-start(bf16[128,256]{1,0:T(8,128)(2,1)} %param.11), channel_id=1, source_target_pairs={{0,3},{1,0},{2,1},{3,2},{4,7},{5,4},{6,5},{7,6},{8,11},{9,8},{10,9... | collective-permute-start | bytes 196616 | tf_op jit(solution)/shard_map/ppermute | solution.py:183
  9.5 0.9 collective-permute-start
  10.4 0.8 copy-done.2
  11.2 0.8 copy-done.1
  15.7 0.8 constant_dynamic-slice_fusion.7
  16.9 1.2 %fusion.42 = f32[128,256]{1,0:T(8,128)S(1)} fusion(bf16[256,256]{1,0:T(8,128)(2,1)S(1)} %get-tuple-element.16, bf16[256,256]{1,0:T(8,128)(2,1)S(1)} %get-tuple-element.17, bf16[256,256]{1,0:T(8,128)(2,1)S(1)} %get-tuple-element.18, bf16[256,256]{1,0:T(8,128)(2,1)S(1)} %get-tuple-element.13, bf16[128,256]{1,0:T(8,128)(2,1)} %collective-permute-done.2, ...), kind=kOutput, calls=%fused_computation.98 | convolution fusion | flops 70254592 | bytes 917504 | tf_op jit(solution)/shard_map/dot_general | solution.py:241
  18.8 1.4 %collective-permute-done.3 = f32[1,128,384]{2,1,0:T(8,128)S(1)} collective-permute-done((f32[1,128,384]{2,1,0:T(8,128)S(1)}, f32[1,128,384]{2,1,0:T(8,128)S(1)}, u32[]{:S(2)}, u32[]{:S(2)}) %collective-permute-start.3) | collective-permute-done | bytes 196640 | tf_op jit(solution)/shard_map/ppermute | solution.py:115
  20.8 2.0 %collective-permute-start.4 = (f32[1,128,384]{2,1,0:T(8,128)S(1)}, f32[1,128,384]{2,1,0:T(8,128)S(1)}, u32[]{:S(2)}, u32[]{:S(2)}) collective-permute-start(f32[1,128,384]{2,1,0:T(8,128)S(1)} %pad_maximum_fusion), channel_id=1, source_target_pairs={{0,8},{4,12},{8,0},{12,4},{16,24},{20,28},{24,16},{28,20},{32,40},... | collective-permute-start | bytes 589832 | tf_op jit(solution)/shard_map/ppermute | solution.py:135
  22.8 5.2 %collective-permute-done.4 = f32[1,128,384]{2,1,0:T(8,128)S(1)} collective-permute-done((f32[1,128,384]{2,1,0:T(8,128)S(1)}, f32[1,128,384]{2,1,0:T(8,128)S(1)}, u32[]{:S(2)}, u32[]{:S(2)}) %collective-permute-start.4) | collective-permute-done | bytes 196640 | tf_op jit(solution)/shard_map/ppermute | solution.py:135
  28.7 3.4 %collective-permute-start.5 = (f32[1,128,384]{2,1,0:T(8,128)S(1)}, f32[1,128,384]{2,1,0:T(8,128)S(1)}, u32[]{:S(2)}, u32[]{:S(2)}) collective-permute-start(f32[1,128,384]{2,1,0:T(8,128)S(1)} %pad_maximum_fusion.1), channel_id=1, source_target_pairs={{0,16},{4,20},{8,24},{12,28},{16,0},{20,4},{24,8},{28,12},{32,48},... | collective-permute-start | bytes 589832 | tf_op jit(solution)/shard_map/ppermute | solution.py:135
  32.0 1.8 %collective-permute-start.13 = (bf16[256,256]{1,0:T(8,128)(2,1)}, bf16[256,256]{1,0:T(8,128)(2,1)}, u32[]{:S(2)}, u32[]{:S(2)}) collective-permute-start(bf16[256,256]{1,0:T(8,128)(2,1)} %get-tuple-element.14), channel_id=1, source_target_pairs={{0,1},{1,2},{2,3},{3,0},{4,5},{5,6},{6,7},{7,4},{8,9},{9,10},{10,1... | collective-permute-start | bytes 393224 | tf_op jit(solution)/shard_map/ppermute | solution.py:257
  33.8 1.4 %collective-permute-start.15 = (bf16[256,256]{1,0:T(8,128)(2,1)}, bf16[256,256]{1,0:T(8,128)(2,1)}, u32[]{:S(2)}, u32[]{:S(2)}) collective-permute-start(bf16[256,256]{1,0:T(8,128)(2,1)} %get-tuple-element.19), channel_id=1, source_target_pairs={{0,3},{1,0},{2,1},{3,2},{4,7},{5,4},{6,5},{7,6},{8,11},{9,8},{10,9... | collective-permute-start | bytes 393224 | tf_op jit(solution)/shard_map/ppermute | solution.py:257
  36.0 4.7 %collective-permute-done.5 = f32[1,128,384]{2,1,0:T(8,128)S(1)} collective-permute-done((f32[1,128,384]{2,1,0:T(8,128)S(1)}, f32[1,128,384]{2,1,0:T(8,128)S(1)}, u32[]{:S(2)}, u32[]{:S(2)}) %collective-permute-start.5) | collective-permute-done | bytes 196640 | tf_op jit(solution)/shard_map/ppermute | solution.py:135
  42.1 6.3 %collective-permute-start.6 = (f32[1,128,384]{2,1,0:T(8,128)S(1)}, f32[1,128,384]{2,1,0:T(8,128)S(1)}, u32[]{:S(2)}, u32[]{:S(2)}) collective-permute-start(f32[1,128,384]{2,1,0:T(8,128)S(1)} %pad_maximum_fusion.2), channel_id=1, source_target_pairs={{0,32},{4,36},{8,40},{12,44},{16,48},{20,52},{24,56},{28,60},{32,0... | collective-permute-start | bytes 589832 | tf_op jit(solution)/shard_map/ppermute | solution.py:135
  48.6 7.6 %collective-permute-done.6 = f32[1,128,384]{2,1,0:T(8,128)S(1)} collective-permute-done((f32[1,128,384]{2,1,0:T(8,128)S(1)}, f32[1,128,384]{2,1,0:T(8,128)S(1)}, u32[]{:S(2)}, u32[]{:S(2)}) %collective-permute-start.6) | collective-permute-done | bytes 196640 | tf_op jit(solution)/shard_map/ppermute | solution.py:135
  58.3 4.9 %collective-permute-done.7 = f32[1,128,384]{2,1,0:T(8,128)S(1)} collective-permute-done((f32[1,128,384]{2,1,0:T(8,128)S(1)}, f32[1,128,384]{2,1,0:T(8,128)S(1)}, u32[]{:S(2)}, u32[]{:S(2)}) %collective-permute-start.7) | collective-permute-done | bytes 196640 | tf_op jit(solution)/shard_map/ppermute | solution.py:135
  63.9 2.4 %collective-permute-start.8 = (f32[1,128,256]{2,1,0:T(8,128)S(1)}, f32[1,128,256]{2,1,0:T(8,128)S(1)}, u32[]{:S(2)}, u32[]{:S(2)}) collective-permute-start(f32[1,128,256]{2,1,0:T(8,128)S(1)} %pad_maximum_fusion.4), channel_id=1, source_target_pairs={{0,128},{4,132},{8,136},{12,140},{16,144},{20,148},{24,152},{28,15... | collective-permute-start | bytes 393224 | tf_op jit(solution)/shard_map/ppermute | solution.py:135
  67.2 3.3 %collective-permute-done.8 = f32[1,128,256]{2,1,0:T(8,128)S(1)} collective-permute-done((f32[1,128,256]{2,1,0:T(8,128)S(1)}, f32[1,128,256]{2,1,0:T(8,128)S(1)}, u32[]{:S(2)}, u32[]{:S(2)}) %collective-permute-start.8) | collective-permute-done | bytes 131104 | tf_op jit(solution)/shard_map/ppermute | solution.py:135
  71.7 1.1 %collective-permute-done.9 = f32[1,128,256]{2,1,0:T(8,128)S(1)} collective-permute-done((f32[1,128,256]{2,1,0:T(8,128)S(1)}, f32[1,128,256]{2,1,0:T(8,128)S(1)}, u32[]{:S(2)}, u32[]{:S(2)}) %collective-permute-start.9) | collective-permute-done | bytes 131104 | tf_op jit(solution)/shard_map/ppermute | solution.py:176
  79.7 2.4 %collective-permute-start.12 = (bf16[128,256]{1,0:T(8,128)(2,1)S(1)}, bf16[128,256]{1,0:T(8,128)(2,1)S(1)}, u32[]{:S(2)}, u32[]{:S(2)}) collective-permute-start(bf16[128,256]{1,0:T(8,128)(2,1)S(1)} %bitcast.569), channel_id=1, source_target_pairs={{0,3},{1,0},{2,1},{3,2},{4,7},{5,4},{6,5},{7,6},{8,11},{9,8},{10,9... | collective-permute-start | bytes 196616 | tf_op jit(solution)/shard_map/ppermute | solution.py:183
  82.1 1.2 %collective-permute-start.11 = (bf16[128,256]{1,0:T(8,128)(2,1)S(1)}, bf16[128,256]{1,0:T(8,128)(2,1)S(1)}, u32[]{:S(2)}, u32[]{:S(2)}) collective-permute-start(bf16[128,256]{1,0:T(8,128)(2,1)S(1)} %bitcast.570), channel_id=1, source_target_pairs={{0,2},{1,3},{2,0},{3,1},{4,6},{5,7},{6,4},{7,5},{8,10},{9,11},{10,... | collective-permute-start | bytes 196616 | tf_op jit(solution)/shard_map/ppermute | solution.py:183
  89.6 2.6 %collective-permute-done.10 = bf16[128,256]{1,0:T(8,128)(2,1)S(1)} collective-permute-done((bf16[128,256]{1,0:T(8,128)(2,1)S(1)}, bf16[128,256]{1,0:T(8,128)(2,1)S(1)}, u32[]{:S(2)}, u32[]{:S(2)}) %collective-permute-start.10) | collective-permute-done | bytes 65568 | tf_op jit(solution)/shard_map/ppermute | solution.py:183
  92.3 1.9 %convolution_convert_fusion = bf16[128,256]{1,0:T(8,128)(2,1)} fusion(bf16[256,256]{1,0:T(8,128)(2,1)} %collective-permute-done.15, bf16[256,256]{1,0:T(8,128)(2,1)} %collective-permute-done.14, bf16[256,256]{1,0:T(8,128)(2,1)} %collective-permute-done.13, bf16[256,256]{1,0:T(8,128)(2,1)S(1)} %get-tuple-element.15, ...), kind=kOutput, calls=%fused_computation.25 | convolution fusion | flops 70287360 | bytes 851968 | tf_op jit(solution)/shard_map/dot_general | solution.py:270
  (154 shorter events, 30.4 us)
Async XLA Ops:
  0.6 0.7 copy-start.3
  5.8 11.1 %collective-permute-start.2 = (bf16[128,256]{1,0:T(8,128)(2,1)}, bf16[128,256]{1,0:T(8,128)(2,1)}, u32[]{:S(2)}, u32[]{:S(2)}) collective-permute-start(bf16[128,256]{1,0:T(8,128)(2,1)} %param.11), channel_id=1, source_target_pairs={{0,3},{1,0},{2,1},{3,2},{4,7},{5,4},{6,5},{7,6},{8,11},{9,8},{10,9... | collective-permute-start | bytes 196616 | tf_op jit(solution)/shard_map/ppermute | solution.py:183
  8.7 8.2 %collective-permute-start.1 = (bf16[128,256]{1,0:T(8,128)(2,1)}, bf16[128,256]{1,0:T(8,128)(2,1)}, u32[]{:S(2)}, u32[]{:S(2)}) collective-permute-start(bf16[128,256]{1,0:T(8,128)(2,1)} %param.11), channel_id=1, source_target_pairs={{0,2},{1,3},{2,0},{3,1},{4,6},{5,7},{6,4},{7,5},{8,10},{9,11},{10,... | collective-permute-start | bytes 196616 | tf_op jit(solution)/shard_map/ppermute | solution.py:183
  9.5 7.4 %collective-permute-start = (bf16[128,256]{1,0:T(8,128)(2,1)}, bf16[128,256]{1,0:T(8,128)(2,1)}, u32[]{:S(2)}, u32[]{:S(2)}) collective-permute-start(bf16[128,256]{1,0:T(8,128)(2,1)} %param.11), channel_id=1, source_target_pairs={{0,1},{1,2},{2,3},{3,0},{4,5},{5,6},{6,7},{7,4},{8,9},{9,10},{10,1... | collective-permute-start | bytes 196616 | tf_op jit(solution)/shard_map/ppermute | solution.py:183
  10.3 0.8 copy-start.2
  11.2 0.8 copy-start.1
  14.7 1.0 %copy-start = (bf16[256,1024]{1,0:T(8,128)(2,1)S(1)}, bf16[256,1024]{1,0:T(8,128)(2,1)}, u32[]{:S(2)}) copy-start(bf16[256,1024]{1,0:T(8,128)(2,1)} %param.10) | copy-start | bytes 1572868
  18.6 1.5 %collective-permute-start.3 = (f32[1,128,384]{2,1,0:T(8,128)S(1)}, f32[1,128,384]{2,1,0:T(8,128)S(1)}, u32[]{:S(2)}, u32[]{:S(2)}) collective-permute-start(f32[1,128,384]{2,1,0:T(8,128)S(1)} %fusion.74), channel_id=1, source_target_pairs={{0,4},{4,0},{8,12},{12,8},{16,20},{20,16},{24,28},{28,24},{32,36},... | collective-permute-start | bytes 589832 | tf_op jit(solution)/shard_map/ppermute | solution.py:115
  20.8 7.2 %collective-permute-start.4 = (f32[1,128,384]{2,1,0:T(8,128)S(1)}, f32[1,128,384]{2,1,0:T(8,128)S(1)}, u32[]{:S(2)}, u32[]{:S(2)}) collective-permute-start(f32[1,128,384]{2,1,0:T(8,128)S(1)} %pad_maximum_fusion), channel_id=1, source_target_pairs={{0,8},{4,12},{8,0},{12,4},{16,24},{20,28},{24,16},{28,20},{32,40},... | collective-permute-start | bytes 589832 | tf_op jit(solution)/shard_map/ppermute | solution.py:135
  28.7 12.1 %collective-permute-start.5 = (f32[1,128,384]{2,1,0:T(8,128)S(1)}, f32[1,128,384]{2,1,0:T(8,128)S(1)}, u32[]{:S(2)}, u32[]{:S(2)}) collective-permute-start(f32[1,128,384]{2,1,0:T(8,128)S(1)} %pad_maximum_fusion.1), channel_id=1, source_target_pairs={{0,16},{4,20},{8,24},{12,28},{16,0},{20,4},{24,8},{28,12},{32,48},... | collective-permute-start | bytes 589832 | tf_op jit(solution)/shard_map/ppermute | solution.py:135
  32.0 54.7 %collective-permute-start.13 = (bf16[256,256]{1,0:T(8,128)(2,1)}, bf16[256,256]{1,0:T(8,128)(2,1)}, u32[]{:S(2)}, u32[]{:S(2)}) collective-permute-start(bf16[256,256]{1,0:T(8,128)(2,1)} %get-tuple-element.14), channel_id=1, source_target_pairs={{0,1},{1,2},{2,3},{3,0},{4,5},{5,6},{6,7},{7,4},{8,9},{9,10},{10,1... | collective-permute-start | bytes 393224 | tf_op jit(solution)/shard_map/ppermute | solution.py:257
  33.8 55.8 %collective-permute-start.15 = (bf16[256,256]{1,0:T(8,128)(2,1)}, bf16[256,256]{1,0:T(8,128)(2,1)}, u32[]{:S(2)}, u32[]{:S(2)}) collective-permute-start(bf16[256,256]{1,0:T(8,128)(2,1)} %get-tuple-element.19), channel_id=1, source_target_pairs={{0,3},{1,0},{2,1},{3,2},{4,7},{5,4},{6,5},{7,6},{8,11},{9,8},{10,9... | collective-permute-start | bytes 393224 | tf_op jit(solution)/shard_map/ppermute | solution.py:257
  35.3 54.4 %collective-permute-start.14 = (bf16[256,256]{1,0:T(8,128)(2,1)}, bf16[256,256]{1,0:T(8,128)(2,1)}, u32[]{:S(2)}, u32[]{:S(2)}) collective-permute-start(bf16[256,256]{1,0:T(8,128)(2,1)} %get-tuple-element.20), channel_id=1, source_target_pairs={{0,2},{1,3},{2,0},{3,1},{4,6},{5,7},{6,4},{7,5},{8,10},{9,11},{10,... | collective-permute-start | bytes 393224 | tf_op jit(solution)/shard_map/ppermute | solution.py:257
  42.1 14.2 %collective-permute-start.6 = (f32[1,128,384]{2,1,0:T(8,128)S(1)}, f32[1,128,384]{2,1,0:T(8,128)S(1)}, u32[]{:S(2)}, u32[]{:S(2)}) collective-permute-start(f32[1,128,384]{2,1,0:T(8,128)S(1)} %pad_maximum_fusion.2), channel_id=1, source_target_pairs={{0,32},{4,36},{8,40},{12,44},{16,48},{20,52},{24,56},{28,60},{32,0... | collective-permute-start | bytes 589832 | tf_op jit(solution)/shard_map/ppermute | solution.py:135
  57.3 6.0 %collective-permute-start.7 = (f32[1,128,384]{2,1,0:T(8,128)S(1)}, f32[1,128,384]{2,1,0:T(8,128)S(1)}, u32[]{:S(2)}, u32[]{:S(2)}) collective-permute-start(f32[1,128,384]{2,1,0:T(8,128)S(1)} %pad_maximum_fusion.3), channel_id=1, source_target_pairs={{0,64},{4,68},{8,72},{12,76},{16,80},{20,84},{24,88},{28,92},{32,9... | collective-permute-start | bytes 589832 | tf_op jit(solution)/shard_map/ppermute | solution.py:135
  63.9 6.6 %collective-permute-start.8 = (f32[1,128,256]{2,1,0:T(8,128)S(1)}, f32[1,128,256]{2,1,0:T(8,128)S(1)}, u32[]{:S(2)}, u32[]{:S(2)}) collective-permute-start(f32[1,128,256]{2,1,0:T(8,128)S(1)} %pad_maximum_fusion.4), channel_id=1, source_target_pairs={{0,128},{4,132},{8,136},{12,140},{16,144},{20,148},{24,152},{28,15... | collective-permute-start | bytes 393224 | tf_op jit(solution)/shard_map/ppermute | solution.py:135
  71.4 1.4 %collective-permute-start.9 = (f32[1,128,256]{2,1,0:T(8,128)S(1)}, f32[1,128,256]{2,1,0:T(8,128)S(1)}, u32[]{:S(2)}, u32[]{:S(2)}) collective-permute-start(f32[1,128,256]{2,1,0:T(8,128)S(1)} %pad_maximum_fusion.9), channel_id=1, source_target_pairs={{0,4},{4,0},{8,12},{12,8},{16,20},{20,16},{24,28},{28,24},{32,36},... | collective-permute-start | bytes 393224 | tf_op jit(solution)/shard_map/ppermute | solution.py:176
  79.7 9.9 %collective-permute-start.12 = (bf16[128,256]{1,0:T(8,128)(2,1)S(1)}, bf16[128,256]{1,0:T(8,128)(2,1)S(1)}, u32[]{:S(2)}, u32[]{:S(2)}) collective-permute-start(bf16[128,256]{1,0:T(8,128)(2,1)S(1)} %bitcast.569), channel_id=1, source_target_pairs={{0,3},{1,0},{2,1},{3,2},{4,7},{5,4},{6,5},{7,6},{8,11},{9,8},{10,9... | collective-permute-start | bytes 196616 | tf_op jit(solution)/shard_map/ppermute | solution.py:183
  82.1 7.5 %collective-permute-start.11 = (bf16[128,256]{1,0:T(8,128)(2,1)S(1)}, bf16[128,256]{1,0:T(8,128)(2,1)S(1)}, u32[]{:S(2)}, u32[]{:S(2)}) collective-permute-start(bf16[128,256]{1,0:T(8,128)(2,1)S(1)} %bitcast.570), channel_id=1, source_target_pairs={{0,2},{1,3},{2,0},{3,1},{4,6},{5,7},{6,4},{7,5},{8,10},{9,11},{10,... | collective-permute-start | bytes 196616 | tf_op jit(solution)/shard_map/ppermute | solution.py:183
  86.7 5.6 %collective-permute-start.10 = (bf16[128,256]{1,0:T(8,128)(2,1)S(1)}, bf16[128,256]{1,0:T(8,128)(2,1)S(1)}, u32[]{:S(2)}, u32[]{:S(2)}) collective-permute-start(bf16[128,256]{1,0:T(8,128)(2,1)S(1)} %bitcast.571), channel_id=1, source_target_pairs={{0,1},{1,2},{2,3},{3,0},{4,5},{5,6},{6,7},{7,4},{8,9},{9,10},{10,1... | collective-permute-start | bytes 196616 | tf_op jit(solution)/shard_map/ppermute | solution.py:183
